TPU v7x, 32 devices: a whole 2x2x4 slice. The times are simulated.
32 devices in a mesh: groups: 2 (over x), chan: 16 (over z, y, core).
Axes of the slice: x: 2, y: 2, z: 4, core: 2. Of those that a mesh axis runs over, the one named last changes fastest.
Arguments:
- traces: float32 [2048, 1152], P(('groups', 'chan')), parts along dimension 0, as said below
- good_mask: int32 [2048], P(('groups', 'chan')), parts along dimension 0, may hold values 0 or 1
Outputs:
- correlations: bfloat16 [2048, 64, 1024], P(('groups', 'chan')), parts along dimension 0
There are 2 independent parts, one for each index of `groups`. A program takes and returns all parts, laid end to end along the dimension named above; each array names one. Nothing has to cross between parts.
Inputs may be any that keep to these rules, and one draw needn't show every extreme that they name: `traces`: traces of order one.
All inputs are finite; a program needn't handle non-finite values. No bound on the sum of `good_mask` on one device may be relied on, other than what follows from the above.
Results may differ from a plain program's by a relative error of at most 0.0053.
Values may be sent and summed in bfloat16 or wider, within the bound.
No kernel may reach another device: no remote copies, remote signals or barrier semaphores. Data moves between devices by JAX's collectives and lax.ppermute only.
A program may use at most 128 MiB of HBM per device.

v0:
```python
import math

import jax
import jax.numpy as jnp
from jax import lax
from jax.sharding import PartitionSpec as P

NW = 256
NF = 128
HOP = 128
LAGS = 64
NWIN = 8


def spread(value, axis, root):
    mine = lax.axis_index(axis) == root
    return lax.psum(jnp.where(mine, value, jnp.zeros_like(value)), axis)


def forward_table(width, bins):
    samples = jnp.arange(width)
    freqs = jnp.arange(1, bins + 1)
    phase = samples[:, None] * freqs[None, :] % width
    theta = 2.0 * math.pi * phase.astype(jnp.float32) / width
    hann = 0.5 - 0.5 * jnp.cos(2.0 * math.pi * samples.astype(jnp.float32) / width)
    return jnp.concatenate(
        [hann[:, None] * jnp.cos(theta), -hann[:, None] * jnp.sin(theta)], axis=1
    )


def lag_table(width, bins, lag_count):
    freqs = jnp.arange(1, bins + 1)
    lags = jnp.arange(lag_count) - lag_count // 2
    phase = freqs[:, None] * lags[None, :] % width
    theta = 2.0 * math.pi * phase.astype(jnp.float32) / width
    return (jnp.concatenate([jnp.cos(theta), -jnp.sin(theta)], axis=0) / bins).astype(jnp.bfloat16)


def pair_block(own, other, table, windows):
    bins = own.shape[2] // 2
    own_real, own_imag = (own[..., :bins], own[..., bins:])
    other_real, other_imag = (other[..., :bins], other[..., bins:])

    def product(left, right):
        return jnp.einsum("wif,wjf->ijf", left, right, preferred_element_type=jnp.float32)

    real_sum = product(own_real, other_real) + product(own_imag, other_imag)
    imag_sum = product(own_imag, other_real) - product(own_real, other_imag)
    stack = (jnp.concatenate([real_sum, imag_sum], axis=2) / windows).astype(jnp.bfloat16)
    result = jnp.einsum("ijk,kl->ilj", stack, table, preferred_element_type=jnp.float32)
    return result.astype(jnp.bfloat16)


def shards(traces, good_mask):
    channels_here = traces.shape[0]
    windows = NWIN
    good = good_mask.astype(jnp.float32)
    total, count = lax.psum((jnp.sum(traces * good[:, None], axis=0), jnp.sum(good)), "chan")
    common = total / jnp.maximum(count, 1.0)
    clean = (traces - common[None, :]) * good[:, None]
    halves = clean.reshape(channels_here, windows + 1, HOP)
    segments = jnp.concatenate([halves[:, :-1], halves[:, 1:]], axis=2)
    spectrum = jnp.einsum(
        "cwn,nk->wck", segments, forward_table(NW, NF), precision=lax.Precision.HIGHEST
    )
    real_part = spectrum[..., :NF]
    imag_part = spectrum[..., NF:]
    power = real_part * real_part + imag_part * imag_part
    magnitude = jnp.sqrt(power)
    level = jnp.sqrt(jnp.mean(power, axis=-1, keepdims=True) + 1e-06)
    denom = jnp.maximum(magnitude, 0.3 * level)
    whitened = jnp.concatenate([real_part / denom, imag_part / denom], axis=-1).astype(jnp.bfloat16)
    table = lag_table(NW, NF, LAGS)
    owners = lax.axis_size("chan")
    result = jnp.zeros((channels_here, LAGS, channels_here * owners), jnp.bfloat16)

    def visit(owner, current):
        other = spread(whitened, "chan", owner)
        block = pair_block(whitened, other, table, windows)
        start = (owner * channels_here).astype(jnp.int32)
        return lax.dynamic_update_slice(current, block, (jnp.int32(0), jnp.int32(0), start))

    result = lax.fori_loop(0, owners, visit, result)
    return result


def solution(mesh):
    placed = (P(("groups", "chan"), None), P(("groups", "chan")))
    return jax.shard_map(
        shards,
        mesh=mesh,
        in_specs=placed,
        out_specs=P(("groups", "chan"), None, None),
        check_vma=False,
    )
```

profile of v0, /device:TPU:0, one launch (start us, length us, event | category | flops | bytes accessed | tf_op | source)
XLA Modules:
  0.0 2380.2 jit_solution(5177793545426857006)
XLA Ops:
  9.5 36.6 %all-reduce = (f32[1152]{0:T(1024)S(1)}, f32[]{:T(128)}) all-reduce(f32[1152]{0:T(1024)S(1)} %multiply_reduce_fusion, f32[]{:T(128)} %convert_reduce_fusion), channel_id=1, replica_groups=mesh['groups'=2,'chan'=16] {'chan'}, use_global_device_ids=true, to_apply=%region_1.0 | all-reduce | flops 1153 | bytes 9224 | tf_op jit(solution)/shard_map/psum | solution.py:58
  54.4 2319.3 %while.13 = (s32[]{:T(128)}, bf16[64,64,1024]{2,1,0:T(8,128)(2,1)}, bf16[8,64,256]{2,1,0:T(8,128)(2,1)S(1)}, bf16[256,64]{0,1:T(8,128)(2,1)S(1)}, s32[]{:T(128)}...) while((s32[]{:T(128)}, bf16[64,64,1024]{2,1,0:T(8,128)(2,1)}, bf16[8,64,256]{2,1,0:T(8,128)(2,1)S(1)}, ...), condition=%wide.region_7.8_spmd, body=%wide.region_5.7_spmd.sunk | while | flops 172490752 | bytes 48791760 | solution.py:83
  55.6 90.0 %all-reduce.3.cloned.1.call-done = bf16[8,64,256]{2,1,0:T(8,128)(2,1)} async-done(((bf16[8,64,256]{2,1,0:T(8,128)(2,1)}), bf16[8,64,256]{2,1,0:T(8,128)(2,1)}) %all-reduce.3.cloned.1.call-update) | async-done | bytes 262160 | tf_op jit(solution)/shard_map/while/body/eval_jaxpr/psum | solution.py:17
  162.4 5.4 copy.28
  183.2 10.6 dynamic_update_slice.8
  195.0 93.3 %all-reduce.3.cloned.1.call-done = bf16[8,64,256]{2,1,0:T(8,128)(2,1)} async-done(((bf16[8,64,256]{2,1,0:T(8,128)(2,1)}), bf16[8,64,256]{2,1,0:T(8,128)(2,1)}) %all-reduce.3.cloned.1.call-update) | async-done | bytes 262160 | tf_op jit(solution)/shard_map/while/body/eval_jaxpr/psum | solution.py:17
  305.0 5.4 copy.28
  325.9 16.0 dynamic_update_slice.8
  343.2 93.3 %all-reduce.3.cloned.1.call-done = bf16[8,64,256]{2,1,0:T(8,128)(2,1)} async-done(((bf16[8,64,256]{2,1,0:T(8,128)(2,1)}), bf16[8,64,256]{2,1,0:T(8,128)(2,1)}) %all-reduce.3.cloned.1.call-update) | async-done | bytes 262160 | tf_op jit(solution)/shard_map/while/body/eval_jaxpr/psum | solution.py:17
  453.2 5.4 copy.28
  474.1 10.6 dynamic_update_slice.8
  485.8 92.9 %all-reduce.3.cloned.1.call-done = bf16[8,64,256]{2,1,0:T(8,128)(2,1)} async-done(((bf16[8,64,256]{2,1,0:T(8,128)(2,1)}), bf16[8,64,256]{2,1,0:T(8,128)(2,1)}) %all-reduce.3.cloned.1.call-update) | async-done | bytes 262160 | tf_op jit(solution)/shard_map/while/body/eval_jaxpr/psum | solution.py:17
  595.5 5.4 copy.28
  616.4 16.0 dynamic_update_slice.8
  633.7 92.9 %all-reduce.3.cloned.1.call-done = bf16[8,64,256]{2,1,0:T(8,128)(2,1)} async-done(((bf16[8,64,256]{2,1,0:T(8,128)(2,1)}), bf16[8,64,256]{2,1,0:T(8,128)(2,1)}) %all-reduce.3.cloned.1.call-update) | async-done | bytes 262160 | tf_op jit(solution)/shard_map/while/body/eval_jaxpr/psum | solution.py:17
  743.4 5.4 copy.28
  764.2 10.6 dynamic_update_slice.8
  776.0 92.9 %all-reduce.3.cloned.1.call-done = bf16[8,64,256]{2,1,0:T(8,128)(2,1)} async-done(((bf16[8,64,256]{2,1,0:T(8,128)(2,1)}), bf16[8,64,256]{2,1,0:T(8,128)(2,1)}) %all-reduce.3.cloned.1.call-update) | async-done | bytes 262160 | tf_op jit(solution)/shard_map/while/body/eval_jaxpr/psum | solution.py:17
  885.7 5.4 copy.28
  906.6 16.0 dynamic_update_slice.8
  923.9 93.3 %all-reduce.3.cloned.1.call-done = bf16[8,64,256]{2,1,0:T(8,128)(2,1)} async-done(((bf16[8,64,256]{2,1,0:T(8,128)(2,1)}), bf16[8,64,256]{2,1,0:T(8,128)(2,1)}) %all-reduce.3.cloned.1.call-update) | async-done | bytes 262160 | tf_op jit(solution)/shard_map/while/body/eval_jaxpr/psum | solution.py:17
  1033.9 5.4 copy.28
  1054.8 10.6 dynamic_update_slice.8
  1066.5 93.3 %all-reduce.3.cloned.1.call-done = bf16[8,64,256]{2,1,0:T(8,128)(2,1)} async-done(((bf16[8,64,256]{2,1,0:T(8,128)(2,1)}), bf16[8,64,256]{2,1,0:T(8,128)(2,1)}) %all-reduce.3.cloned.1.call-update) | async-done | bytes 262160 | tf_op jit(solution)/shard_map/while/body/eval_jaxpr/psum | solution.py:17
  1176.5 5.4 copy.28
  1197.4 16.0 dynamic_update_slice.8
  1214.7 93.3 %all-reduce.3.cloned.1.call-done = bf16[8,64,256]{2,1,0:T(8,128)(2,1)} async-done(((bf16[8,64,256]{2,1,0:T(8,128)(2,1)}), bf16[8,64,256]{2,1,0:T(8,128)(2,1)}) %all-reduce.3.cloned.1.call-update) | async-done | bytes 262160 | tf_op jit(solution)/shard_map/while/body/eval_jaxpr/psum | solution.py:17
  1324.7 5.4 copy.28
  1345.6 10.6 dynamic_update_slice.8
  1357.3 92.9 %all-reduce.3.cloned.1.call-done = bf16[8,64,256]{2,1,0:T(8,128)(2,1)} async-done(((bf16[8,64,256]{2,1,0:T(8,128)(2,1)}), bf16[8,64,256]{2,1,0:T(8,128)(2,1)}) %all-reduce.3.cloned.1.call-update) | async-done | bytes 262160 | tf_op jit(solution)/shard_map/while/body/eval_jaxpr/psum | solution.py:17
  1467.0 5.4 copy.28
  1487.9 16.0 dynamic_update_slice.8
  1505.2 93.3 %all-reduce.3.cloned.1.call-done = bf16[8,64,256]{2,1,0:T(8,128)(2,1)} async-done(((bf16[8,64,256]{2,1,0:T(8,128)(2,1)}), bf16[8,64,256]{2,1,0:T(8,128)(2,1)}) %all-reduce.3.cloned.1.call-update) | async-done | bytes 262160 | tf_op jit(solution)/shard_map/while/body/eval_jaxpr/psum | solution.py:17
  1615.2 5.4 copy.28
  1636.1 10.6 dynamic_update_slice.8
  1647.8 92.9 %all-reduce.3.cloned.1.call-done = bf16[8,64,256]{2,1,0:T(8,128)(2,1)} async-done(((bf16[8,64,256]{2,1,0:T(8,128)(2,1)}), bf16[8,64,256]{2,1,0:T(8,128)(2,1)}) %all-reduce.3.cloned.1.call-update) | async-done | bytes 262160 | tf_op jit(solution)/shard_map/while/body/eval_jaxpr/psum | solution.py:17
  1757.5 5.4 copy.28
  1778.4 16.0 dynamic_update_slice.8
  1795.7 93.3 %all-reduce.3.cloned.1.call-done = bf16[8,64,256]{2,1,0:T(8,128)(2,1)} async-done(((bf16[8,64,256]{2,1,0:T(8,128)(2,1)}), bf16[8,64,256]{2,1,0:T(8,128)(2,1)}) %all-reduce.3.cloned.1.call-update) | async-done | bytes 262160 | tf_op jit(solution)/shard_map/while/body/eval_jaxpr/psum | solution.py:17
  1905.7 5.4 copy.28
  1926.6 10.6 dynamic_update_slice.8
  1938.3 92.9 %all-reduce.3.cloned.1.call-done = bf16[8,64,256]{2,1,0:T(8,128)(2,1)} async-done(((bf16[8,64,256]{2,1,0:T(8,128)(2,1)}), bf16[8,64,256]{2,1,0:T(8,128)(2,1)}) %all-reduce.3.cloned.1.call-update) | async-done | bytes 262160 | tf_op jit(solution)/shard_map/while/body/eval_jaxpr/psum | solution.py:17
  2068.9 16.0 dynamic_update_slice.8
  2086.2 93.0 %all-reduce.3.cloned.1.call-done = bf16[8,64,256]{2,1,0:T(8,128)(2,1)} async-done(((bf16[8,64,256]{2,1,0:T(8,128)(2,1)}), bf16[8,64,256]{2,1,0:T(8,128)(2,1)}) %all-reduce.3.cloned.1.call-update) | async-done | bytes 262160 | tf_op jit(solution)/shard_map/while/body/eval_jaxpr/psum | solution.py:17
  2195.9 5.4 copy.28
  2216.8 9.9 dynamic_update_slice.8
  2227.8 92.9 %all-reduce.3.cloned.1.call-done = bf16[8,64,256]{2,1,0:T(8,128)(2,1)} async-done(((bf16[8,64,256]{2,1,0:T(8,128)(2,1)}), bf16[8,64,256]{2,1,0:T(8,128)(2,1)}) %all-reduce.3.cloned.1.call-update) | async-done | bytes 262160 | tf_op jit(solution)/shard_map/while/body/eval_jaxpr/psum | solution.py:17
  2358.4 15.3 dynamic_update_slice.8
  (311 shorter events, 555.9 us)
Async XLA Ops:
  54.4 91.2 %all-reduce.3.cloned.1.call-start = ((), (), s32[]{:S(2)}) async-start(), calls=%async_computation | async-start | bytes 524288 | tf_op jit(solution)/shard_map/while/body/eval_jaxpr/psum | solution.py:17
  193.8 94.5 %all-reduce.3.cloned.1.call-start = ((), (), s32[]{:S(2)}) async-start(), calls=%async_computation | async-start | bytes 524288 | tf_op jit(solution)/shard_map/while/body/eval_jaxpr/psum | solution.py:17
  342.0 94.5 %all-reduce.3.cloned.1.call-start = ((), (), s32[]{:S(2)}) async-start(), calls=%async_computation | async-start | bytes 524288 | tf_op jit(solution)/shard_map/while/body/eval_jaxpr/psum | solution.py:17
  484.6 94.2 %all-reduce.3.cloned.1.call-start = ((), (), s32[]{:S(2)}) async-start(), calls=%async_computation | async-start | bytes 524288 | tf_op jit(solution)/shard_map/while/body/eval_jaxpr/psum | solution.py:17
  632.5 94.2 %all-reduce.3.cloned.1.call-start = ((), (), s32[]{:S(2)}) async-start(), calls=%async_computation | async-start | bytes 524288 | tf_op jit(solution)/shard_map/while/body/eval_jaxpr/psum | solution.py:17
  774.8 94.2 %all-reduce.3.cloned.1.call-start = ((), (), s32[]{:S(2)}) async-start(), calls=%async_computation | async-start | bytes 524288 | tf_op jit(solution)/shard_map/while/body/eval_jaxpr/psum | solution.py:17
  922.6 94.5 %all-reduce.3.cloned.1.call-start = ((), (), s32[]{:S(2)}) async-start(), calls=%async_computation | async-start | bytes 524288 | tf_op jit(solution)/shard_map/while/body/eval_jaxpr/psum | solution.py:17
  1065.3 94.5 %all-reduce.3.cloned.1.call-start = ((), (), s32[]{:S(2)}) async-start(), calls=%async_computation | async-start | bytes 524288 | tf_op jit(solution)/shard_map/while/body/eval_jaxpr/psum | solution.py:17
  1213.5 94.5 %all-reduce.3.cloned.1.call-start = ((), (), s32[]{:S(2)}) async-start(), calls=%async_computation | async-start | bytes 524288 | tf_op jit(solution)/shard_map/while/body/eval_jaxpr/psum | solution.py:17
  1356.1 94.2 %all-reduce.3.cloned.1.call-start = ((), (), s32[]{:S(2)}) async-start(), calls=%async_computation | async-start | bytes 524288 | tf_op jit(solution)/shard_map/while/body/eval_jaxpr/psum | solution.py:17
  1504.0 94.5 %all-reduce.3.cloned.1.call-start = ((), (), s32[]{:S(2)}) async-start(), calls=%async_computation | async-start | bytes 524288 | tf_op jit(solution)/shard_map/while/body/eval_jaxpr/psum | solution.py:17
  1646.6 94.2 %all-reduce.3.cloned.1.call-start = ((), (), s32[]{:S(2)}) async-start(), calls=%async_computation | async-start | bytes 524288 | tf_op jit(solution)/shard_map/while/body/eval_jaxpr/psum | solution.py:17
  1794.5 94.5 %all-reduce.3.cloned.1.call-start = ((), (), s32[]{:S(2)}) async-start(), calls=%async_computation | async-start | bytes 524288 | tf_op jit(solution)/shard_map/while/body/eval_jaxpr/psum | solution.py:17
  1937.1 94.2 %all-reduce.3.cloned.1.call-start = ((), (), s32[]{:S(2)}) async-start(), calls=%async_computation | async-start | bytes 524288 | tf_op jit(solution)/shard_map/while/body/eval_jaxpr/psum | solution.py:17
  2085.0 94.2 %all-reduce.3.cloned.1.call-start = ((), (), s32[]{:S(2)}) async-start(), calls=%async_computation | async-start | bytes 524288 | tf_op jit(solution)/shard_map/while/body/eval_jaxpr/psum | solution.py:17
  2226.6 94.2 %all-reduce.3.cloned.1.call-start = ((), (), s32[]{:S(2)}) async-start(), calls=%async_computation | async-start | bytes 524288 | tf_op jit(solution)/shard_map/while/body/eval_jaxpr/psum | solution.py:17
Sparse Core Ops, SparseCore 0:
  58.6 87.0 all-reduce.2
  198.0 90.2 all-reduce.2
  346.1 90.2 all-reduce.2
  488.5 90.2 all-reduce.2
  636.3 90.2 all-reduce.2
  778.7 90.2 all-reduce.2
  926.8 90.2 all-reduce.2
  1069.5 90.2 all-reduce.2
  1217.6 90.2 all-reduce.2
  1360.0 90.2 all-reduce.2
  1508.1 90.2 all-reduce.2
  1650.5 90.2 all-reduce.2
  1798.6 90.2 all-reduce.2
  1941.0 90.2 all-reduce.2
  2088.8 90.2 all-reduce.2
  2230.5 90.2 all-reduce.2
where the time goes:
time: 2390 us; the launch traced here: 2380 us
  waiting for transfers between devices  1490 us (62%)
  local copies, waits for them, and re-layouts  572 us (24%)
  matrix products  192 us (8%)
  other arithmetic  77.3 us (3%)
  blocking collectives  36.6 us (2%)
    psum x16, waiting for transfers between devices, spread(): return lax.psum(jnp.where(mine, value, jnp.zeros_like(value)), axis)  1490 us
    dot_general x64, local copies, waits for them, and re-layouts, product(): jnp.einsum('wif,wjf->ijf', left, right, preferred_element_type=jnp.float32)  327 us
    dynamic_update_slice x16, local copies, waits for them, and re-layouts, visit(): lax.dynamic_update_slice(current, block, (jnp.int32(0), jnp.int32(0), sta...  211 us
    dot_general x64, matrix products, product(): jnp.einsum('wif,wjf->ijf', left, right, preferred_element_type=jnp.float32)  174 us
    sub x16, other arithmetic, pair_block(): imag_sum = product(own_imag, other_real) - product(own_real, other_imag)  60.6 us
  transfers between devices with their start and end apart: 16, of which 16 were waited for; matrix products, arithmetic and copies ran while one was open for 0% of the time, Pallas kernels for 0%

commit v1 on v0

v1 whole, which is shorter than its diff:
```python
import math

import jax
import jax.numpy as jnp
from jax import lax
from jax.sharding import PartitionSpec as P

NW = 256
NF = 128
HOP = 128
LAGS = 64
NWIN = 8


def forward_table(width, bins):
    samples = jnp.arange(width)
    freqs = jnp.arange(1, bins + 1)
    phase = samples[:, None] * freqs[None, :] % width
    theta = 2.0 * math.pi * phase.astype(jnp.float32) / width
    hann = 0.5 - 0.5 * jnp.cos(2.0 * math.pi * samples.astype(jnp.float32) / width)
    return jnp.concatenate(
        [hann[:, None] * jnp.cos(theta), -hann[:, None] * jnp.sin(theta)], axis=1
    )


def lag_rotation(width, bins, lag_count):
    freqs = jnp.arange(1, bins + 1)
    lags = jnp.arange(lag_count) - lag_count // 2
    phase = freqs[:, None] * lags[None, :] % width
    theta = 2.0 * math.pi * phase.astype(jnp.float32) / width
    return jnp.cos(theta), jnp.sin(theta)


def whiten(traces, good_mask):
    channels_here = traces.shape[0]
    good = good_mask.astype(jnp.float32)
    total, count = lax.psum((jnp.sum(traces * good[:, None], axis=0), jnp.sum(good)), "chan")
    common = total / jnp.maximum(count, 1.0)
    clean = (traces - common[None, :]) * good[:, None]
    halves = clean.reshape(channels_here, NWIN + 1, HOP)
    segments = jnp.concatenate([halves[:, :-1], halves[:, 1:]], axis=2)
    spectrum = jnp.einsum(
        "cwn,nk->wck", segments, forward_table(NW, NF), precision=lax.Precision.HIGHEST
    )
    real_part = spectrum[..., :NF]
    imag_part = spectrum[..., NF:]
    power = real_part * real_part + imag_part * imag_part
    magnitude = jnp.sqrt(power)
    level = jnp.sqrt(jnp.mean(power, axis=-1, keepdims=True) + 1e-06)
    denom = jnp.maximum(magnitude, 0.3 * level)
    return jnp.concatenate([real_part / denom, imag_part / denom], axis=-1).astype(jnp.bfloat16)


def shards(traces, good_mask):
    whitened = whiten(traces, good_mask)
    others = lax.all_gather(whitened, "chan", axis=1, tiled=True)
    own = whitened.astype(jnp.float32)
    own_real, own_imag = own[..., :NF], own[..., NF:]
    cos, sin = lag_rotation(NW, NF, LAGS)
    scale = 1.0 / (NWIN * NF)
    cos = cos * scale
    sin = sin * scale
    rot_real = own_real[:, :, None, :] * cos.T[None, None] - own_imag[:, :, None, :] * sin.T[None, None]
    rot_imag = own_real[:, :, None, :] * sin.T[None, None] + own_imag[:, :, None, :] * cos.T[None, None]
    rotated = jnp.concatenate([rot_real, rot_imag], axis=-1).astype(jnp.bfloat16)
    result = jnp.einsum(
        "wilk,wjk->ilj", rotated, others, preferred_element_type=jnp.float32
    )
    return result.astype(jnp.bfloat16)


def solution(mesh):
    placed = (P(("groups", "chan"), None), P(("groups", "chan")))
    return jax.shard_map(
        shards,
        mesh=mesh,
        in_specs=placed,
        out_specs=P(("groups", "chan"), None, None),
        check_vma=False,
    )
```

time: 2390 us -> 129 us (0.05)
  waiting for transfers between devices: 1490 us -> 39.7 us
  local copies, waits for them, and re-layouts: 572 us -> 0.55 us
  matrix products: 192 us -> 24.6 us
  other arithmetic: 77.3 us -> 13.4 us
    psum x16 -> x0, waiting for transfers between devices: 1490 us -> none  [spread(): return lax.psum(jnp.where(mine, value, jnp.zeros_like(value)), axis)]
    dot_general x64 -> x0, local copies, waits for them, and re-layouts: 327 us -> none  [product(): jnp.einsum('wif,wjf->ijf', left, right, preferred_element_type=jnp.float32)]
    dynamic_update_slice x16 -> x0, local copies, waits for them, and re-layouts: 211 us -> none  [visit(): lax.dynamic_update_slice(current, block, (jnp.int32(0), jnp.int32(0), sta...]
    dot_general x81 -> x2, matrix products: 192 us -> 24.6 us  [the longest x1 24 us: shards(): jnp.einsum('wilk,wjk->ilj', rotated, others, preferred_element_type=jnp.f...]
    sub x17 -> x1, other arithmetic: 60.6 us -> 0.01 us  [lag_rotation(): lags = jnp.arange(lag_count) - lag_count // 2]
    all_gather x0 -> x1, waiting for transfers between devices: none -> 39.7 us  [shards(): others = lax.all_gather(whitened, 'chan', axis=1, tiled=True)]
    slice x97 -> x4, local copies, waits for them, and re-layouts: 29.1 us -> 0.4 us  [the longest x3 0.36 us: shards(): own_real, own_imag = (own[..., :NF], own[..., NF:])]
  transfers between devices with their start and end apart: 16 -> 1, of which waited for: 16 -> 1; matrix products, arithmetic and copies ran while one was open for 0% -> 6% of each run, Pallas kernels for 0% -> 0%
where the time goes in v1:
time: 129 us
  waiting for transfers between devices  39.7 us (31%)
  blocking collectives  36.6 us (28%)
  matrix products  24.6 us (19%)
  between operations  14.1 us (11%)
  other arithmetic  13.4 us (10%)
    all_gather x1, waiting for transfers between devices, shards(): others = lax.all_gather(whitened, 'chan', axis=1, tiled=True)  39.7 us
    psum x1, blocking collectives, whiten(): lax.psum((jnp.sum(traces * good[:, None], axis=0), jnp.sum(good)), 'chan')  36.6 us
    dot_general x1, matrix products, shards(): jnp.einsum('wilk,wjk->ilj', rotated, others, preferred_element_type=jnp.f...  24 us
    another operation x2, other arithmetic  7.65 us
  transfers between devices with their start and end apart: 1, of which 1 were waited for; matrix products, arithmetic and copies ran while one was open for 6% of the time, Pallas kernels for 0%

profile of v1, /device:TPU:0, one launch (start us, length us, event | category | flops | bytes accessed | tf_op | source)
XLA Modules:
  0.0 129.0 jit_solution(4269690971907902461)
XLA Ops:
  6.5 0.0 all-gather.2.cloned.1.call-start
  6.5 1.3 convert_reduce_fusion
  7.8 0.7 convert_element_type.48
  8.5 1.1 multiply_reduce_fusion
  9.6 36.6 %all-reduce = (f32[1152]{0:T(1024)S(1)}, f32[]{:T(128)}) all-reduce(f32[1152]{0:T(1024)S(1)} %multiply_reduce_fusion, f32[]{:T(128)} %convert_reduce_fusion), channel_id=1, replica_groups=mesh['groups'=2,'chan'=16] {'chan'}, use_global_device_ids=true, to_apply=%region_1.0 | all-reduce | flops 1153 | bytes 9224 | tf_op jit(solution)/shard_map/psum | solution.py:37
  46.9 1.1 subtract_multiply_fusion
  48.0 0.1 copy.10
  48.1 0.1 copy.11
  48.2 0.5 cosine_multiply_fusion
  48.7 0.6 convolution_bitcast_fusion
  49.3 0.1 fusion.25
  49.5 0.2 divide_convert_fusion.1
  49.6 0.8 pad_maximum_fusion
  50.4 0.0 all-gather.2.cloned.1.call-update
  50.5 0.2 copy.7
  50.6 0.2 copy.8
  50.8 0.2 cosine_multiply_fusion.1
  51.0 7.5 %subtract_convert_fusion = (bf16[8,64,64,128]{3,2,0,1:T(8,128)(2,1)}, bf16[8,64,64,128]{3,2,0,1:T(8,128)(2,1)}) fusion(f32[64,128]{1,0:T(8,128)S(1)} %get-tuple-element.18, f32[8,64,128]{2,0,1:T(8,128)S(1)} %copy.8, f32[64,128]{1,0:T(8,128)S(1)} %get-tuple-element.17, f32[8,64,128]{2,0,1:T(8,128)S(1)} %copy.7), kind=kLoop, calls=%fused_computation.6 | loop fusion | flops 33554432 | bytes 17367040 | tf_op jit(solution)/shard_map/convert
  58.5 39.7 %all-gather.2.cloned.1.call-done = bf16[8,1024,256]{2,1,0:T(8,128)(2,1)} async-done(((bf16[8,64,256]{2,1,0:T(8,128)(2,1)}), bf16[8,1024,256]{2,1,0:T(8,128)(2,1)}) %all-gather.2.cloned.1.call-update) | async-done | bytes 4194320 | tf_op jit(solution)/shard_map/all_gather | solution.py:56
  98.2 24.0 %bitcast_convert_fusion = bf16[64,64,1024]{2,1,0:T(8,128)(2,1)} fusion(bf16[8,64,64,128]{3,2,0,1:T(8,128)(2,1)} %get-tuple-element.8, bf16[8,64,64,128]{3,2,0,1:T(8,128)(2,1)} %get-tuple-element.7, bf16[8,1024,256]{2,1,0:T(8,128)(2,1)} %all-gather.2.cloned.1.call-done), kind=kOutput, calls=%fused_computation.4 | convolution fusion | flops 17217617920 | bytes 29360128 | tf_op jit(solution)/shard_map/wilk,wjk->ilj/dot_general | solution.py:66
  (8 shorter events, 0.2 us)
Async XLA Ops:
  6.5 91.7 %all-gather.2.cloned.1.call-start = ((), (), s32[]{:S(2)}) async-start(), calls=%async_computation | async-start | bytes 4456448 | tf_op jit(solution)/shard_map/all_gather | solution.py:56
Sparse Core Ops, SparseCore 0:
  50.5 47.6 all-gather.1

commit v2 on v1

--- a/solution.py
+++ b/solution.py
@@ -10,6 +10,21 @@
 HOP = 128
 LAGS = 64
 NWIN = 8
+
+
+def butterfly_sum(value, axis, order):
+    size = lax.axis_size(axis)
+    steps = []
+    step = 1
+    while step < size:
+        steps.append(step)
+        step *= 2
+    if order == "far":
+        steps = steps[::-1]
+    for step in steps:
+        pairs = [(i, i ^ step) for i in range(size)]
+        value = value + lax.ppermute(value, axis, pairs)
+    return value
 
 
 def forward_table(width, bins):
@@ -34,7 +49,9 @@
 def whiten(traces, good_mask):
     channels_here = traces.shape[0]
     good = good_mask.astype(jnp.float32)
-    total, count = lax.psum((jnp.sum(traces * good[:, None], axis=0), jnp.sum(good)), "chan")
+    part = jnp.concatenate([jnp.sum(traces * good[:, None], axis=0), jnp.sum(good)[None]])
+    summed = butterfly_sum(part, "chan", "far")
+    total, count = summed[:-1], summed[-1]
     common = total / jnp.maximum(count, 1.0)
     clean = (traces - common[None, :]) * good[:, None]
     halves = clean.reshape(channels_here, NWIN + 1, HOP)

time: 129 us -> 112 us (0.87)
  blocking collectives: 36.6 us -> 0 us
  waiting for transfers between devices: 39.7 us -> 49.7 us
  starting transfers between devices: 0.01 us -> 7.96 us
  other arithmetic: 13.4 us -> 14.8 us
    psum x1 -> x0, blocking collectives: 36.6 us -> none  [whiten(): lax.psum((jnp.sum(traces * good[:, None], axis=0), jnp.sum(good)), 'chan')]
    ppermute x0 -> x4, starting transfers between devices: none -> 7.95 us  [butterfly_sum(): value = value + lax.ppermute(value, axis, pairs)]
    ppermute x0 -> x4, waiting for transfers between devices: none -> 5.76 us  [butterfly_sum(): value = value + lax.ppermute(value, axis, pairs)]
    all_gather x1, waiting for transfers between devices: 39.7 us -> 44 us  [shards(): others = lax.all_gather(whitened, 'chan', axis=1, tiled=True)]
  transfers between devices with their start and end apart: 1 -> 5, of which waited for: 1 -> 5; matrix products, arithmetic and copies ran while one was open for 6% -> 8% of each run, Pallas kernels for 0% -> 0%
where the time goes in v2:
time: 112 us
  waiting for transfers between devices  49.7 us (44%)
  matrix products  24.6 us (22%)
  other arithmetic  14.8 us (13%)
  between operations  14.2 us (13%)
  starting transfers between devices  7.96 us (7%)
    all_gather x1, waiting for transfers between devices, shards(): others = lax.all_gather(whitened, 'chan', axis=1, tiled=True)  44 us
    dot_general x1, matrix products, shards(): jnp.einsum('wilk,wjk->ilj', rotated, others, preferred_element_type=jnp.f...  24 us
    ppermute x4, starting transfers between devices, butterfly_sum(): value = value + lax.ppermute(value, axis, pairs)  7.95 us
    another operation x2, other arithmetic  7.72 us
    ppermute x4, waiting for transfers between devices, butterfly_sum(): value = value + lax.ppermute(value, axis, pairs)  5.76 us
  transfers between devices with their start and end apart: 5, of which 5 were waited for; matrix products, arithmetic and copies ran while one was open for 8% of the time, Pallas kernels for 0%

profile of v2, /device:TPU:0, one launch (start us, length us, event | category | flops | bytes accessed | tf_op | source)
XLA Modules:
  0.0 112.3 jit_solution(9401206487856603261)
XLA Ops:
  6.5 0.0 all-gather.2.cloned.1.call-start
  6.5 1.3 %convert_reduce_fusion = f32[]{:T(128)} fusion(s32[64]{0:T(128)} %param.3), kind=kLoop, calls=%fused_computation.52 | loop fusion | flops 127 | bytes 260 | tf_op jit(solution)/shard_map/reduce_sum | solution.py:52
  7.8 0.7 convert_element_type.48
  8.5 1.1 multiply_reduce_fusion
  9.5 0.7 pad_maximum_fusion.1
  10.2 4.1 %collective-permute-start = (f32[1153]{0:T(1024)S(1)}, f32[1153]{0:T(1024)S(1)}, u32[]{:S(2)}, u32[]{:S(2)}) collective-permute-start(f32[1153]{0:T(1024)S(1)} %pad_maximum_fusion.1), channel_id=1, source_target_pairs={{0,8},{1,9},{2,10},{3,11},{4,12},{5,13},{6,14},{7,15},{8,0},{9,1},... | collective-permute-start | bytes 13844 | tf_op jit(solution)/shard_map/ppermute | solution.py:26
  14.3 1.6 %collective-permute-done = f32[1153]{0:T(1024)S(1)} collective-permute-done((f32[1153]{0:T(1024)S(1)}, f32[1153]{0:T(1024)S(1)}, u32[]{:S(2)}, u32[]{:S(2)}) %collective-permute-start) | collective-permute-done | bytes 4644 | tf_op jit(solution)/shard_map/ppermute | solution.py:26
  15.9 0.7 fusion.28
  16.6 2.0 %collective-permute-start.1 = (f32[1153]{0:T(1024)S(1)}, f32[1153]{0:T(1024)S(1)}, u32[]{:S(2)}, u32[]{:S(2)}) collective-permute-start(f32[1153]{0:T(1024)S(1)} %fusion.28), channel_id=1, source_target_pairs={{0,4},{1,5},{2,6},{3,7},{4,0},{5,1},{6,2},{7,3},{8,12},{9,13},{10,... | collective-permute-start | bytes 13844 | tf_op jit(solution)/shard_map/ppermute | solution.py:26
  18.6 1.7 %collective-permute-done.1 = f32[1153]{0:T(1024)S(1)} collective-permute-done((f32[1153]{0:T(1024)S(1)}, f32[1153]{0:T(1024)S(1)}, u32[]{:S(2)}, u32[]{:S(2)}) %collective-permute-start.1) | collective-permute-done | bytes 4644 | tf_op jit(solution)/shard_map/ppermute | solution.py:26
  20.3 1.8 %collective-permute-start.2 = (f32[1153]{0:T(1024)S(1)}, f32[1153]{0:T(1024)S(1)}, u32[]{:S(2)}, u32[]{:S(2)}) collective-permute-start(f32[1153]{0:T(1024)S(1)} %add.88), channel_id=1, source_target_pairs={{0,2},{1,3},{2,0},{3,1},{4,6},{5,7},{6,4},{7,5},{8,10},{9,11},{10,... | collective-permute-start | bytes 13844 | tf_op jit(solution)/shard_map/ppermute | solution.py:26
  22.2 1.8 %collective-permute-done.2 = f32[1153]{0:T(1024)S(1)} collective-permute-done((f32[1153]{0:T(1024)S(1)}, f32[1153]{0:T(1024)S(1)}, u32[]{:S(2)}, u32[]{:S(2)}) %collective-permute-start.2) | collective-permute-done | bytes 4644 | tf_op jit(solution)/shard_map/ppermute | solution.py:26
  24.0 0.0 collective-permute-start.3
  24.0 0.5 cosine_multiply_fusion
  24.5 0.6 collective-permute-done.3
  25.2 0.5 slice.33
  26.3 1.1 subtract_multiply_fusion
  27.5 0.1 copy.10
  27.6 0.1 copy.11
  27.6 0.6 convolution_bitcast_fusion
  28.2 0.1 fusion.25
  28.4 0.2 divide_convert_fusion.1
  28.5 0.8 pad_maximum_fusion
  29.3 0.0 all-gather.2.cloned.1.call-update
  29.3 0.2 cosine_multiply_fusion.1
  29.6 0.2 copy.7
  29.8 0.2 copy.8
  29.9 7.6 %subtract_convert_fusion = (bf16[8,64,64,128]{3,2,0,1:T(8,128)(2,1)}, bf16[8,64,64,128]{3,2,0,1:T(8,128)(2,1)}) fusion(f32[64,128]{1,0:T(8,128)S(1)} %get-tuple-element.16, f32[8,64,128]{2,0,1:T(8,128)S(1)} %copy.8, f32[64,128]{1,0:T(8,128)S(1)} %get-tuple-element.15, f32[8,64,128]{2,0,1:T(8,128)S(1)} %copy.7), kind=kLoop, calls=%fused_computation.6 | loop fusion | flops 33554432 | bytes 17367040 | tf_op jit(solution)/shard_map/convert
  37.5 44.0 %all-gather.2.cloned.1.call-done = bf16[8,1024,256]{2,1,0:T(8,128)(2,1)} async-done(((bf16[8,64,256]{2,1,0:T(8,128)(2,1)}), bf16[8,1024,256]{2,1,0:T(8,128)(2,1)}) %all-gather.2.cloned.1.call-update) | async-done | bytes 4194320 | tf_op jit(solution)/shard_map/all_gather | solution.py:73
  81.5 24.0 %bitcast_convert_fusion = bf16[64,64,1024]{2,1,0:T(8,128)(2,1)} fusion(bf16[8,64,64,128]{3,2,0,1:T(8,128)(2,1)} %get-tuple-element.6, bf16[8,64,64,128]{3,2,0,1:T(8,128)(2,1)} %get-tuple-element.5, bf16[8,1024,256]{2,1,0:T(8,128)(2,1)} %all-gather.2.cloned.1.call-done), kind=kOutput, calls=%fused_computation.4 | convolution fusion | flops 17217617920 | bytes 29360128 | tf_op jit(solution)/shard_map/wilk,wjk->ilj/dot_general | solution.py:83
  (11 shorter events, 0.2 us)
Async XLA Ops:
  6.5 74.9 %all-gather.2.cloned.1.call-start = ((), (), s32[]{:S(2)}) async-start(), calls=%async_computation | async-start | bytes 4456448 | tf_op jit(solution)/shard_map/all_gather | solution.py:73
  10.2 5.8 %collective-permute-start = (f32[1153]{0:T(1024)S(1)}, f32[1153]{0:T(1024)S(1)}, u32[]{:S(2)}, u32[]{:S(2)}) collective-permute-start(f32[1153]{0:T(1024)S(1)} %pad_maximum_fusion.1), channel_id=1, source_target_pairs={{0,8},{1,9},{2,10},{3,11},{4,12},{5,13},{6,14},{7,15},{8,0},{9,1},... | collective-permute-start | bytes 13844 | tf_op jit(solution)/shard_map/ppermute | solution.py:26
  16.6 3.7 %collective-permute-start.1 = (f32[1153]{0:T(1024)S(1)}, f32[1153]{0:T(1024)S(1)}, u32[]{:S(2)}, u32[]{:S(2)}) collective-permute-start(f32[1153]{0:T(1024)S(1)} %fusion.28), channel_id=1, source_target_pairs={{0,4},{1,5},{2,6},{3,7},{4,0},{5,1},{6,2},{7,3},{8,12},{9,13},{10,... | collective-permute-start | bytes 13844 | tf_op jit(solution)/shard_map/ppermute | solution.py:26
  20.3 3.7 %collective-permute-start.2 = (f32[1153]{0:T(1024)S(1)}, f32[1153]{0:T(1024)S(1)}, u32[]{:S(2)}, u32[]{:S(2)}) collective-permute-start(f32[1153]{0:T(1024)S(1)} %add.88), channel_id=1, source_target_pairs={{0,2},{1,3},{2,0},{3,1},{4,6},{5,7},{6,4},{7,5},{8,10},{9,11},{10,... | collective-permute-start | bytes 13844 | tf_op jit(solution)/shard_map/ppermute | solution.py:26
  24.0 1.2 %collective-permute-start.3 = (f32[1153]{0:T(1024)S(1)}, f32[1153]{0:T(1024)S(1)}, u32[]{:S(2)}, u32[]{:S(2)}) collective-permute-start(f32[1153]{0:T(1024)S(1)} %add.89), channel_id=1, source_target_pairs={{0,1},{1,0},{2,3},{3,2},{4,5},{5,4},{6,7},{7,6},{8,9},{9,8},{10,11... | collective-permute-start | bytes 13844 | tf_op jit(solution)/shard_map/ppermute | solution.py:26
Sparse Core Ops, SparseCore 0:
  29.5 51.9 all-gather.1

commit v3 on v2

--- a/solution.py
+++ b/solution.py
@@ -1,3 +1,4 @@
+import functools
 import math
 
 import jax
@@ -68,9 +69,84 @@
     return jnp.concatenate([real_part / denom, imag_part / denom], axis=-1).astype(jnp.bfloat16)
 
 
-def shards(traces, good_mask):
-    whitened = whiten(traces, good_mask)
-    others = lax.all_gather(whitened, "chan", axis=1, tiled=True)
+def ring_plan(mesh):
+    row = list(mesh.devices.reshape(-1, mesh.devices.shape[-1])[0])
+    size = len(row)
+    coords = [tuple(getattr(d, "coords", (0, 0, i // 2))) for i, d in enumerate(row)]
+    cores = [getattr(d, "core_on_chip", i % 2) for i, d in enumerate(row)]
+    chips = size // 2
+    paired = size % 2 == 0 and all(
+        coords[2 * k] == coords[2 * k + 1] and cores[2 * k] == 0 and cores[2 * k + 1] == 1
+        for k in range(chips)
+    )
+    if not paired:
+        return None
+    places = [coords[2 * k] for k in range(chips)]
+    ys = sorted({p[1] for p in places})
+    if len(ys) == 2:
+        lower = sorted((k for k in range(chips) if places[k][1] == ys[0]), key=lambda k: places[k][2])
+        upper = sorted((k for k in range(chips) if places[k][1] == ys[1]), key=lambda k: -places[k][2])
+        cycle = lower + upper
+    else:
+        cycle = sorted(range(chips), key=lambda k: (places[k][1], places[k][2], places[k][0]))
+    position = {k: p for p, k in enumerate(cycle)}
+    return size, chips, cycle, position
+
+
+def correlate(whitened, rotated, plan):
+    size, chips, cycle, position = plan
+    here = whitened.shape[1]
+    me = lax.axis_index("chan")
+    my_chip = me // 2
+    is_first_core = (me % 2) == 0
+
+    def shifted(k, s):
+        return cycle[(position[k] + s) % chips]
+
+    def pairs(s):
+        return [(i, 2 * shifted(i // 2, s) + i % 2) for i in range(size)]
+
+    partner = [(i, i ^ 1) for i in range(size)]
+    forward, backward = pairs(1), pairs(-1)
+    forward_hops, backward_hops = chips // 2, (chips - 1) // 2
+    result = jnp.zeros((rotated.shape[1], rotated.shape[2], size * here), jnp.bfloat16)
+
+    def chip_block(mine, other):
+        first = jnp.where(is_first_core, mine, other)
+        second = jnp.where(is_first_core, other, mine)
+        return jnp.concatenate([first, second], axis=1)
+
+    def emit(result, pieces):
+        rhs = jnp.concatenate([block for _, block in pieces], axis=1)
+        out = jnp.einsum("wilk,wjk->ilj", rotated, rhs, preferred_element_type=jnp.float32)
+        out = out.astype(jnp.bfloat16)
+        for t, (table, _) in enumerate(pieces):
+            chip = jnp.asarray(table, jnp.int32)[my_chip]
+            piece = out[:, :, t * 2 * here:(t + 1) * 2 * here]
+            result = lax.dynamic_update_slice(result, piece, (0, 0, chip * 2 * here))
+        return result
+
+    own_partner = lax.ppermute(whitened, "chan", partner)
+    ahead = lax.ppermute(whitened, "chan", forward)
+    behind = lax.ppermute(whitened, "chan", backward) if backward_hops else None
+    result = emit(result, [(list(range(chips)), chip_block(whitened, own_partner))])
+    for s in range(1, forward_hops + 1):
+        ahead_partner = lax.ppermute(ahead, "chan", partner)
+        pieces = [([shifted(k, -s) for k in range(chips)], None)]
+        behind_partner = None
+        if s <= backward_hops:
+            behind_partner = lax.ppermute(behind, "chan", partner)
+        next_ahead = lax.ppermute(ahead, "chan", forward) if s < forward_hops else None
+        next_behind = lax.ppermute(behind, "chan", backward) if s < backward_hops else None
+        pieces = [([shifted(k, -s) for k in range(chips)], chip_block(ahead, ahead_partner))]
+        if s <= backward_hops:
+            pieces.append(([shifted(k, s) for k in range(chips)], chip_block(behind, behind_partner)))
+        result = emit(result, pieces)
+        ahead, behind = next_ahead, next_behind
+    return result
+
+
+def rotate(whitened):
     own = whitened.astype(jnp.float32)
     own_real, own_imag = own[..., :NF], own[..., NF:]
     cos, sin = lag_rotation(NW, NF, LAGS)
@@ -79,7 +155,15 @@
     sin = sin * scale
     rot_real = own_real[:, :, None, :] * cos.T[None, None] - own_imag[:, :, None, :] * sin.T[None, None]
     rot_imag = own_real[:, :, None, :] * sin.T[None, None] + own_imag[:, :, None, :] * cos.T[None, None]
-    rotated = jnp.concatenate([rot_real, rot_imag], axis=-1).astype(jnp.bfloat16)
+    return jnp.concatenate([rot_real, rot_imag], axis=-1).astype(jnp.bfloat16)
+
+
+def shards(traces, good_mask, plan=None):
+    whitened = whiten(traces, good_mask)
+    rotated = rotate(whitened)
+    if plan is not None:
+        return correlate(whitened, rotated, plan)
+    others = lax.all_gather(whitened, "chan", axis=1, tiled=True)
     result = jnp.einsum(
         "wilk,wjk->ilj", rotated, others, preferred_element_type=jnp.float32
     )
@@ -88,8 +172,9 @@
 
 def solution(mesh):
     placed = (P(("groups", "chan"), None), P(("groups", "chan")))
+    plan = ring_plan(mesh)
     return jax.shard_map(
-        shards,
+        functools.partial(shards, plan=plan),
         mesh=mesh,
         in_specs=placed,
         out_specs=P(("groups", "chan"), None, None),

time: 112 us -> 95 us (0.85)
  waiting for transfers between devices: 49.7 us -> 14.2 us
  local copies, waits for them, and re-layouts: 1.07 us -> 21.6 us
  between operations: 14.2 us -> 5.51 us
  starting transfers between devices: 7.96 us -> 15.6 us
  other arithmetic: 14.8 us -> 11.4 us
  matrix products: 24.6 us -> 26.3 us
    all_gather x1 -> x0, waiting for transfers between devices: 44 us -> none  [shards(): others = lax.all_gather(whitened, 'chan', axis=1, tiled=True)]
    dynamic_slice x0 -> x7, local copies, waits for them, and re-layouts: none -> 8.99 us  [emit(): chip = jnp.asarray(table, jnp.int32)[my_chip]]
    ppermute x0 -> x15, waiting for transfers between devices: none -> 8.49 us  [the longest x2 3.03 us: correlate(): lax.ppermute(behind, 'chan', backward)]
    ppermute x0 -> x15, starting transfers between devices: none -> 7.61 us  [the longest x2 3.15 us: correlate(): lax.ppermute(behind, 'chan', backward)]
    dynamic_update_slice x0 -> x6, local copies, waits for them, and re-layouts: none -> 7.05 us  [emit(): result = lax.dynamic_update_slice(result, piece, (0, 0, chip * 2 * here))]
    broadcast_in_dim x0 -> x1, local copies, waits for them, and re-layouts: none -> 4.47 us  [correlate(): jnp.zeros((rotated.shape[1], rotated.shape[2], size * here), jnp.bfloat16)]
    another operation x2, other arithmetic: 7.72 us -> 4.59 us
    dot_general x1 -> x5, matrix products: 24 us -> 25.7 us  [emit(): jnp.einsum('wilk,wjk->ilj', rotated, rhs, preferred_element_type=jnp.floa...]
  transfers between devices with their start and end apart: 5 -> 19, of which waited for: 5 -> 12; matrix products, arithmetic and copies ran while one was open for 8% -> 49% of each run, Pallas kernels for 0% -> 0%
where the time goes in v3:
time: 95 us; the launch traced here: 94.6 us
  matrix products  26.3 us (28%)
  local copies, waits for them, and re-layouts  21.6 us (23%)
  starting transfers between devices  15.6 us (16%)
  waiting for transfers between devices  14.2 us (15%)
  other arithmetic  11.4 us (12%)
  between operations  5.51 us (6%)
    dot_general x5, matrix products, emit(): jnp.einsum('wilk,wjk->ilj', rotated, rhs, preferred_element_type=jnp.floa...  25.7 us
    dynamic_slice x7, local copies, waits for them, and re-layouts, emit(): chip = jnp.asarray(table, jnp.int32)[my_chip]  8.99 us
    ppermute x4, starting transfers between devices, butterfly_sum(): value = value + lax.ppermute(value, axis, pairs)  7.95 us
    dynamic_update_slice x6, local copies, waits for them, and re-layouts, emit(): result = lax.dynamic_update_slice(result, piece, (0, 0, chip * 2 * here))  7.05 us
    ppermute x4, waiting for transfers between devices, butterfly_sum(): value = value + lax.ppermute(value, axis, pairs)  5.76 us
    another operation x2, other arithmetic  4.59 us
    broadcast_in_dim x1, local copies, waits for them, and re-layouts, correlate(): jnp.zeros((rotated.shape[1], rotated.shape[2], size * here), jnp.bfloat16)  4.47 us
    ppermute x2, starting transfers between devices, correlate(): lax.ppermute(behind, 'chan', backward)  3.15 us
  transfers between devices with their start and end apart: 19, of which 12 were waited for; matrix products, arithmetic and copies ran while one was open for 49% of the time, Pallas kernels for 0%

profile of v3, /device:TPU:0, one launch (start us, length us, event | category | flops | bytes accessed | tf_op | source)
XLA Modules:
  0.0 94.6 jit_solution(17153441798398289277)
XLA Ops:
  0.0 1.3 %convert_reduce_fusion = f32[]{:T(128)} fusion(s32[64]{0:T(128)} %param.11), kind=kLoop, calls=%fused_computation.107 | loop fusion | flops 127 | bytes 260 | tf_op jit(solution)/shard_map/reduce_sum | solution.py:53
  1.3 0.7 convert_element_type.60
  1.9 1.1 %multiply_reduce_fusion = f32[1152]{0:T(1024)S(1)} fusion(f32[64,1152]{1,0:T(8,128)} %param.10, f32[64]{0:T(128)S(1)} %convert_element_type.60), kind=kLoop, calls=%fused_computation.48 | loop fusion | flops 146304 | bytes 299776 | tf_op jit(solution)/shard_map/reduce_sum | solution.py:53
  3.0 0.7 pad_maximum_fusion.2
  3.6 4.1 %collective-permute-start = (f32[1153]{0:T(1024)S(1)}, f32[1153]{0:T(1024)S(1)}, u32[]{:S(2)}, u32[]{:S(2)}) collective-permute-start(f32[1153]{0:T(1024)S(1)} %pad_maximum_fusion.2), channel_id=1, source_target_pairs={{0,8},{1,9},{2,10},{3,11},{4,12},{5,13},{6,14},{7,15},{8,0},{9,1},... | collective-permute-start | bytes 13844 | tf_op jit(solution)/shard_map/ppermute | solution.py:27
  7.8 1.6 %collective-permute-done = f32[1153]{0:T(1024)S(1)} collective-permute-done((f32[1153]{0:T(1024)S(1)}, f32[1153]{0:T(1024)S(1)}, u32[]{:S(2)}, u32[]{:S(2)}) %collective-permute-start) | collective-permute-done | bytes 4644 | tf_op jit(solution)/shard_map/ppermute | solution.py:27
  9.4 0.7 fusion.49
  10.1 2.0 %collective-permute-start.1 = (f32[1153]{0:T(1024)S(1)}, f32[1153]{0:T(1024)S(1)}, u32[]{:S(2)}, u32[]{:S(2)}) collective-permute-start(f32[1153]{0:T(1024)S(1)} %fusion.49), channel_id=1, source_target_pairs={{0,4},{1,5},{2,6},{3,7},{4,0},{5,1},{6,2},{7,3},{8,12},{9,13},{10,... | collective-permute-start | bytes 13844 | tf_op jit(solution)/shard_map/ppermute | solution.py:27
  12.1 1.7 %collective-permute-done.1 = f32[1153]{0:T(1024)S(1)} collective-permute-done((f32[1153]{0:T(1024)S(1)}, f32[1153]{0:T(1024)S(1)}, u32[]{:S(2)}, u32[]{:S(2)}) %collective-permute-start.1) | collective-permute-done | bytes 4644 | tf_op jit(solution)/shard_map/ppermute | solution.py:27
  13.8 1.8 %collective-permute-start.2 = (f32[1153]{0:T(1024)S(1)}, f32[1153]{0:T(1024)S(1)}, u32[]{:S(2)}, u32[]{:S(2)}) collective-permute-start(f32[1153]{0:T(1024)S(1)} %add.127), channel_id=1, source_target_pairs={{0,2},{1,3},{2,0},{3,1},{4,6},{5,7},{6,4},{7,5},{8,10},{9,11},{10,... | collective-permute-start | bytes 13844 | tf_op jit(solution)/shard_map/ppermute | solution.py:27
  15.6 1.8 %collective-permute-done.2 = f32[1153]{0:T(1024)S(1)} collective-permute-done((f32[1153]{0:T(1024)S(1)}, f32[1153]{0:T(1024)S(1)}, u32[]{:S(2)}, u32[]{:S(2)}) %collective-permute-start.2) | collective-permute-done | bytes 4644 | tf_op jit(solution)/shard_map/ppermute | solution.py:27
  17.4 0.5 cosine_multiply_fusion
  18.0 0.6 collective-permute-done.3
  18.6 0.5 slice.57
  19.8 1.1 %subtract_multiply_fusion = f32[64,1152]{1,0:T(8,128)S(1)} fusion(f32[64,1152]{1,0:T(8,128)} %param.10, f32[1152]{0:T(1024)S(1)} %slice_divide_fusion, f32[64]{0:T(128)S(1)} %convert_element_type.60), kind=kLoop, calls=%fused_computation.47 | loop fusion | flops 147456 | bytes 594688 | tf_op jit(solution)/shard_map/mul | solution.py:57
  21.1 0.6 convolution_bitcast_fusion
  22.3 1.2 %dynamic_slice.25 = s32[1]{0:T(128)} dynamic-slice(s32[8]{0:T(128)} %constant.125.clone, s32[]{:T(128)S(6)} %select_n.149), dynamic_slice_sizes={1} | dynamic-slice | bytes 12 | tf_op jit(solution)/shard_map/dynamic_slice | solution.py:124
  24.2 1.3 %dynamic_slice.26 = s32[1]{0:T(128)} dynamic-slice(s32[8]{0:T(128)} %constant.126.clone, s32[]{:T(128)S(6)} %select_n.149), dynamic_slice_sizes={1} | dynamic-slice | bytes 12 | tf_op jit(solution)/shard_map/dynamic_slice | solution.py:124
  26.2 1.2 %dynamic_slice.27 = s32[1]{0:T(128)} dynamic-slice(s32[8]{0:T(128)} %constant.127.clone, s32[]{:T(128)S(6)} %select_n.149), dynamic_slice_sizes={1} | dynamic-slice | bytes 12 | tf_op jit(solution)/shard_map/dynamic_slice | solution.py:124
  28.0 1.3 %dynamic_slice.28 = s32[1]{0:T(128)} dynamic-slice(s32[8]{0:T(128)} %constant.128.clone, s32[]{:T(128)S(6)} %select_n.149), dynamic_slice_sizes={1} | dynamic-slice | bytes 12 | tf_op jit(solution)/shard_map/dynamic_slice | solution.py:124
  30.0 1.3 %dynamic_slice.29 = s32[1]{0:T(128)} dynamic-slice(s32[8]{0:T(128)} %constant.129.clone, s32[]{:T(128)S(6)} %select_n.149), dynamic_slice_sizes={1} | dynamic-slice | bytes 12 | tf_op jit(solution)/shard_map/dynamic_slice | solution.py:124
  32.0 1.3 %dynamic_slice.30 = s32[1]{0:T(128)} dynamic-slice(s32[8]{0:T(128)} %constant.130.clone, s32[]{:T(128)S(6)} %select_n.149), dynamic_slice_sizes={1} | dynamic-slice | bytes 12 | tf_op jit(solution)/shard_map/dynamic_slice | solution.py:124
  34.0 1.3 %dynamic_slice.31 = s32[1]{0:T(128)} dynamic-slice(s32[8]{0:T(128)} %constant.131.clone, s32[]{:T(128)S(6)} %select_n.149), dynamic_slice_sizes={1} | dynamic-slice | bytes 12 | tf_op jit(solution)/shard_map/dynamic_slice | solution.py:124
  36.1 1.9 %collective-permute-start.7 = (bf16[8,64,256]{2,1,0:T(8,128)(2,1)S(1)}, bf16[8,64,256]{2,1,0:T(8,128)(2,1)S(1)}, u32[]{:S(2)}, u32[]{:S(2)}) collective-permute-start(bf16[8,64,256]{2,1,0:T(8,128)(2,1)S(1)} %pad_maximum_fusion.1), channel_id=1, source_target_pairs={{0,2},{1,3},{2,6},{3,7},{4,0},{5,1},{6,10},{7,11},{8,4},{9,5},{10,... | collective-permute-start | bytes 786440 | tf_op jit(solution)/shard_map/ppermute | solution.py:131
  38.7 4.4 %subtract_convert_fusion = (bf16[8,64,64,128]{3,2,0,1:T(8,128)(2,1)S(1)}, bf16[8,64,64,128]{3,2,0,1:T(8,128)(2,1)S(1)}) fusion(f32[64,128]{1,0:T(8,128)S(1)} %get-tuple-element.31, f32[8,64,128]{2,0,1:T(8,128)S(1)} %copy.16, f32[64,128]{1,0:T(8,128)S(1)} %get-tuple-element.30, f32[8,64,128]{2,0,1:T(8,128)S(1)} %copy.15), kind=kLoop, calls=%fused_computation.2 | loop fusion | flops 33554432 | bytes 17367040 | tf_op jit(solution)/shard_map/convert
  43.2 1.7 %collective-permute-done.7 = bf16[8,64,256]{2,1,0:T(8,128)(2,1)S(1)} collective-permute-done((bf16[8,64,256]{2,1,0:T(8,128)(2,1)S(1)}, bf16[8,64,256]{2,1,0:T(8,128)(2,1)S(1)}, u32[]{:S(2)}, u32[]{:S(2)}) %collective-permute-start.7) | collective-permute-done | bytes 262176 | tf_op jit(solution)/shard_map/ppermute | solution.py:131
  44.9 1.4 %collective-permute-done.5 = bf16[8,64,256]{2,1,0:T(8,128)(2,1)S(1)} collective-permute-done((bf16[8,64,256]{2,1,0:T(8,128)(2,1)S(1)}, bf16[8,64,256]{2,1,0:T(8,128)(2,1)S(1)}, u32[]{:S(2)}, u32[]{:S(2)}) %collective-permute-start.5) | collective-permute-done | bytes 262176 | tf_op jit(solution)/shard_map/ppermute | solution.py:130
  46.3 4.5 %broadcast_in_dim.4 = bf16[64,64,1024]{2,1,0:T(8,128)(2,1)} broadcast(bf16[]{:T(256)} %constant.105.clone.1), dimensions={} | broadcast | bytes 8388610 | tf_op jit(solution)/shard_map/broadcast_in_dim | solution.py:112
  50.8 5.6 %fusion = bf16[64,64,1024]{2,1,0:T(8,128)(2,1)} fusion(bf16[64,64,1024]{2,1,0:T(8,128)(2,1)} %broadcast_in_dim.4, s32[]{:T(128)S(6)} %select_n.150, bf16[8,64,256]{2,1,0:T(8,128)(2,1)S(1)} %get-tuple-element.26, bf16[8,64,256]{2,1,0:T(8,128)(2,1)S(1)} %get-tuple-element.25, bf16[8,64,64,128]{3,2,0,1:T(8,128)(2,1)S(1)} %get-tuple-element.6, ...), kind=kOutput, calls=%fused_computation.8 | convolution fusion | flops 2182610944 | bytes 18350084 | tf_op jit(solution)/shard_map/wilk,wjk->ilj/dot_general | solution.py:121
  56.3 1.6 %collective-permute-start.11 = (bf16[8,64,256]{2,1,0:T(8,128)(2,1)S(1)}, bf16[8,64,256]{2,1,0:T(8,128)(2,1)S(1)}, u32[]{:S(2)}, u32[]{:S(2)}) collective-permute-start(bf16[8,64,256]{2,1,0:T(8,128)(2,1)S(1)} %collective-permute-done.7), channel_id=1, source_target_pairs={{0,2},{1,3},{2,6},{3,7},{4,0},{5,1},{6,10},{7,11},{8,4},{9,5},{10,... | collective-permute-start | bytes 786440 | tf_op jit(solution)/shard_map/ppermute | solution.py:140
  57.9 0.5 collective-permute-start.9
  58.5 4.8 %bitcast_convert_fusion.2 = bf16[64,64,256]{2,1,0:T(8,128)(2,1)S(1)} fusion(bf16[8,64,256]{2,1,0:T(8,128)(2,1)S(1)} %get-tuple-element.22, bf16[8,64,256]{2,1,0:T(8,128)(2,1)S(1)} %get-tuple-element.21, bf16[8,64,256]{2,1,0:T(8,128)(2,1)S(1)} %get-tuple-element.20, bf16[8,64,256]{2,1,0:T(8,128)(2,1)S(1)} %get-tuple-element.19, ...), kind=kOutput, calls=%fused_computation.5 | convolution fusion | flops 4333764608 | bytes 19922944 | tf_op jit(solution)/shard_map/wilk,wjk->ilj/dot_general | solution.py:121
  63.3 1.7 %collective-permute-done.11 = bf16[8,64,256]{2,1,0:T(8,128)(2,1)S(1)} collective-permute-done((bf16[8,64,256]{2,1,0:T(8,128)(2,1)S(1)}, bf16[8,64,256]{2,1,0:T(8,128)(2,1)S(1)}, u32[]{:S(2)}, u32[]{:S(2)}) %collective-permute-start.11) | collective-permute-done | bytes 262176 | tf_op jit(solution)/shard_map/ppermute | solution.py:140
  65.1 1.2 %slice_dynamic-update-slice_fusion.5 = bf16[64,64,1024]{2,1,0:T(8,128)(2,1)} fusion(bf16[64,64,1024]{2,1,0:T(8,128)(2,1)} %fusion, s32[]{:T(128)S(6)} %select_n.155, bf16[64,64,256]{2,1,0:T(8,128)(2,1)S(1)} %bitcast_convert_fusion.2), kind=kLoop, calls=%fused_computation.16 | loop fusion | bytes 2097156 | tf_op jit(solution)/shard_map/dynamic_update_slice | solution.py:126
  66.8 1.2 %slice_dynamic-update-slice_fusion.4 = bf16[64,64,1024]{2,1,0:T(8,128)(2,1)} fusion(bf16[64,64,1024]{2,1,0:T(8,128)(2,1)} %slice_dynamic-update-slice_fusion.5, s32[]{:T(128)S(6)} %select_n.156, bf16[64,64,256]{2,1,0:T(8,128)(2,1)S(1)} %bitcast_convert_fusion.2), kind=kLoop, calls=%fused_computation.15 | loop fusion | bytes 2097156 | tf_op jit(solution)/shard_map/dynamic_update_slice | solution.py:126
  67.9 1.6 %collective-permute-start.15 = (bf16[8,64,256]{2,1,0:T(8,128)(2,1)S(1)}, bf16[8,64,256]{2,1,0:T(8,128)(2,1)S(1)}, u32[]{:S(2)}, u32[]{:S(2)}) collective-permute-start(bf16[8,64,256]{2,1,0:T(8,128)(2,1)S(1)} %collective-permute-done.11), channel_id=1, source_target_pairs={{0,2},{1,3},{2,6},{3,7},{4,0},{5,1},{6,10},{7,11},{8,4},{9,5},{10,... | collective-permute-start | bytes 786440 | tf_op jit(solution)/shard_map/ppermute | solution.py:140
  69.5 0.4 collective-permute-start.13
  70.1 4.8 %bitcast_convert_fusion.1 = bf16[64,64,256]{2,1,0:T(8,128)(2,1)S(1)} fusion(bf16[8,64,256]{2,1,0:T(8,128)(2,1)S(1)} %get-tuple-element.18, bf16[8,64,256]{2,1,0:T(8,128)(2,1)S(1)} %get-tuple-element.17, bf16[8,64,256]{2,1,0:T(8,128)(2,1)S(1)} %get-tuple-element.16, bf16[8,64,256]{2,1,0:T(8,128)(2,1)S(1)} %get-tuple-element.15, ...), kind=kOutput, calls=%fused_computation.4 | convolution fusion | flops 4333764608 | bytes 19922944 | tf_op jit(solution)/shard_map/wilk,wjk->ilj/dot_general | solution.py:121
  74.9 1.3 %collective-permute-done.15 = bf16[8,64,256]{2,1,0:T(8,128)(2,1)S(1)} collective-permute-done((bf16[8,64,256]{2,1,0:T(8,128)(2,1)S(1)}, bf16[8,64,256]{2,1,0:T(8,128)(2,1)S(1)}, u32[]{:S(2)}, u32[]{:S(2)}) %collective-permute-start.15) | collective-permute-done | bytes 262176 | tf_op jit(solution)/shard_map/ppermute | solution.py:140
  76.3 1.2 %slice_dynamic-update-slice_fusion.3 = bf16[64,64,1024]{2,1,0:T(8,128)(2,1)} fusion(bf16[64,64,1024]{2,1,0:T(8,128)(2,1)} %slice_dynamic-update-slice_fusion.4, s32[]{:T(128)S(6)} %select_n.161, bf16[64,64,256]{2,1,0:T(8,128)(2,1)S(1)} %bitcast_convert_fusion.1), kind=kLoop, calls=%fused_computation.14 | loop fusion | bytes 2097156 | tf_op jit(solution)/shard_map/dynamic_update_slice | solution.py:126
  77.5 0.4 collective-permute-start.14
  77.9 1.2 %slice_dynamic-update-slice_fusion.2 = bf16[64,64,1024]{2,1,0:T(8,128)(2,1)} fusion(bf16[64,64,1024]{2,1,0:T(8,128)(2,1)} %slice_dynamic-update-slice_fusion.3, s32[]{:T(128)S(6)} %select_n.162, bf16[64,64,256]{2,1,0:T(8,128)(2,1)S(1)} %bitcast_convert_fusion.1), kind=kLoop, calls=%fused_computation.13 | loop fusion | bytes 2097156 | tf_op jit(solution)/shard_map/dynamic_update_slice | solution.py:126
  79.1 0.4 collective-permute-start.17
  79.7 4.8 %bitcast_convert_fusion = bf16[64,64,256]{2,1,0:T(8,128)(2,1)S(1)} fusion(bf16[8,64,256]{2,1,0:T(8,128)(2,1)S(1)} %get-tuple-element.14, bf16[8,64,256]{2,1,0:T(8,128)(2,1)S(1)} %get-tuple-element.13, bf16[8,64,256]{2,1,0:T(8,128)(2,1)S(1)} %get-tuple-element.12, bf16[8,64,256]{2,1,0:T(8,128)(2,1)S(1)} %get-tuple-element.11, ...), kind=kOutput, calls=%fused_computation.3 | convolution fusion | flops 4333764608 | bytes 19922944 | tf_op jit(solution)/shard_map/wilk,wjk->ilj/dot_general | solution.py:121
  84.5 1.2 %slice_dynamic-update-slice_fusion.1 = bf16[64,64,1024]{2,1,0:T(8,128)(2,1)} fusion(bf16[64,64,1024]{2,1,0:T(8,128)(2,1)} %slice_dynamic-update-slice_fusion.2, s32[]{:T(128)S(6)} %select_n.167, bf16[64,64,256]{2,1,0:T(8,128)(2,1)S(1)} %bitcast_convert_fusion), kind=kLoop, calls=%fused_computation.12 | loop fusion | bytes 2097156 | tf_op jit(solution)/shard_map/dynamic_update_slice | solution.py:126
  85.7 1.7 %collective-permute-done.17 = bf16[8,64,256]{2,1,0:T(8,128)(2,1)S(1)} collective-permute-done((bf16[8,64,256]{2,1,0:T(8,128)(2,1)S(1)}, bf16[8,64,256]{2,1,0:T(8,128)(2,1)S(1)}, u32[]{:S(2)}, u32[]{:S(2)}) %collective-permute-start.17) | collective-permute-done | bytes 262176 | tf_op jit(solution)/shard_map/ppermute | solution.py:139
  87.4 1.2 %slice_dynamic-update-slice_fusion = bf16[64,64,1024]{2,1,0:T(8,128)(2,1)} fusion(bf16[64,64,1024]{2,1,0:T(8,128)(2,1)} %slice_dynamic-update-slice_fusion.1, s32[]{:T(128)S(6)} %select_n.168, bf16[64,64,256]{2,1,0:T(8,128)(2,1)S(1)} %bitcast_convert_fusion), kind=kLoop, calls=%fused_computation.11 | loop fusion | bytes 2097156 | tf_op jit(solution)/shard_map/dynamic_update_slice | solution.py:126
  89.0 5.6 %fusion.1 = bf16[64,64,1024]{2,1,0:T(8,128)(2,1)} fusion(bf16[64,64,1024]{2,1,0:T(8,128)(2,1)} %slice_dynamic-update-slice_fusion, s32[]{:T(128)S(6)} %select_n.171, bf16[8,64,256]{2,1,0:T(8,128)(2,1)S(1)} %get-tuple-element.10, bf16[8,64,256]{2,1,0:T(8,128)(2,1)S(1)} %get-tuple-element.9, bf16[8,64,64,128]{3,2,0,1:T(8,128)(2,1)S(1)} %get-tuple-element.6, ...), kind=kOutput, calls=%fused_computation.9 | convolution fusion | flops 2182610944 | bytes 18350084 | tf_op jit(solution)/shard_map/wilk,wjk->ilj/dot_general | solution.py:121
  (46 shorter events, 3.1 us)
Async XLA Ops:
  3.6 5.8 %collective-permute-start = (f32[1153]{0:T(1024)S(1)}, f32[1153]{0:T(1024)S(1)}, u32[]{:S(2)}, u32[]{:S(2)}) collective-permute-start(f32[1153]{0:T(1024)S(1)} %pad_maximum_fusion.2), channel_id=1, source_target_pairs={{0,8},{1,9},{2,10},{3,11},{4,12},{5,13},{6,14},{7,15},{8,0},{9,1},... | collective-permute-start | bytes 13844 | tf_op jit(solution)/shard_map/ppermute | solution.py:27
  10.1 3.7 %collective-permute-start.1 = (f32[1153]{0:T(1024)S(1)}, f32[1153]{0:T(1024)S(1)}, u32[]{:S(2)}, u32[]{:S(2)}) collective-permute-start(f32[1153]{0:T(1024)S(1)} %fusion.49), channel_id=1, source_target_pairs={{0,4},{1,5},{2,6},{3,7},{4,0},{5,1},{6,2},{7,3},{8,12},{9,13},{10,... | collective-permute-start | bytes 13844 | tf_op jit(solution)/shard_map/ppermute | solution.py:27
  13.8 3.7 %collective-permute-start.2 = (f32[1153]{0:T(1024)S(1)}, f32[1153]{0:T(1024)S(1)}, u32[]{:S(2)}, u32[]{:S(2)}) collective-permute-start(f32[1153]{0:T(1024)S(1)} %add.127), channel_id=1, source_target_pairs={{0,2},{1,3},{2,0},{3,1},{4,6},{5,7},{6,4},{7,5},{8,10},{9,11},{10,... | collective-permute-start | bytes 13844 | tf_op jit(solution)/shard_map/ppermute | solution.py:27
  17.4 1.2 %collective-permute-start.3 = (f32[1153]{0:T(1024)S(1)}, f32[1153]{0:T(1024)S(1)}, u32[]{:S(2)}, u32[]{:S(2)}) collective-permute-start(f32[1153]{0:T(1024)S(1)} %add.128), channel_id=1, source_target_pairs={{0,1},{1,0},{2,3},{3,2},{4,5},{5,4},{6,7},{7,6},{8,9},{9,8},{10,11... | collective-permute-start | bytes 13844 | tf_op jit(solution)/shard_map/ppermute | solution.py:27
  22.1 16.1 %collective-permute-start.4 = (bf16[8,64,256]{2,1,0:T(8,128)(2,1)S(1)}, bf16[8,64,256]{2,1,0:T(8,128)(2,1)S(1)}, u32[]{:S(2)}, u32[]{:S(2)}) collective-permute-start(bf16[8,64,256]{2,1,0:T(8,128)(2,1)S(1)} %pad_maximum_fusion.1), channel_id=1, source_target_pairs={{0,1},{1,0},{2,3},{3,2},{4,5},{5,4},{6,7},{7,6},{8,9},{9,8},{10,11... | collective-permute-start | bytes 786440 | tf_op jit(solution)/shard_map/ppermute | solution.py:129
  36.1 8.8 %collective-permute-start.7 = (bf16[8,64,256]{2,1,0:T(8,128)(2,1)S(1)}, bf16[8,64,256]{2,1,0:T(8,128)(2,1)S(1)}, u32[]{:S(2)}, u32[]{:S(2)}) collective-permute-start(bf16[8,64,256]{2,1,0:T(8,128)(2,1)S(1)} %pad_maximum_fusion.1), channel_id=1, source_target_pairs={{0,2},{1,3},{2,6},{3,7},{4,0},{5,1},{6,10},{7,11},{8,4},{9,5},{10,... | collective-permute-start | bytes 786440 | tf_op jit(solution)/shard_map/ppermute | solution.py:131
  38.0 8.3 %collective-permute-start.5 = (bf16[8,64,256]{2,1,0:T(8,128)(2,1)S(1)}, bf16[8,64,256]{2,1,0:T(8,128)(2,1)S(1)}, u32[]{:S(2)}, u32[]{:S(2)}) collective-permute-start(bf16[8,64,256]{2,1,0:T(8,128)(2,1)S(1)} %pad_maximum_fusion.1), channel_id=1, source_target_pairs={{0,4},{1,5},{2,0},{3,1},{4,8},{5,9},{6,2},{7,3},{8,12},{9,13},{10,... | collective-permute-start | bytes 786440 | tf_op jit(solution)/shard_map/ppermute | solution.py:130
  44.9 13.5 %collective-permute-start.8 = (bf16[8,64,256]{2,1,0:T(8,128)(2,1)S(1)}, bf16[8,64,256]{2,1,0:T(8,128)(2,1)S(1)}, u32[]{:S(2)}, u32[]{:S(2)}) collective-permute-start(bf16[8,64,256]{2,1,0:T(8,128)(2,1)S(1)} %collective-permute-done.7), channel_id=1, source_target_pairs={{0,1},{1,0},{2,3},{3,2},{4,5},{5,4},{6,7},{7,6},{8,9},{9,8},{10,11... | collective-permute-start | bytes 786440 | tf_op jit(solution)/shard_map/ppermute | solution.py:138
  46.3 12.1 %collective-permute-start.6 = (bf16[8,64,256]{2,1,0:T(8,128)(2,1)S(1)}, bf16[8,64,256]{2,1,0:T(8,128)(2,1)S(1)}, u32[]{:S(2)}, u32[]{:S(2)}) collective-permute-start(bf16[8,64,256]{2,1,0:T(8,128)(2,1)S(1)} %collective-permute-done.5), channel_id=1, source_target_pairs={{0,1},{1,0},{2,3},{3,2},{4,5},{5,4},{6,7},{7,6},{8,9},{9,8},{10,11... | collective-permute-start | bytes 786440 | tf_op jit(solution)/shard_map/ppermute | solution.py:134
  56.3 8.7 %collective-permute-start.11 = (bf16[8,64,256]{2,1,0:T(8,128)(2,1)S(1)}, bf16[8,64,256]{2,1,0:T(8,128)(2,1)S(1)}, u32[]{:S(2)}, u32[]{:S(2)}) collective-permute-start(bf16[8,64,256]{2,1,0:T(8,128)(2,1)S(1)} %collective-permute-done.7), channel_id=1, source_target_pairs={{0,2},{1,3},{2,6},{3,7},{4,0},{5,1},{6,10},{7,11},{8,4},{9,5},{10,... | collective-permute-start | bytes 786440 | tf_op jit(solution)/shard_map/ppermute | solution.py:140
  57.9 8.4 %collective-permute-start.9 = (bf16[8,64,256]{2,1,0:T(8,128)(2,1)S(1)}, bf16[8,64,256]{2,1,0:T(8,128)(2,1)S(1)}, u32[]{:S(2)}, u32[]{:S(2)}) collective-permute-start(bf16[8,64,256]{2,1,0:T(8,128)(2,1)S(1)} %collective-permute-done.5), channel_id=1, source_target_pairs={{0,4},{1,5},{2,0},{3,1},{4,8},{5,9},{6,2},{7,3},{8,12},{9,13},{10,... | collective-permute-start | bytes 786440 | tf_op jit(solution)/shard_map/ppermute | solution.py:139
  65.1 4.9 %collective-permute-start.12 = (bf16[8,64,256]{2,1,0:T(8,128)(2,1)S(1)}, bf16[8,64,256]{2,1,0:T(8,128)(2,1)S(1)}, u32[]{:S(2)}, u32[]{:S(2)}) collective-permute-start(bf16[8,64,256]{2,1,0:T(8,128)(2,1)S(1)} %collective-permute-done.11), channel_id=1, source_target_pairs={{0,1},{1,0},{2,3},{3,2},{4,5},{5,4},{6,7},{7,6},{8,9},{9,8},{10,11... | collective-permute-start | bytes 786440 | tf_op jit(solution)/shard_map/ppermute | solution.py:138
  66.4 3.7 %collective-permute-start.10 = (bf16[8,64,256]{2,1,0:T(8,128)(2,1)S(1)}, bf16[8,64,256]{2,1,0:T(8,128)(2,1)S(1)}, u32[]{:S(2)}, u32[]{:S(2)}) collective-permute-start(bf16[8,64,256]{2,1,0:T(8,128)(2,1)S(1)} %collective-permute-done.9), channel_id=1, source_target_pairs={{0,1},{1,0},{2,3},{3,2},{4,5},{5,4},{6,7},{7,6},{8,9},{9,8},{10,11... | collective-permute-start | bytes 786440 | tf_op jit(solution)/shard_map/ppermute | solution.py:134
  67.9 8.3 %collective-permute-start.15 = (bf16[8,64,256]{2,1,0:T(8,128)(2,1)S(1)}, bf16[8,64,256]{2,1,0:T(8,128)(2,1)S(1)}, u32[]{:S(2)}, u32[]{:S(2)}) collective-permute-start(bf16[8,64,256]{2,1,0:T(8,128)(2,1)S(1)} %collective-permute-done.11), channel_id=1, source_target_pairs={{0,2},{1,3},{2,6},{3,7},{4,0},{5,1},{6,10},{7,11},{8,4},{9,5},{10,... | collective-permute-start | bytes 786440 | tf_op jit(solution)/shard_map/ppermute | solution.py:140
  69.5 8.0 %collective-permute-start.13 = (bf16[8,64,256]{2,1,0:T(8,128)(2,1)S(1)}, bf16[8,64,256]{2,1,0:T(8,128)(2,1)S(1)}, u32[]{:S(2)}, u32[]{:S(2)}) collective-permute-start(bf16[8,64,256]{2,1,0:T(8,128)(2,1)S(1)} %collective-permute-done.9), channel_id=1, source_target_pairs={{0,4},{1,5},{2,0},{3,1},{4,8},{5,9},{6,2},{7,3},{8,12},{9,13},{10,... | collective-permute-start | bytes 786440 | tf_op jit(solution)/shard_map/ppermute | solution.py:139
  76.2 3.3 %collective-permute-start.16 = (bf16[8,64,256]{2,1,0:T(8,128)(2,1)S(1)}, bf16[8,64,256]{2,1,0:T(8,128)(2,1)S(1)}, u32[]{:S(2)}, u32[]{:S(2)}) collective-permute-start(bf16[8,64,256]{2,1,0:T(8,128)(2,1)S(1)} %collective-permute-done.15), channel_id=1, source_target_pairs={{0,1},{1,0},{2,3},{3,2},{4,5},{5,4},{6,7},{7,6},{8,9},{9,8},{10,11... | collective-permute-start | bytes 786440 | tf_op jit(solution)/shard_map/ppermute | solution.py:138
  77.5 2.1 %collective-permute-start.14 = (bf16[8,64,256]{2,1,0:T(8,128)(2,1)S(1)}, bf16[8,64,256]{2,1,0:T(8,128)(2,1)S(1)}, u32[]{:S(2)}, u32[]{:S(2)}) collective-permute-start(bf16[8,64,256]{2,1,0:T(8,128)(2,1)S(1)} %collective-permute-done.13), channel_id=1, source_target_pairs={{0,1},{1,0},{2,3},{3,2},{4,5},{5,4},{6,7},{7,6},{8,9},{9,8},{10,11... | collective-permute-start | bytes 786440 | tf_op jit(solution)/shard_map/ppermute | solution.py:134
  79.1 8.3 %collective-permute-start.17 = (bf16[8,64,256]{2,1,0:T(8,128)(2,1)S(1)}, bf16[8,64,256]{2,1,0:T(8,128)(2,1)S(1)}, u32[]{:S(2)}, u32[]{:S(2)}) collective-permute-start(bf16[8,64,256]{2,1,0:T(8,128)(2,1)S(1)} %collective-permute-done.13), channel_id=1, source_target_pairs={{0,4},{1,5},{2,0},{3,1},{4,8},{5,9},{6,2},{7,3},{8,12},{9,13},{10,... | collective-permute-start | bytes 786440 | tf_op jit(solution)/shard_map/ppermute | solution.py:139
  87.4 1.5 %collective-permute-start.18 = (bf16[8,64,256]{2,1,0:T(8,128)(2,1)S(1)}, bf16[8,64,256]{2,1,0:T(8,128)(2,1)S(1)}, u32[]{:S(2)}, u32[]{:S(2)}) collective-permute-start(bf16[8,64,256]{2,1,0:T(8,128)(2,1)S(1)} %collective-permute-done.17), channel_id=1, source_target_pairs={{0,1},{1,0},{2,3},{3,2},{4,5},{5,4},{6,7},{7,6},{8,9},{9,8},{10,11... | collective-permute-start | bytes 786440 | tf_op jit(solution)/shard_map/ppermute | solution.py:134

commit v4 on v3

--- a/solution.py
+++ b/solution.py
@@ -116,12 +116,17 @@
         second = jnp.where(is_first_core, other, mine)
         return jnp.concatenate([first, second], axis=1)
 
+    shifts = [0] + [s for h in range(1, forward_hops + 1) for s in ((-h, h) if h <= backward_hops else (-h,))]
+    table = jnp.asarray([[shifted(k, s) for s in shifts] for k in range(chips)], jnp.int32)
+    placed_chips = table[my_chip]
+    slot = {s: n for n, s in enumerate(shifts)}
+
     def emit(result, pieces):
         rhs = jnp.concatenate([block for _, block in pieces], axis=1)
         out = jnp.einsum("wilk,wjk->ilj", rotated, rhs, preferred_element_type=jnp.float32)
         out = out.astype(jnp.bfloat16)
-        for t, (table, _) in enumerate(pieces):
-            chip = jnp.asarray(table, jnp.int32)[my_chip]
+        for t, (s, _) in enumerate(pieces):
+            chip = placed_chips[slot[s]]
             piece = out[:, :, t * 2 * here:(t + 1) * 2 * here]
             result = lax.dynamic_update_slice(result, piece, (0, 0, chip * 2 * here))
         return result
@@ -129,18 +134,17 @@
     own_partner = lax.ppermute(whitened, "chan", partner)
     ahead = lax.ppermute(whitened, "chan", forward)
     behind = lax.ppermute(whitened, "chan", backward) if backward_hops else None
-    result = emit(result, [(list(range(chips)), chip_block(whitened, own_partner))])
+    result = emit(result, [(0, chip_block(whitened, own_partner))])
     for s in range(1, forward_hops + 1):
         ahead_partner = lax.ppermute(ahead, "chan", partner)
-        pieces = [([shifted(k, -s) for k in range(chips)], None)]
         behind_partner = None
         if s <= backward_hops:
             behind_partner = lax.ppermute(behind, "chan", partner)
         next_ahead = lax.ppermute(ahead, "chan", forward) if s < forward_hops else None
         next_behind = lax.ppermute(behind, "chan", backward) if s < backward_hops else None
-        pieces = [([shifted(k, -s) for k in range(chips)], chip_block(ahead, ahead_partner))]
+        pieces = [(-s, chip_block(ahead, ahead_partner))]
         if s <= backward_hops:
-            pieces.append(([shifted(k, s) for k in range(chips)], chip_block(behind, behind_partner)))
+            pieces.append((s, chip_block(behind, behind_partner)))
         result = emit(result, pieces)
         ahead, behind = next_ahead, next_behind
     return result

time: 95 us -> 86.5 us (0.911)
  local copies, waits for them, and re-layouts: 21.6 us -> 14 us
  waiting for transfers between devices: 14.2 us -> 12.8 us
    dynamic_slice x7 -> x1, local copies, waits for them, and re-layouts: 8.99 us -> 0.69 us  [correlate(): placed_chips = table[my_chip]]
    ppermute x4, waiting for transfers between devices: 5.76 us -> 4.37 us  [butterfly_sum(): value = value + lax.ppermute(value, axis, pairs)]
  transfers between devices with their start and end apart: 19 -> 19, of which waited for: 12 -> 12; matrix products, arithmetic and copies ran while one was open for 49% -> 45% of each run, Pallas kernels for 0% -> 0%
where the time goes in v4:
time: 86.5 us; the launch traced here: 86.2 us
  matrix products  26.3 us (30%)
  starting transfers between devices  15.6 us (18%)
  local copies, waits for them, and re-layouts  14 us (16%)
  waiting for transfers between devices  12.8 us (15%)
  other arithmetic  11.4 us (13%)
  between operations  6.02 us (7%)
    dot_general x5, matrix products, emit(): jnp.einsum('wilk,wjk->ilj', rotated, rhs, preferred_element_type=jnp.floa...  25.7 us
    ppermute x4, starting transfers between devices, butterfly_sum(): value = value + lax.ppermute(value, axis, pairs)  7.95 us
    dynamic_update_slice x6, local copies, waits for them, and re-layouts, emit(): result = lax.dynamic_update_slice(result, piece, (0, 0, chip * 2 * here))  7.05 us
    another operation x2, other arithmetic  4.59 us
    broadcast_in_dim x1, local copies, waits for them, and re-layouts, correlate(): jnp.zeros((rotated.shape[1], rotated.shape[2], size * here), jnp.bfloat16)  4.47 us
    ppermute x4, waiting for transfers between devices, butterfly_sum(): value = value + lax.ppermute(value, axis, pairs)  4.37 us
    ppermute x2, starting transfers between devices, correlate(): lax.ppermute(behind, 'chan', backward)  3.14 us
    ppermute x2, waiting for transfers between devices, correlate(): lax.ppermute(behind, 'chan', backward)  3.02 us
  transfers between devices with their start and end apart: 19, of which 12 were waited for; matrix products, arithmetic and copies ran while one was open for 45% of the time, Pallas kernels for 0%

profile of v4, /device:TPU:0, one launch (start us, length us, event | category | flops | bytes accessed | tf_op | source)
XLA Modules:
  0.0 86.2 jit_solution(13878334499015269849)
XLA Ops:
  0.0 1.3 %convert_reduce_fusion = f32[]{:T(128)} fusion(s32[64]{0:T(128)} %param.4), kind=kLoop, calls=%fused_computation.108 | loop fusion | flops 127 | bytes 260 | tf_op jit(solution)/shard_map/reduce_sum | solution.py:53
  1.3 0.7 convert_element_type.60
  1.9 1.1 %multiply_reduce_fusion = f32[1152]{0:T(1024)S(1)} fusion(f32[64,1152]{1,0:T(8,128)} %param.3, f32[64]{0:T(128)S(1)} %convert_element_type.60), kind=kLoop, calls=%fused_computation.48 | loop fusion | flops 146304 | bytes 299776 | tf_op jit(solution)/shard_map/reduce_sum | solution.py:53
  3.0 0.7 pad_maximum_fusion.2
  3.6 4.1 %collective-permute-start = (f32[1153]{0:T(1024)S(1)}, f32[1153]{0:T(1024)S(1)}, u32[]{:S(2)}, u32[]{:S(2)}) collective-permute-start(f32[1153]{0:T(1024)S(1)} %pad_maximum_fusion.2), channel_id=1, source_target_pairs={{0,8},{1,9},{2,10},{3,11},{4,12},{5,13},{6,14},{7,15},{8,0},{9,1},... | collective-permute-start | bytes 13844 | tf_op jit(solution)/shard_map/ppermute | solution.py:27
  7.8 1.6 %collective-permute-done = f32[1153]{0:T(1024)S(1)} collective-permute-done((f32[1153]{0:T(1024)S(1)}, f32[1153]{0:T(1024)S(1)}, u32[]{:S(2)}, u32[]{:S(2)}) %collective-permute-start) | collective-permute-done | bytes 4644 | tf_op jit(solution)/shard_map/ppermute | solution.py:27
  9.4 0.7 fusion.50
  10.1 2.0 %collective-permute-start.1 = (f32[1153]{0:T(1024)S(1)}, f32[1153]{0:T(1024)S(1)}, u32[]{:S(2)}, u32[]{:S(2)}) collective-permute-start(f32[1153]{0:T(1024)S(1)} %fusion.50), channel_id=1, source_target_pairs={{0,4},{1,5},{2,6},{3,7},{4,0},{5,1},{6,2},{7,3},{8,12},{9,13},{10,... | collective-permute-start | bytes 13844 | tf_op jit(solution)/shard_map/ppermute | solution.py:27
  12.0 0.5 cosine_multiply_fusion
  12.6 1.2 %collective-permute-done.1 = f32[1153]{0:T(1024)S(1)} collective-permute-done((f32[1153]{0:T(1024)S(1)}, f32[1153]{0:T(1024)S(1)}, u32[]{:S(2)}, u32[]{:S(2)}) %collective-permute-start.1) | collective-permute-done | bytes 4644 | tf_op jit(solution)/shard_map/ppermute | solution.py:27
  13.8 1.8 %collective-permute-start.2 = (f32[1153]{0:T(1024)S(1)}, f32[1153]{0:T(1024)S(1)}, u32[]{:S(2)}, u32[]{:S(2)}) collective-permute-start(f32[1153]{0:T(1024)S(1)} %add.120), channel_id=1, source_target_pairs={{0,2},{1,3},{2,0},{3,1},{4,6},{5,7},{6,4},{7,5},{8,10},{9,11},{10,... | collective-permute-start | bytes 13844 | tf_op jit(solution)/shard_map/ppermute | solution.py:27
  15.6 0.7 constant_dynamic-slice_fusion
  16.3 1.1 %collective-permute-done.2 = f32[1153]{0:T(1024)S(1)} collective-permute-done((f32[1153]{0:T(1024)S(1)}, f32[1153]{0:T(1024)S(1)}, u32[]{:S(2)}, u32[]{:S(2)}) %collective-permute-start.2) | collective-permute-done | bytes 4644 | tf_op jit(solution)/shard_map/ppermute | solution.py:27
  17.4 0.7 fusion.49
  18.1 0.5 collective-permute-done.3
  18.6 0.6 slice.97
  19.9 1.1 %subtract_multiply_fusion = f32[64,1152]{1,0:T(8,128)S(1)} fusion(f32[64,1152]{1,0:T(8,128)} %param.3, f32[1152]{0:T(1024)S(1)} %slice_divide_fusion, f32[64]{0:T(128)S(1)} %convert_element_type.60), kind=kLoop, calls=%fused_computation.47 | loop fusion | flops 147456 | bytes 594688 | tf_op jit(solution)/shard_map/mul | solution.py:57
  21.2 0.6 convolution_bitcast_fusion
  22.2 0.2 collective-permute-start.4
  27.5 0.2 cosine_multiply_fusion.1
  27.7 1.9 %collective-permute-start.7 = (bf16[8,64,256]{2,1,0:T(8,128)(2,1)S(1)}, bf16[8,64,256]{2,1,0:T(8,128)(2,1)S(1)}, u32[]{:S(2)}, u32[]{:S(2)}) collective-permute-start(bf16[8,64,256]{2,1,0:T(8,128)(2,1)S(1)} %pad_maximum_fusion.1), channel_id=1, source_target_pairs={{0,2},{1,3},{2,6},{3,7},{4,0},{5,1},{6,10},{7,11},{8,4},{9,5},{10,... | collective-permute-start | bytes 786440 | tf_op jit(solution)/shard_map/ppermute | solution.py:136
  29.6 0.2 collective-permute-start.5
  30.3 4.4 %subtract_convert_fusion = (bf16[8,64,64,128]{3,2,0,1:T(8,128)(2,1)S(1)}, bf16[8,64,64,128]{3,2,0,1:T(8,128)(2,1)S(1)}) fusion(f32[64,128]{1,0:T(8,128)S(1)} %get-tuple-element.31, f32[8,64,128]{2,0,1:T(8,128)S(1)} %copy.9, f32[64,128]{1,0:T(8,128)S(1)} %get-tuple-element.30, f32[8,64,128]{2,0,1:T(8,128)S(1)} %copy.8), kind=kLoop, calls=%fused_computation.2 | loop fusion | flops 33554432 | bytes 17367040 | tf_op jit(solution)/shard_map/convert
  34.7 1.7 %collective-permute-done.7 = bf16[8,64,256]{2,1,0:T(8,128)(2,1)S(1)} collective-permute-done((bf16[8,64,256]{2,1,0:T(8,128)(2,1)S(1)}, bf16[8,64,256]{2,1,0:T(8,128)(2,1)S(1)}, u32[]{:S(2)}, u32[]{:S(2)}) %collective-permute-start.7) | collective-permute-done | bytes 262176 | tf_op jit(solution)/shard_map/ppermute | solution.py:136
  36.5 1.4 %collective-permute-done.5 = bf16[8,64,256]{2,1,0:T(8,128)(2,1)S(1)} collective-permute-done((bf16[8,64,256]{2,1,0:T(8,128)(2,1)S(1)}, bf16[8,64,256]{2,1,0:T(8,128)(2,1)S(1)}, u32[]{:S(2)}, u32[]{:S(2)}) %collective-permute-start.5) | collective-permute-done | bytes 262176 | tf_op jit(solution)/shard_map/ppermute | solution.py:135
  37.9 4.5 %broadcast_in_dim.4 = bf16[64,64,1024]{2,1,0:T(8,128)(2,1)} broadcast(bf16[]{:T(256)} %constant.91.clone.1), dimensions={} | broadcast | bytes 8388610 | tf_op jit(solution)/shard_map/broadcast_in_dim | solution.py:112
  42.4 5.6 %fusion = bf16[64,64,1024]{2,1,0:T(8,128)(2,1)} fusion(bf16[64,64,1024]{2,1,0:T(8,128)(2,1)} %broadcast_in_dim.4, s32[]{:T(128)S(6)} %select_n.143, bf16[8,64,256]{2,1,0:T(8,128)(2,1)S(1)} %get-tuple-element.26, bf16[8,64,256]{2,1,0:T(8,128)(2,1)S(1)} %get-tuple-element.25, bf16[8,64,64,128]{3,2,0,1:T(8,128)(2,1)S(1)} %get-tuple-element.6, ...), kind=kOutput, calls=%fused_computation.8 | convolution fusion | flops 2182610944 | bytes 18350084 | tf_op jit(solution)/shard_map/wilk,wjk->ilj/dot_general | solution.py:126
  47.9 1.6 %collective-permute-start.11 = (bf16[8,64,256]{2,1,0:T(8,128)(2,1)S(1)}, bf16[8,64,256]{2,1,0:T(8,128)(2,1)S(1)}, u32[]{:S(2)}, u32[]{:S(2)}) collective-permute-start(bf16[8,64,256]{2,1,0:T(8,128)(2,1)S(1)} %collective-permute-done.7), channel_id=1, source_target_pairs={{0,2},{1,3},{2,6},{3,7},{4,0},{5,1},{6,10},{7,11},{8,4},{9,5},{10,... | collective-permute-start | bytes 786440 | tf_op jit(solution)/shard_map/ppermute | solution.py:144
  49.5 0.4 collective-permute-start.9
  50.1 4.8 %bitcast_convert_fusion.2 = bf16[64,64,256]{2,1,0:T(8,128)(2,1)S(1)} fusion(bf16[8,64,256]{2,1,0:T(8,128)(2,1)S(1)} %get-tuple-element.22, bf16[8,64,256]{2,1,0:T(8,128)(2,1)S(1)} %get-tuple-element.21, bf16[8,64,256]{2,1,0:T(8,128)(2,1)S(1)} %get-tuple-element.20, bf16[8,64,256]{2,1,0:T(8,128)(2,1)S(1)} %get-tuple-element.19, ...), kind=kOutput, calls=%fused_computation.5 | convolution fusion | flops 4333764608 | bytes 19922944 | tf_op jit(solution)/shard_map/wilk,wjk->ilj/dot_general | solution.py:126
  54.9 1.7 %collective-permute-done.11 = bf16[8,64,256]{2,1,0:T(8,128)(2,1)S(1)} collective-permute-done((bf16[8,64,256]{2,1,0:T(8,128)(2,1)S(1)}, bf16[8,64,256]{2,1,0:T(8,128)(2,1)S(1)}, u32[]{:S(2)}, u32[]{:S(2)}) %collective-permute-start.11) | collective-permute-done | bytes 262176 | tf_op jit(solution)/shard_map/ppermute | solution.py:144
  56.7 1.2 %slice_dynamic-update-slice_fusion.5 = bf16[64,64,1024]{2,1,0:T(8,128)(2,1)} fusion(bf16[64,64,1024]{2,1,0:T(8,128)(2,1)} %fusion, s32[]{:T(128)S(6)} %select_n.148, bf16[64,64,256]{2,1,0:T(8,128)(2,1)S(1)} %bitcast_convert_fusion.2), kind=kLoop, calls=%fused_computation.16 | loop fusion | bytes 2097156 | tf_op jit(solution)/shard_map/dynamic_update_slice | solution.py:131
  57.9 0.4 collective-permute-start.10
  58.3 1.2 %slice_dynamic-update-slice_fusion.4 = bf16[64,64,1024]{2,1,0:T(8,128)(2,1)} fusion(bf16[64,64,1024]{2,1,0:T(8,128)(2,1)} %slice_dynamic-update-slice_fusion.5, s32[]{:T(128)S(6)} %select_n.149, bf16[64,64,256]{2,1,0:T(8,128)(2,1)S(1)} %bitcast_convert_fusion.2), kind=kLoop, calls=%fused_computation.15 | loop fusion | bytes 2097156 | tf_op jit(solution)/shard_map/dynamic_update_slice | solution.py:131
  59.5 1.6 %collective-permute-start.15 = (bf16[8,64,256]{2,1,0:T(8,128)(2,1)S(1)}, bf16[8,64,256]{2,1,0:T(8,128)(2,1)S(1)}, u32[]{:S(2)}, u32[]{:S(2)}) collective-permute-start(bf16[8,64,256]{2,1,0:T(8,128)(2,1)S(1)} %collective-permute-done.11), channel_id=1, source_target_pairs={{0,2},{1,3},{2,6},{3,7},{4,0},{5,1},{6,10},{7,11},{8,4},{9,5},{10,... | collective-permute-start | bytes 786440 | tf_op jit(solution)/shard_map/ppermute | solution.py:144
  61.1 0.5 collective-permute-start.13
  61.7 4.8 %bitcast_convert_fusion.1 = bf16[64,64,256]{2,1,0:T(8,128)(2,1)S(1)} fusion(bf16[8,64,256]{2,1,0:T(8,128)(2,1)S(1)} %get-tuple-element.18, bf16[8,64,256]{2,1,0:T(8,128)(2,1)S(1)} %get-tuple-element.17, bf16[8,64,256]{2,1,0:T(8,128)(2,1)S(1)} %get-tuple-element.16, bf16[8,64,256]{2,1,0:T(8,128)(2,1)S(1)} %get-tuple-element.15, ...), kind=kOutput, calls=%fused_computation.4 | convolution fusion | flops 4333764608 | bytes 19922944 | tf_op jit(solution)/shard_map/wilk,wjk->ilj/dot_general | solution.py:126
  66.5 1.3 %collective-permute-done.15 = bf16[8,64,256]{2,1,0:T(8,128)(2,1)S(1)} collective-permute-done((bf16[8,64,256]{2,1,0:T(8,128)(2,1)S(1)}, bf16[8,64,256]{2,1,0:T(8,128)(2,1)S(1)}, u32[]{:S(2)}, u32[]{:S(2)}) %collective-permute-start.15) | collective-permute-done | bytes 262176 | tf_op jit(solution)/shard_map/ppermute | solution.py:144
  67.8 1.2 %slice_dynamic-update-slice_fusion.3 = bf16[64,64,1024]{2,1,0:T(8,128)(2,1)} fusion(bf16[64,64,1024]{2,1,0:T(8,128)(2,1)} %slice_dynamic-update-slice_fusion.4, s32[]{:T(128)S(6)} %select_n.154, bf16[64,64,256]{2,1,0:T(8,128)(2,1)S(1)} %bitcast_convert_fusion.1), kind=kLoop, calls=%fused_computation.14 | loop fusion | bytes 2097156 | tf_op jit(solution)/shard_map/dynamic_update_slice | solution.py:131
  69.1 0.4 collective-permute-start.14
  69.5 1.2 %slice_dynamic-update-slice_fusion.2 = bf16[64,64,1024]{2,1,0:T(8,128)(2,1)} fusion(bf16[64,64,1024]{2,1,0:T(8,128)(2,1)} %slice_dynamic-update-slice_fusion.3, s32[]{:T(128)S(6)} %select_n.155, bf16[64,64,256]{2,1,0:T(8,128)(2,1)S(1)} %bitcast_convert_fusion.1), kind=kLoop, calls=%fused_computation.13 | loop fusion | bytes 2097156 | tf_op jit(solution)/shard_map/dynamic_update_slice | solution.py:131
  70.7 0.5 collective-permute-start.17
  71.3 4.8 %bitcast_convert_fusion = bf16[64,64,256]{2,1,0:T(8,128)(2,1)S(1)} fusion(bf16[8,64,256]{2,1,0:T(8,128)(2,1)S(1)} %get-tuple-element.14, bf16[8,64,256]{2,1,0:T(8,128)(2,1)S(1)} %get-tuple-element.13, bf16[8,64,256]{2,1,0:T(8,128)(2,1)S(1)} %get-tuple-element.12, bf16[8,64,256]{2,1,0:T(8,128)(2,1)S(1)} %get-tuple-element.11, ...), kind=kOutput, calls=%fused_computation.3 | convolution fusion | flops 4333764608 | bytes 19922944 | tf_op jit(solution)/shard_map/wilk,wjk->ilj/dot_general | solution.py:126
  76.1 1.2 %slice_dynamic-update-slice_fusion.1 = bf16[64,64,1024]{2,1,0:T(8,128)(2,1)} fusion(bf16[64,64,1024]{2,1,0:T(8,128)(2,1)} %slice_dynamic-update-slice_fusion.2, s32[]{:T(128)S(6)} %select_n.160, bf16[64,64,256]{2,1,0:T(8,128)(2,1)S(1)} %bitcast_convert_fusion), kind=kLoop, calls=%fused_computation.12 | loop fusion | bytes 2097156 | tf_op jit(solution)/shard_map/dynamic_update_slice | solution.py:131
  77.3 1.7 %collective-permute-done.17 = bf16[8,64,256]{2,1,0:T(8,128)(2,1)S(1)} collective-permute-done((bf16[8,64,256]{2,1,0:T(8,128)(2,1)S(1)}, bf16[8,64,256]{2,1,0:T(8,128)(2,1)S(1)}, u32[]{:S(2)}, u32[]{:S(2)}) %collective-permute-start.17) | collective-permute-done | bytes 262176 | tf_op jit(solution)/shard_map/ppermute | solution.py:143
  79.0 1.2 %slice_dynamic-update-slice_fusion = bf16[64,64,1024]{2,1,0:T(8,128)(2,1)} fusion(bf16[64,64,1024]{2,1,0:T(8,128)(2,1)} %slice_dynamic-update-slice_fusion.1, s32[]{:T(128)S(6)} %select_n.161, bf16[64,64,256]{2,1,0:T(8,128)(2,1)S(1)} %bitcast_convert_fusion), kind=kLoop, calls=%fused_computation.11 | loop fusion | bytes 2097156 | tf_op jit(solution)/shard_map/dynamic_update_slice | solution.py:131
  80.2 0.4 collective-permute-done.18
  80.6 5.6 %fusion.1 = bf16[64,64,1024]{2,1,0:T(8,128)(2,1)} fusion(bf16[64,64,1024]{2,1,0:T(8,128)(2,1)} %slice_dynamic-update-slice_fusion, s32[]{:T(128)S(6)} %select_n.164, bf16[8,64,256]{2,1,0:T(8,128)(2,1)S(1)} %get-tuple-element.10, bf16[8,64,256]{2,1,0:T(8,128)(2,1)S(1)} %get-tuple-element.9, bf16[8,64,64,128]{3,2,0,1:T(8,128)(2,1)S(1)} %get-tuple-element.6, ...), kind=kOutput, calls=%fused_computation.9 | convolution fusion | flops 2182610944 | bytes 18350084 | tf_op jit(solution)/shard_map/wilk,wjk->ilj/dot_general | solution.py:126
  (41 shorter events, 1.7 us)
Async XLA Ops:
  3.6 5.8 %collective-permute-start = (f32[1153]{0:T(1024)S(1)}, f32[1153]{0:T(1024)S(1)}, u32[]{:S(2)}, u32[]{:S(2)}) collective-permute-start(f32[1153]{0:T(1024)S(1)} %pad_maximum_fusion.2), channel_id=1, source_target_pairs={{0,8},{1,9},{2,10},{3,11},{4,12},{5,13},{6,14},{7,15},{8,0},{9,1},... | collective-permute-start | bytes 13844 | tf_op jit(solution)/shard_map/ppermute | solution.py:27
  10.1 3.7 %collective-permute-start.1 = (f32[1153]{0:T(1024)S(1)}, f32[1153]{0:T(1024)S(1)}, u32[]{:S(2)}, u32[]{:S(2)}) collective-permute-start(f32[1153]{0:T(1024)S(1)} %fusion.50), channel_id=1, source_target_pairs={{0,4},{1,5},{2,6},{3,7},{4,0},{5,1},{6,2},{7,3},{8,12},{9,13},{10,... | collective-permute-start | bytes 13844 | tf_op jit(solution)/shard_map/ppermute | solution.py:27
  13.8 3.7 %collective-permute-start.2 = (f32[1153]{0:T(1024)S(1)}, f32[1153]{0:T(1024)S(1)}, u32[]{:S(2)}, u32[]{:S(2)}) collective-permute-start(f32[1153]{0:T(1024)S(1)} %add.120), channel_id=1, source_target_pairs={{0,2},{1,3},{2,0},{3,1},{4,6},{5,7},{6,4},{7,5},{8,10},{9,11},{10,... | collective-permute-start | bytes 13844 | tf_op jit(solution)/shard_map/ppermute | solution.py:27
  17.4 1.2 %collective-permute-start.3 = (f32[1153]{0:T(1024)S(1)}, f32[1153]{0:T(1024)S(1)}, u32[]{:S(2)}, u32[]{:S(2)}) collective-permute-start(f32[1153]{0:T(1024)S(1)} %add.121), channel_id=1, source_target_pairs={{0,1},{1,0},{2,3},{3,2},{4,5},{5,4},{6,7},{7,6},{8,9},{9,8},{10,11... | collective-permute-start | bytes 13844 | tf_op jit(solution)/shard_map/ppermute | solution.py:27
  22.2 7.6 %collective-permute-start.4 = (bf16[8,64,256]{2,1,0:T(8,128)(2,1)S(1)}, bf16[8,64,256]{2,1,0:T(8,128)(2,1)S(1)}, u32[]{:S(2)}, u32[]{:S(2)}) collective-permute-start(bf16[8,64,256]{2,1,0:T(8,128)(2,1)S(1)} %pad_maximum_fusion.1), channel_id=1, source_target_pairs={{0,1},{1,0},{2,3},{3,2},{4,5},{5,4},{6,7},{7,6},{8,9},{9,8},{10,11... | collective-permute-start | bytes 786440 | tf_op jit(solution)/shard_map/ppermute | solution.py:134
  27.7 8.8 %collective-permute-start.7 = (bf16[8,64,256]{2,1,0:T(8,128)(2,1)S(1)}, bf16[8,64,256]{2,1,0:T(8,128)(2,1)S(1)}, u32[]{:S(2)}, u32[]{:S(2)}) collective-permute-start(bf16[8,64,256]{2,1,0:T(8,128)(2,1)S(1)} %pad_maximum_fusion.1), channel_id=1, source_target_pairs={{0,2},{1,3},{2,6},{3,7},{4,0},{5,1},{6,10},{7,11},{8,4},{9,5},{10,... | collective-permute-start | bytes 786440 | tf_op jit(solution)/shard_map/ppermute | solution.py:136
  29.6 8.3 %collective-permute-start.5 = (bf16[8,64,256]{2,1,0:T(8,128)(2,1)S(1)}, bf16[8,64,256]{2,1,0:T(8,128)(2,1)S(1)}, u32[]{:S(2)}, u32[]{:S(2)}) collective-permute-start(bf16[8,64,256]{2,1,0:T(8,128)(2,1)S(1)} %pad_maximum_fusion.1), channel_id=1, source_target_pairs={{0,4},{1,5},{2,0},{3,1},{4,8},{5,9},{6,2},{7,3},{8,12},{9,13},{10,... | collective-permute-start | bytes 786440 | tf_op jit(solution)/shard_map/ppermute | solution.py:135
  36.5 13.5 %collective-permute-start.8 = (bf16[8,64,256]{2,1,0:T(8,128)(2,1)S(1)}, bf16[8,64,256]{2,1,0:T(8,128)(2,1)S(1)}, u32[]{:S(2)}, u32[]{:S(2)}) collective-permute-start(bf16[8,64,256]{2,1,0:T(8,128)(2,1)S(1)} %collective-permute-done.7), channel_id=1, source_target_pairs={{0,1},{1,0},{2,3},{3,2},{4,5},{5,4},{6,7},{7,6},{8,9},{9,8},{10,11... | collective-permute-start | bytes 786440 | tf_op jit(solution)/shard_map/ppermute | solution.py:142
  37.9 12.1 %collective-permute-start.6 = (bf16[8,64,256]{2,1,0:T(8,128)(2,1)S(1)}, bf16[8,64,256]{2,1,0:T(8,128)(2,1)S(1)}, u32[]{:S(2)}, u32[]{:S(2)}) collective-permute-start(bf16[8,64,256]{2,1,0:T(8,128)(2,1)S(1)} %collective-permute-done.5), channel_id=1, source_target_pairs={{0,1},{1,0},{2,3},{3,2},{4,5},{5,4},{6,7},{7,6},{8,9},{9,8},{10,11... | collective-permute-start | bytes 786440 | tf_op jit(solution)/shard_map/ppermute | solution.py:139
  47.9 8.7 %collective-permute-start.11 = (bf16[8,64,256]{2,1,0:T(8,128)(2,1)S(1)}, bf16[8,64,256]{2,1,0:T(8,128)(2,1)S(1)}, u32[]{:S(2)}, u32[]{:S(2)}) collective-permute-start(bf16[8,64,256]{2,1,0:T(8,128)(2,1)S(1)} %collective-permute-done.7), channel_id=1, source_target_pairs={{0,2},{1,3},{2,6},{3,7},{4,0},{5,1},{6,10},{7,11},{8,4},{9,5},{10,... | collective-permute-start | bytes 786440 | tf_op jit(solution)/shard_map/ppermute | solution.py:144
  49.5 8.4 %collective-permute-start.9 = (bf16[8,64,256]{2,1,0:T(8,128)(2,1)S(1)}, bf16[8,64,256]{2,1,0:T(8,128)(2,1)S(1)}, u32[]{:S(2)}, u32[]{:S(2)}) collective-permute-start(bf16[8,64,256]{2,1,0:T(8,128)(2,1)S(1)} %collective-permute-done.5), channel_id=1, source_target_pairs={{0,4},{1,5},{2,0},{3,1},{4,8},{5,9},{6,2},{7,3},{8,12},{9,13},{10,... | collective-permute-start | bytes 786440 | tf_op jit(solution)/shard_map/ppermute | solution.py:143
  56.6 4.9 %collective-permute-start.12 = (bf16[8,64,256]{2,1,0:T(8,128)(2,1)S(1)}, bf16[8,64,256]{2,1,0:T(8,128)(2,1)S(1)}, u32[]{:S(2)}, u32[]{:S(2)}) collective-permute-start(bf16[8,64,256]{2,1,0:T(8,128)(2,1)S(1)} %collective-permute-done.11), channel_id=1, source_target_pairs={{0,1},{1,0},{2,3},{3,2},{4,5},{5,4},{6,7},{7,6},{8,9},{9,8},{10,11... | collective-permute-start | bytes 786440 | tf_op jit(solution)/shard_map/ppermute | solution.py:142
  57.9 3.7 %collective-permute-start.10 = (bf16[8,64,256]{2,1,0:T(8,128)(2,1)S(1)}, bf16[8,64,256]{2,1,0:T(8,128)(2,1)S(1)}, u32[]{:S(2)}, u32[]{:S(2)}) collective-permute-start(bf16[8,64,256]{2,1,0:T(8,128)(2,1)S(1)} %collective-permute-done.9), channel_id=1, source_target_pairs={{0,1},{1,0},{2,3},{3,2},{4,5},{5,4},{6,7},{7,6},{8,9},{9,8},{10,11... | collective-permute-start | bytes 786440 | tf_op jit(solution)/shard_map/ppermute | solution.py:139
  59.5 8.3 %collective-permute-start.15 = (bf16[8,64,256]{2,1,0:T(8,128)(2,1)S(1)}, bf16[8,64,256]{2,1,0:T(8,128)(2,1)S(1)}, u32[]{:S(2)}, u32[]{:S(2)}) collective-permute-start(bf16[8,64,256]{2,1,0:T(8,128)(2,1)S(1)} %collective-permute-done.11), channel_id=1, source_target_pairs={{0,2},{1,3},{2,6},{3,7},{4,0},{5,1},{6,10},{7,11},{8,4},{9,5},{10,... | collective-permute-start | bytes 786440 | tf_op jit(solution)/shard_map/ppermute | solution.py:144
  61.1 8.0 %collective-permute-start.13 = (bf16[8,64,256]{2,1,0:T(8,128)(2,1)S(1)}, bf16[8,64,256]{2,1,0:T(8,128)(2,1)S(1)}, u32[]{:S(2)}, u32[]{:S(2)}) collective-permute-start(bf16[8,64,256]{2,1,0:T(8,128)(2,1)S(1)} %collective-permute-done.9), channel_id=1, source_target_pairs={{0,4},{1,5},{2,0},{3,1},{4,8},{5,9},{6,2},{7,3},{8,12},{9,13},{10,... | collective-permute-start | bytes 786440 | tf_op jit(solution)/shard_map/ppermute | solution.py:143
  67.8 3.3 %collective-permute-start.16 = (bf16[8,64,256]{2,1,0:T(8,128)(2,1)S(1)}, bf16[8,64,256]{2,1,0:T(8,128)(2,1)S(1)}, u32[]{:S(2)}, u32[]{:S(2)}) collective-permute-start(bf16[8,64,256]{2,1,0:T(8,128)(2,1)S(1)} %collective-permute-done.15), channel_id=1, source_target_pairs={{0,1},{1,0},{2,3},{3,2},{4,5},{5,4},{6,7},{7,6},{8,9},{9,8},{10,11... | collective-permute-start | bytes 786440 | tf_op jit(solution)/shard_map/ppermute | solution.py:142
  69.1 2.1 %collective-permute-start.14 = (bf16[8,64,256]{2,1,0:T(8,128)(2,1)S(1)}, bf16[8,64,256]{2,1,0:T(8,128)(2,1)S(1)}, u32[]{:S(2)}, u32[]{:S(2)}) collective-permute-start(bf16[8,64,256]{2,1,0:T(8,128)(2,1)S(1)} %collective-permute-done.13), channel_id=1, source_target_pairs={{0,1},{1,0},{2,3},{3,2},{4,5},{5,4},{6,7},{7,6},{8,9},{9,8},{10,11... | collective-permute-start | bytes 786440 | tf_op jit(solution)/shard_map/ppermute | solution.py:139
  70.7 8.3 %collective-permute-start.17 = (bf16[8,64,256]{2,1,0:T(8,128)(2,1)S(1)}, bf16[8,64,256]{2,1,0:T(8,128)(2,1)S(1)}, u32[]{:S(2)}, u32[]{:S(2)}) collective-permute-start(bf16[8,64,256]{2,1,0:T(8,128)(2,1)S(1)} %collective-permute-done.13), channel_id=1, source_target_pairs={{0,4},{1,5},{2,0},{3,1},{4,8},{5,9},{6,2},{7,3},{8,12},{9,13},{10,... | collective-permute-start | bytes 786440 | tf_op jit(solution)/shard_map/ppermute | solution.py:143
  79.0 1.5 %collective-permute-start.18 = (bf16[8,64,256]{2,1,0:T(8,128)(2,1)S(1)}, bf16[8,64,256]{2,1,0:T(8,128)(2,1)S(1)}, u32[]{:S(2)}, u32[]{:S(2)}) collective-permute-start(bf16[8,64,256]{2,1,0:T(8,128)(2,1)S(1)} %collective-permute-done.17), channel_id=1, source_target_pairs={{0,1},{1,0},{2,3},{3,2},{4,5},{5,4},{6,7},{7,6},{8,9},{9,8},{10,11... | collective-permute-start | bytes 786440 | tf_op jit(solution)/shard_map/ppermute | solution.py:139

commit v5 on v4

--- a/solution.py
+++ b/solution.py
@@ -93,6 +93,13 @@
     return size, chips, cycle, position
 
 
+def pick(values, index):
+    chosen = jnp.int32(values[0])
+    for n in range(1, len(values)):
+        chosen = jnp.where(index == n, jnp.int32(values[n]), chosen)
+    return chosen
+
+
 def correlate(whitened, rotated, plan):
     size, chips, cycle, position = plan
     here = whitened.shape[1]
@@ -117,8 +124,8 @@
         return jnp.concatenate([first, second], axis=1)
 
     shifts = [0] + [s for h in range(1, forward_hops + 1) for s in ((-h, h) if h <= backward_hops else (-h,))]
-    table = jnp.asarray([[shifted(k, s) for s in shifts] for k in range(chips)], jnp.int32)
-    placed_chips = table[my_chip]
+    my_position = pick([position[k] for k in range(chips)], my_chip)
+    placed_chips = [pick([cycle[(p + s) % chips] for p in range(chips)], my_position) for s in shifts]
     slot = {s: n for n, s in enumerate(shifts)}
 
     def emit(result, pieces):

time: 86.5 us -> 81.2 us (0.939)
  between operations: 6.02 us -> 0.92 us
  local copies, waits for them, and re-layouts: 14 us -> 12.6 us
  waiting for transfers between devices: 12.8 us -> 14.2 us
    ppermute x4, waiting for transfers between devices: 4.37 us -> 5.76 us  [butterfly_sum(): value = value + lax.ppermute(value, axis, pairs)]
  transfers between devices with their start and end apart: 19 -> 19, of which waited for: 12 -> 12; matrix products, arithmetic and copies ran while one was open for 45% -> 46% of each run, Pallas kernels for 0% -> 0%
where the time goes in v5:
time: 81.2 us; the launch traced here: 81 us
  matrix products  26.3 us (32%)
  starting transfers between devices  15.6 us (19%)
  waiting for transfers between devices  14.2 us (17%)
  local copies, waits for them, and re-layouts  12.6 us (16%)
  other arithmetic  11.4 us (14%)
  between operations  0.92 us (1%)
    dot_general x5, matrix products, emit(): jnp.einsum('wilk,wjk->ilj', rotated, rhs, preferred_element_type=jnp.floa...  25.7 us
    ppermute x4, starting transfers between devices, butterfly_sum(): value = value + lax.ppermute(value, axis, pairs)  7.95 us
    dynamic_update_slice x6, local copies, waits for them, and re-layouts, emit(): result = lax.dynamic_update_slice(result, piece, (0, 0, chip * 2 * here))  7.05 us
    ppermute x4, waiting for transfers between devices, butterfly_sum(): value = value + lax.ppermute(value, axis, pairs)  5.76 us
    another operation x2, other arithmetic  4.59 us
    broadcast_in_dim x1, local copies, waits for them, and re-layouts, correlate(): jnp.zeros((rotated.shape[1], rotated.shape[2], size * here), jnp.bfloat16)  4.47 us
    ppermute x2, starting transfers between devices, correlate(): lax.ppermute(behind, 'chan', backward)  3.15 us
    ppermute x2, waiting for transfers between devices, correlate(): lax.ppermute(behind, 'chan', backward)  3.03 us
  transfers between devices with their start and end apart: 19, of which 12 were waited for; matrix products, arithmetic and copies ran while one was open for 46% of the time, Pallas kernels for 0%

profile of v5, /device:TPU:0, one launch (start us, length us, event | category | flops | bytes accessed | tf_op | source)
XLA Modules:
  0.0 81.0 jit_solution(15757191259346152137)
XLA Ops:
  0.0 1.3 %convert_reduce_fusion = f32[]{:T(128)} fusion(s32[64]{0:T(128)} %param.3), kind=kLoop, calls=%fused_computation.107 | loop fusion | flops 127 | bytes 260 | tf_op jit(solution)/shard_map/reduce_sum | solution.py:53
  1.3 0.7 convert_element_type.60
  1.9 1.1 %multiply_reduce_fusion = f32[1152]{0:T(1024)S(1)} fusion(f32[64,1152]{1,0:T(8,128)} %param.2, f32[64]{0:T(128)S(1)} %convert_element_type.60), kind=kLoop, calls=%fused_computation.48 | loop fusion | flops 146304 | bytes 299776 | tf_op jit(solution)/shard_map/reduce_sum | solution.py:53
  3.0 0.7 pad_maximum_fusion.2
  3.6 4.1 %collective-permute-start = (f32[1153]{0:T(1024)S(1)}, f32[1153]{0:T(1024)S(1)}, u32[]{:S(2)}, u32[]{:S(2)}) collective-permute-start(f32[1153]{0:T(1024)S(1)} %pad_maximum_fusion.2), channel_id=1, source_target_pairs={{0,8},{1,9},{2,10},{3,11},{4,12},{5,13},{6,14},{7,15},{8,0},{9,1},... | collective-permute-start | bytes 13844 | tf_op jit(solution)/shard_map/ppermute | solution.py:27
  7.8 1.6 %collective-permute-done = f32[1153]{0:T(1024)S(1)} collective-permute-done((f32[1153]{0:T(1024)S(1)}, f32[1153]{0:T(1024)S(1)}, u32[]{:S(2)}, u32[]{:S(2)}) %collective-permute-start) | collective-permute-done | bytes 4644 | tf_op jit(solution)/shard_map/ppermute | solution.py:27
  9.4 0.7 fusion.49
  10.1 2.0 %collective-permute-start.1 = (f32[1153]{0:T(1024)S(1)}, f32[1153]{0:T(1024)S(1)}, u32[]{:S(2)}, u32[]{:S(2)}) collective-permute-start(f32[1153]{0:T(1024)S(1)} %fusion.49), channel_id=1, source_target_pairs={{0,4},{1,5},{2,6},{3,7},{4,0},{5,1},{6,2},{7,3},{8,12},{9,13},{10,... | collective-permute-start | bytes 13844 | tf_op jit(solution)/shard_map/ppermute | solution.py:27
  12.1 1.7 %collective-permute-done.1 = f32[1153]{0:T(1024)S(1)} collective-permute-done((f32[1153]{0:T(1024)S(1)}, f32[1153]{0:T(1024)S(1)}, u32[]{:S(2)}, u32[]{:S(2)}) %collective-permute-start.1) | collective-permute-done | bytes 4644 | tf_op jit(solution)/shard_map/ppermute | solution.py:27
  13.8 1.8 %collective-permute-start.2 = (f32[1153]{0:T(1024)S(1)}, f32[1153]{0:T(1024)S(1)}, u32[]{:S(2)}, u32[]{:S(2)}) collective-permute-start(f32[1153]{0:T(1024)S(1)} %add.117), channel_id=1, source_target_pairs={{0,2},{1,3},{2,0},{3,1},{4,6},{5,7},{6,4},{7,5},{8,10},{9,11},{10,... | collective-permute-start | bytes 13844 | tf_op jit(solution)/shard_map/ppermute | solution.py:27
  15.6 1.8 %collective-permute-done.2 = f32[1153]{0:T(1024)S(1)} collective-permute-done((f32[1153]{0:T(1024)S(1)}, f32[1153]{0:T(1024)S(1)}, u32[]{:S(2)}, u32[]{:S(2)}) %collective-permute-start.2) | collective-permute-done | bytes 4644 | tf_op jit(solution)/shard_map/ppermute | solution.py:27
  17.4 0.5 cosine_multiply_fusion
  18.0 0.6 collective-permute-done.3
  18.6 0.5 slice.57
  19.8 1.1 %subtract_multiply_fusion = f32[64,1152]{1,0:T(8,128)S(1)} fusion(f32[64,1152]{1,0:T(8,128)} %param.2, f32[1152]{0:T(1024)S(1)} %slice_divide_fusion, f32[64]{0:T(128)S(1)} %convert_element_type.60), kind=kLoop, calls=%fused_computation.47 | loop fusion | flops 147456 | bytes 594688 | tf_op jit(solution)/shard_map/mul | solution.py:57
  21.1 0.6 convolution_bitcast_fusion
  22.1 0.2 collective-permute-start.4
  22.3 0.2 cosine_multiply_fusion.1
  22.5 1.9 %collective-permute-start.7 = (bf16[8,64,256]{2,1,0:T(8,128)(2,1)S(1)}, bf16[8,64,256]{2,1,0:T(8,128)(2,1)S(1)}, u32[]{:S(2)}, u32[]{:S(2)}) collective-permute-start(bf16[8,64,256]{2,1,0:T(8,128)(2,1)S(1)} %pad_maximum_fusion.1), channel_id=1, source_target_pairs={{0,2},{1,3},{2,6},{3,7},{4,0},{5,1},{6,10},{7,11},{8,4},{9,5},{10,... | collective-permute-start | bytes 786440 | tf_op jit(solution)/shard_map/ppermute | solution.py:143
  24.4 0.2 collective-permute-start.5
  24.8 0.2 copy.8
  25.0 0.2 copy.7
  25.1 4.4 %subtract_convert_fusion = (bf16[8,64,64,128]{3,2,0,1:T(8,128)(2,1)S(1)}, bf16[8,64,64,128]{3,2,0,1:T(8,128)(2,1)S(1)}) fusion(f32[64,128]{1,0:T(8,128)S(1)} %get-tuple-element.31, f32[8,64,128]{2,0,1:T(8,128)S(1)} %copy.8, f32[64,128]{1,0:T(8,128)S(1)} %get-tuple-element.30, f32[8,64,128]{2,0,1:T(8,128)S(1)} %copy.7), kind=kLoop, calls=%fused_computation.2 | loop fusion | flops 33554432 | bytes 17367040 | tf_op jit(solution)/shard_map/convert
  29.6 1.7 %collective-permute-done.7 = bf16[8,64,256]{2,1,0:T(8,128)(2,1)S(1)} collective-permute-done((bf16[8,64,256]{2,1,0:T(8,128)(2,1)S(1)}, bf16[8,64,256]{2,1,0:T(8,128)(2,1)S(1)}, u32[]{:S(2)}, u32[]{:S(2)}) %collective-permute-start.7) | collective-permute-done | bytes 262176 | tf_op jit(solution)/shard_map/ppermute | solution.py:143
  31.3 1.4 %collective-permute-done.5 = bf16[8,64,256]{2,1,0:T(8,128)(2,1)S(1)} collective-permute-done((bf16[8,64,256]{2,1,0:T(8,128)(2,1)S(1)}, bf16[8,64,256]{2,1,0:T(8,128)(2,1)S(1)}, u32[]{:S(2)}, u32[]{:S(2)}) %collective-permute-start.5) | collective-permute-done | bytes 262176 | tf_op jit(solution)/shard_map/ppermute | solution.py:142
  32.7 4.5 %broadcast_in_dim.4 = bf16[64,64,1024]{2,1,0:T(8,128)(2,1)} broadcast(bf16[]{:T(256)} %constant.86.clone.1), dimensions={} | broadcast | bytes 8388610 | tf_op jit(solution)/shard_map/broadcast_in_dim | solution.py:119
  37.2 5.6 %fusion = bf16[64,64,1024]{2,1,0:T(8,128)(2,1)} fusion(bf16[64,64,1024]{2,1,0:T(8,128)(2,1)} %broadcast_in_dim.4, s32[]{:T(128)S(6)} %select_n.342, bf16[8,64,256]{2,1,0:T(8,128)(2,1)S(1)} %get-tuple-element.26, bf16[8,64,256]{2,1,0:T(8,128)(2,1)S(1)} %get-tuple-element.25, bf16[8,64,64,128]{3,2,0,1:T(8,128)(2,1)S(1)} %get-tuple-element.6, ...), kind=kOutput, calls=%fused_computation.8 | convolution fusion | flops 2182610944 | bytes 18350084 | tf_op jit(solution)/shard_map/wilk,wjk->ilj/dot_general | solution.py:133
  42.7 1.6 %collective-permute-start.11 = (bf16[8,64,256]{2,1,0:T(8,128)(2,1)S(1)}, bf16[8,64,256]{2,1,0:T(8,128)(2,1)S(1)}, u32[]{:S(2)}, u32[]{:S(2)}) collective-permute-start(bf16[8,64,256]{2,1,0:T(8,128)(2,1)S(1)} %collective-permute-done.7), channel_id=1, source_target_pairs={{0,2},{1,3},{2,6},{3,7},{4,0},{5,1},{6,10},{7,11},{8,4},{9,5},{10,... | collective-permute-start | bytes 786440 | tf_op jit(solution)/shard_map/ppermute | solution.py:151
  44.3 0.4 collective-permute-start.9
  44.9 4.8 %bitcast_convert_fusion.2 = bf16[64,64,256]{2,1,0:T(8,128)(2,1)S(1)} fusion(bf16[8,64,256]{2,1,0:T(8,128)(2,1)S(1)} %get-tuple-element.22, bf16[8,64,256]{2,1,0:T(8,128)(2,1)S(1)} %get-tuple-element.21, bf16[8,64,256]{2,1,0:T(8,128)(2,1)S(1)} %get-tuple-element.20, bf16[8,64,256]{2,1,0:T(8,128)(2,1)S(1)} %get-tuple-element.19, ...), kind=kOutput, calls=%fused_computation.5 | convolution fusion | flops 4333764608 | bytes 19922944 | tf_op jit(solution)/shard_map/wilk,wjk->ilj/dot_general | solution.py:133
  49.7 1.7 %collective-permute-done.11 = bf16[8,64,256]{2,1,0:T(8,128)(2,1)S(1)} collective-permute-done((bf16[8,64,256]{2,1,0:T(8,128)(2,1)S(1)}, bf16[8,64,256]{2,1,0:T(8,128)(2,1)S(1)}, u32[]{:S(2)}, u32[]{:S(2)}) %collective-permute-start.11) | collective-permute-done | bytes 262176 | tf_op jit(solution)/shard_map/ppermute | solution.py:151
  51.5 1.2 %slice_dynamic-update-slice_fusion.5 = bf16[64,64,1024]{2,1,0:T(8,128)(2,1)} fusion(bf16[64,64,1024]{2,1,0:T(8,128)(2,1)} %fusion, s32[]{:T(128)S(6)} %select_n.354, bf16[64,64,256]{2,1,0:T(8,128)(2,1)S(1)} %bitcast_convert_fusion.2), kind=kLoop, calls=%fused_computation.16 | loop fusion | bytes 2097156 | tf_op jit(solution)/shard_map/dynamic_update_slice | solution.py:138
  52.7 0.4 collective-permute-start.10
  53.1 1.2 %slice_dynamic-update-slice_fusion.4 = bf16[64,64,1024]{2,1,0:T(8,128)(2,1)} fusion(bf16[64,64,1024]{2,1,0:T(8,128)(2,1)} %slice_dynamic-update-slice_fusion.5, s32[]{:T(128)S(6)} %select_n.362, bf16[64,64,256]{2,1,0:T(8,128)(2,1)S(1)} %bitcast_convert_fusion.2), kind=kLoop, calls=%fused_computation.15 | loop fusion | bytes 2097156 | tf_op jit(solution)/shard_map/dynamic_update_slice | solution.py:138
  54.3 1.6 %collective-permute-start.15 = (bf16[8,64,256]{2,1,0:T(8,128)(2,1)S(1)}, bf16[8,64,256]{2,1,0:T(8,128)(2,1)S(1)}, u32[]{:S(2)}, u32[]{:S(2)}) collective-permute-start(bf16[8,64,256]{2,1,0:T(8,128)(2,1)S(1)} %collective-permute-done.11), channel_id=1, source_target_pairs={{0,2},{1,3},{2,6},{3,7},{4,0},{5,1},{6,10},{7,11},{8,4},{9,5},{10,... | collective-permute-start | bytes 786440 | tf_op jit(solution)/shard_map/ppermute | solution.py:151
  55.9 0.5 collective-permute-start.13
  56.5 4.8 %bitcast_convert_fusion.1 = bf16[64,64,256]{2,1,0:T(8,128)(2,1)S(1)} fusion(bf16[8,64,256]{2,1,0:T(8,128)(2,1)S(1)} %get-tuple-element.18, bf16[8,64,256]{2,1,0:T(8,128)(2,1)S(1)} %get-tuple-element.17, bf16[8,64,256]{2,1,0:T(8,128)(2,1)S(1)} %get-tuple-element.16, bf16[8,64,256]{2,1,0:T(8,128)(2,1)S(1)} %get-tuple-element.15, ...), kind=kOutput, calls=%fused_computation.4 | convolution fusion | flops 4333764608 | bytes 19922944 | tf_op jit(solution)/shard_map/wilk,wjk->ilj/dot_general | solution.py:133
  61.3 1.3 %collective-permute-done.15 = bf16[8,64,256]{2,1,0:T(8,128)(2,1)S(1)} collective-permute-done((bf16[8,64,256]{2,1,0:T(8,128)(2,1)S(1)}, bf16[8,64,256]{2,1,0:T(8,128)(2,1)S(1)}, u32[]{:S(2)}, u32[]{:S(2)}) %collective-permute-start.15) | collective-permute-done | bytes 262176 | tf_op jit(solution)/shard_map/ppermute | solution.py:151
  62.6 1.2 %slice_dynamic-update-slice_fusion.3 = bf16[64,64,1024]{2,1,0:T(8,128)(2,1)} fusion(bf16[64,64,1024]{2,1,0:T(8,128)(2,1)} %slice_dynamic-update-slice_fusion.4, s32[]{:T(128)S(6)} %select_n.374, bf16[64,64,256]{2,1,0:T(8,128)(2,1)S(1)} %bitcast_convert_fusion.1), kind=kLoop, calls=%fused_computation.14 | loop fusion | bytes 2097156 | tf_op jit(solution)/shard_map/dynamic_update_slice | solution.py:138
  63.9 0.4 collective-permute-start.14
  64.3 1.2 %slice_dynamic-update-slice_fusion.2 = bf16[64,64,1024]{2,1,0:T(8,128)(2,1)} fusion(bf16[64,64,1024]{2,1,0:T(8,128)(2,1)} %slice_dynamic-update-slice_fusion.3, s32[]{:T(128)S(6)} %select_n.382, bf16[64,64,256]{2,1,0:T(8,128)(2,1)S(1)} %bitcast_convert_fusion.1), kind=kLoop, calls=%fused_computation.13 | loop fusion | bytes 2097156 | tf_op jit(solution)/shard_map/dynamic_update_slice | solution.py:138
  65.5 0.5 collective-permute-start.17
  66.1 4.8 %bitcast_convert_fusion = bf16[64,64,256]{2,1,0:T(8,128)(2,1)S(1)} fusion(bf16[8,64,256]{2,1,0:T(8,128)(2,1)S(1)} %get-tuple-element.14, bf16[8,64,256]{2,1,0:T(8,128)(2,1)S(1)} %get-tuple-element.13, bf16[8,64,256]{2,1,0:T(8,128)(2,1)S(1)} %get-tuple-element.12, bf16[8,64,256]{2,1,0:T(8,128)(2,1)S(1)} %get-tuple-element.11, ...), kind=kOutput, calls=%fused_computation.3 | convolution fusion | flops 4333764608 | bytes 19922944 | tf_op jit(solution)/shard_map/wilk,wjk->ilj/dot_general | solution.py:133
  70.9 1.2 %slice_dynamic-update-slice_fusion.1 = bf16[64,64,1024]{2,1,0:T(8,128)(2,1)} fusion(bf16[64,64,1024]{2,1,0:T(8,128)(2,1)} %slice_dynamic-update-slice_fusion.2, s32[]{:T(128)S(6)} %select_n.394, bf16[64,64,256]{2,1,0:T(8,128)(2,1)S(1)} %bitcast_convert_fusion), kind=kLoop, calls=%fused_computation.12 | loop fusion | bytes 2097156 | tf_op jit(solution)/shard_map/dynamic_update_slice | solution.py:138
  72.1 1.7 %collective-permute-done.17 = bf16[8,64,256]{2,1,0:T(8,128)(2,1)S(1)} collective-permute-done((bf16[8,64,256]{2,1,0:T(8,128)(2,1)S(1)}, bf16[8,64,256]{2,1,0:T(8,128)(2,1)S(1)}, u32[]{:S(2)}, u32[]{:S(2)}) %collective-permute-start.17) | collective-permute-done | bytes 262176 | tf_op jit(solution)/shard_map/ppermute | solution.py:150
  73.8 1.2 %slice_dynamic-update-slice_fusion = bf16[64,64,1024]{2,1,0:T(8,128)(2,1)} fusion(bf16[64,64,1024]{2,1,0:T(8,128)(2,1)} %slice_dynamic-update-slice_fusion.1, s32[]{:T(128)S(6)} %select_n.402, bf16[64,64,256]{2,1,0:T(8,128)(2,1)S(1)} %bitcast_convert_fusion), kind=kLoop, calls=%fused_computation.11 | loop fusion | bytes 2097156 | tf_op jit(solution)/shard_map/dynamic_update_slice | solution.py:138
  75.0 0.4 collective-permute-done.18
  75.4 5.6 %fusion.1 = bf16[64,64,1024]{2,1,0:T(8,128)(2,1)} fusion(bf16[64,64,1024]{2,1,0:T(8,128)(2,1)} %slice_dynamic-update-slice_fusion, s32[]{:T(128)S(6)} %select_n.412, bf16[8,64,256]{2,1,0:T(8,128)(2,1)S(1)} %get-tuple-element.10, bf16[8,64,256]{2,1,0:T(8,128)(2,1)S(1)} %get-tuple-element.9, bf16[8,64,64,128]{3,2,0,1:T(8,128)(2,1)S(1)} %get-tuple-element.6, ...), kind=kOutput, calls=%fused_computation.9 | convolution fusion | flops 2182610944 | bytes 18350084 | tf_op jit(solution)/shard_map/wilk,wjk->ilj/dot_general | solution.py:133
  (39 shorter events, 1.4 us)
Async XLA Ops:
  3.6 5.8 %collective-permute-start = (f32[1153]{0:T(1024)S(1)}, f32[1153]{0:T(1024)S(1)}, u32[]{:S(2)}, u32[]{:S(2)}) collective-permute-start(f32[1153]{0:T(1024)S(1)} %pad_maximum_fusion.2), channel_id=1, source_target_pairs={{0,8},{1,9},{2,10},{3,11},{4,12},{5,13},{6,14},{7,15},{8,0},{9,1},... | collective-permute-start | bytes 13844 | tf_op jit(solution)/shard_map/ppermute | solution.py:27
  10.1 3.7 %collective-permute-start.1 = (f32[1153]{0:T(1024)S(1)}, f32[1153]{0:T(1024)S(1)}, u32[]{:S(2)}, u32[]{:S(2)}) collective-permute-start(f32[1153]{0:T(1024)S(1)} %fusion.49), channel_id=1, source_target_pairs={{0,4},{1,5},{2,6},{3,7},{4,0},{5,1},{6,2},{7,3},{8,12},{9,13},{10,... | collective-permute-start | bytes 13844 | tf_op jit(solution)/shard_map/ppermute | solution.py:27
  13.8 3.7 %collective-permute-start.2 = (f32[1153]{0:T(1024)S(1)}, f32[1153]{0:T(1024)S(1)}, u32[]{:S(2)}, u32[]{:S(2)}) collective-permute-start(f32[1153]{0:T(1024)S(1)} %add.117), channel_id=1, source_target_pairs={{0,2},{1,3},{2,0},{3,1},{4,6},{5,7},{6,4},{7,5},{8,10},{9,11},{10,... | collective-permute-start | bytes 13844 | tf_op jit(solution)/shard_map/ppermute | solution.py:27
  17.4 1.2 %collective-permute-start.3 = (f32[1153]{0:T(1024)S(1)}, f32[1153]{0:T(1024)S(1)}, u32[]{:S(2)}, u32[]{:S(2)}) collective-permute-start(f32[1153]{0:T(1024)S(1)} %add.118), channel_id=1, source_target_pairs={{0,1},{1,0},{2,3},{3,2},{4,5},{5,4},{6,7},{7,6},{8,9},{9,8},{10,11... | collective-permute-start | bytes 13844 | tf_op jit(solution)/shard_map/ppermute | solution.py:27
  22.1 2.6 %collective-permute-start.4 = (bf16[8,64,256]{2,1,0:T(8,128)(2,1)S(1)}, bf16[8,64,256]{2,1,0:T(8,128)(2,1)S(1)}, u32[]{:S(2)}, u32[]{:S(2)}) collective-permute-start(bf16[8,64,256]{2,1,0:T(8,128)(2,1)S(1)} %pad_maximum_fusion.1), channel_id=1, source_target_pairs={{0,1},{1,0},{2,3},{3,2},{4,5},{5,4},{6,7},{7,6},{8,9},{9,8},{10,11... | collective-permute-start | bytes 786440 | tf_op jit(solution)/shard_map/ppermute | solution.py:141
  22.5 8.7 %collective-permute-start.7 = (bf16[8,64,256]{2,1,0:T(8,128)(2,1)S(1)}, bf16[8,64,256]{2,1,0:T(8,128)(2,1)S(1)}, u32[]{:S(2)}, u32[]{:S(2)}) collective-permute-start(bf16[8,64,256]{2,1,0:T(8,128)(2,1)S(1)} %pad_maximum_fusion.1), channel_id=1, source_target_pairs={{0,2},{1,3},{2,6},{3,7},{4,0},{5,1},{6,10},{7,11},{8,4},{9,5},{10,... | collective-permute-start | bytes 786440 | tf_op jit(solution)/shard_map/ppermute | solution.py:143
  24.4 8.2 %collective-permute-start.5 = (bf16[8,64,256]{2,1,0:T(8,128)(2,1)S(1)}, bf16[8,64,256]{2,1,0:T(8,128)(2,1)S(1)}, u32[]{:S(2)}, u32[]{:S(2)}) collective-permute-start(bf16[8,64,256]{2,1,0:T(8,128)(2,1)S(1)} %pad_maximum_fusion.1), channel_id=1, source_target_pairs={{0,4},{1,5},{2,0},{3,1},{4,8},{5,9},{6,2},{7,3},{8,12},{9,13},{10,... | collective-permute-start | bytes 786440 | tf_op jit(solution)/shard_map/ppermute | solution.py:142
  31.3 13.5 %collective-permute-start.8 = (bf16[8,64,256]{2,1,0:T(8,128)(2,1)S(1)}, bf16[8,64,256]{2,1,0:T(8,128)(2,1)S(1)}, u32[]{:S(2)}, u32[]{:S(2)}) collective-permute-start(bf16[8,64,256]{2,1,0:T(8,128)(2,1)S(1)} %collective-permute-done.7), channel_id=1, source_target_pairs={{0,1},{1,0},{2,3},{3,2},{4,5},{5,4},{6,7},{7,6},{8,9},{9,8},{10,11... | collective-permute-start | bytes 786440 | tf_op jit(solution)/shard_map/ppermute | solution.py:149
  32.7 12.1 %collective-permute-start.6 = (bf16[8,64,256]{2,1,0:T(8,128)(2,1)S(1)}, bf16[8,64,256]{2,1,0:T(8,128)(2,1)S(1)}, u32[]{:S(2)}, u32[]{:S(2)}) collective-permute-start(bf16[8,64,256]{2,1,0:T(8,128)(2,1)S(1)} %collective-permute-done.5), channel_id=1, source_target_pairs={{0,1},{1,0},{2,3},{3,2},{4,5},{5,4},{6,7},{7,6},{8,9},{9,8},{10,11... | collective-permute-start | bytes 786440 | tf_op jit(solution)/shard_map/ppermute | solution.py:146
  42.7 8.7 %collective-permute-start.11 = (bf16[8,64,256]{2,1,0:T(8,128)(2,1)S(1)}, bf16[8,64,256]{2,1,0:T(8,128)(2,1)S(1)}, u32[]{:S(2)}, u32[]{:S(2)}) collective-permute-start(bf16[8,64,256]{2,1,0:T(8,128)(2,1)S(1)} %collective-permute-done.7), channel_id=1, source_target_pairs={{0,2},{1,3},{2,6},{3,7},{4,0},{5,1},{6,10},{7,11},{8,4},{9,5},{10,... | collective-permute-start | bytes 786440 | tf_op jit(solution)/shard_map/ppermute | solution.py:151
  44.3 8.4 %collective-permute-start.9 = (bf16[8,64,256]{2,1,0:T(8,128)(2,1)S(1)}, bf16[8,64,256]{2,1,0:T(8,128)(2,1)S(1)}, u32[]{:S(2)}, u32[]{:S(2)}) collective-permute-start(bf16[8,64,256]{2,1,0:T(8,128)(2,1)S(1)} %collective-permute-done.5), channel_id=1, source_target_pairs={{0,4},{1,5},{2,0},{3,1},{4,8},{5,9},{6,2},{7,3},{8,12},{9,13},{10,... | collective-permute-start | bytes 786440 | tf_op jit(solution)/shard_map/ppermute | solution.py:150
  51.5 4.9 %collective-permute-start.12 = (bf16[8,64,256]{2,1,0:T(8,128)(2,1)S(1)}, bf16[8,64,256]{2,1,0:T(8,128)(2,1)S(1)}, u32[]{:S(2)}, u32[]{:S(2)}) collective-permute-start(bf16[8,64,256]{2,1,0:T(8,128)(2,1)S(1)} %collective-permute-done.11), channel_id=1, source_target_pairs={{0,1},{1,0},{2,3},{3,2},{4,5},{5,4},{6,7},{7,6},{8,9},{9,8},{10,11... | collective-permute-start | bytes 786440 | tf_op jit(solution)/shard_map/ppermute | solution.py:149
  52.7 3.7 %collective-permute-start.10 = (bf16[8,64,256]{2,1,0:T(8,128)(2,1)S(1)}, bf16[8,64,256]{2,1,0:T(8,128)(2,1)S(1)}, u32[]{:S(2)}, u32[]{:S(2)}) collective-permute-start(bf16[8,64,256]{2,1,0:T(8,128)(2,1)S(1)} %collective-permute-done.9), channel_id=1, source_target_pairs={{0,1},{1,0},{2,3},{3,2},{4,5},{5,4},{6,7},{7,6},{8,9},{9,8},{10,11... | collective-permute-start | bytes 786440 | tf_op jit(solution)/shard_map/ppermute | solution.py:146
  54.3 8.3 %collective-permute-start.15 = (bf16[8,64,256]{2,1,0:T(8,128)(2,1)S(1)}, bf16[8,64,256]{2,1,0:T(8,128)(2,1)S(1)}, u32[]{:S(2)}, u32[]{:S(2)}) collective-permute-start(bf16[8,64,256]{2,1,0:T(8,128)(2,1)S(1)} %collective-permute-done.11), channel_id=1, source_target_pairs={{0,2},{1,3},{2,6},{3,7},{4,0},{5,1},{6,10},{7,11},{8,4},{9,5},{10,... | collective-permute-start | bytes 786440 | tf_op jit(solution)/shard_map/ppermute | solution.py:151
  55.9 8.0 %collective-permute-start.13 = (bf16[8,64,256]{2,1,0:T(8,128)(2,1)S(1)}, bf16[8,64,256]{2,1,0:T(8,128)(2,1)S(1)}, u32[]{:S(2)}, u32[]{:S(2)}) collective-permute-start(bf16[8,64,256]{2,1,0:T(8,128)(2,1)S(1)} %collective-permute-done.9), channel_id=1, source_target_pairs={{0,4},{1,5},{2,0},{3,1},{4,8},{5,9},{6,2},{7,3},{8,12},{9,13},{10,... | collective-permute-start | bytes 786440 | tf_op jit(solution)/shard_map/ppermute | solution.py:150
  62.6 3.3 %collective-permute-start.16 = (bf16[8,64,256]{2,1,0:T(8,128)(2,1)S(1)}, bf16[8,64,256]{2,1,0:T(8,128)(2,1)S(1)}, u32[]{:S(2)}, u32[]{:S(2)}) collective-permute-start(bf16[8,64,256]{2,1,0:T(8,128)(2,1)S(1)} %collective-permute-done.15), channel_id=1, source_target_pairs={{0,1},{1,0},{2,3},{3,2},{4,5},{5,4},{6,7},{7,6},{8,9},{9,8},{10,11... | collective-permute-start | bytes 786440 | tf_op jit(solution)/shard_map/ppermute | solution.py:149
  63.9 2.1 %collective-permute-start.14 = (bf16[8,64,256]{2,1,0:T(8,128)(2,1)S(1)}, bf16[8,64,256]{2,1,0:T(8,128)(2,1)S(1)}, u32[]{:S(2)}, u32[]{:S(2)}) collective-permute-start(bf16[8,64,256]{2,1,0:T(8,128)(2,1)S(1)} %collective-permute-done.13), channel_id=1, source_target_pairs={{0,1},{1,0},{2,3},{3,2},{4,5},{5,4},{6,7},{7,6},{8,9},{9,8},{10,11... | collective-permute-start | bytes 786440 | tf_op jit(solution)/shard_map/ppermute | solution.py:146
  65.5 8.3 %collective-permute-start.17 = (bf16[8,64,256]{2,1,0:T(8,128)(2,1)S(1)}, bf16[8,64,256]{2,1,0:T(8,128)(2,1)S(1)}, u32[]{:S(2)}, u32[]{:S(2)}) collective-permute-start(bf16[8,64,256]{2,1,0:T(8,128)(2,1)S(1)} %collective-permute-done.13), channel_id=1, source_target_pairs={{0,4},{1,5},{2,0},{3,1},{4,8},{5,9},{6,2},{7,3},{8,12},{9,13},{10,... | collective-permute-start | bytes 786440 | tf_op jit(solution)/shard_map/ppermute | solution.py:150
  73.8 1.5 %collective-permute-start.18 = (bf16[8,64,256]{2,1,0:T(8,128)(2,1)S(1)}, bf16[8,64,256]{2,1,0:T(8,128)(2,1)S(1)}, u32[]{:S(2)}, u32[]{:S(2)}) collective-permute-start(bf16[8,64,256]{2,1,0:T(8,128)(2,1)S(1)} %collective-permute-done.17), channel_id=1, source_target_pairs={{0,1},{1,0},{2,3},{3,2},{4,5},{5,4},{6,7},{7,6},{8,9},{9,8},{10,11... | collective-permute-start | bytes 786440 | tf_op jit(solution)/shard_map/ppermute | solution.py:146

commit v6 on v5

--- a/solution.py
+++ b/solution.py
@@ -50,7 +50,8 @@
 def whiten(traces, good_mask):
     channels_here = traces.shape[0]
     good = good_mask.astype(jnp.float32)
-    part = jnp.concatenate([jnp.sum(traces * good[:, None], axis=0), jnp.sum(good)[None]])
+    widened = jnp.concatenate([traces, jnp.ones((traces.shape[0], 1), traces.dtype)], axis=1)
+    part = jnp.sum(widened * good[:, None], axis=0)
     summed = butterfly_sum(part, "chan", "far")
     total, count = summed[:-1], summed[-1]
     common = total / jnp.maximum(count, 1.0)

time: 81.2 us -> 78.6 us (0.968)
  other arithmetic: 11.4 us -> 8.88 us
    reduce_sum x2 -> x1, other arithmetic: 2.32 us -> 1.06 us  [whiten(): part = jnp.sum(widened * good[:, None], axis=0)]
  transfers between devices with their start and end apart: 19 -> 19, of which waited for: 12 -> 12; matrix products, arithmetic and copies ran while one was open for 46% -> 48% of each run, Pallas kernels for 0% -> 0%
where the time goes in v6:
time: 78.6 us; the launch traced here: 78.4 us
  matrix products  26.3 us (33%)
  starting transfers between devices  15.5 us (20%)
  waiting for transfers between devices  14.2 us (18%)
  local copies, waits for them, and re-layouts  12.6 us (16%)
  other arithmetic  8.88 us (11%)
  between operations  0.91 us (1%)
    dot_general x5, matrix products, emit(): jnp.einsum('wilk,wjk->ilj', rotated, rhs, preferred_element_type=jnp.floa...  25.7 us
    ppermute x4, starting transfers between devices, butterfly_sum(): value = value + lax.ppermute(value, axis, pairs)  7.89 us
    dynamic_update_slice x6, local copies, waits for them, and re-layouts, emit(): result = lax.dynamic_update_slice(result, piece, (0, 0, chip * 2 * here))  7.05 us
    ppermute x4, waiting for transfers between devices, butterfly_sum(): value = value + lax.ppermute(value, axis, pairs)  5.76 us
    another operation x2, other arithmetic  4.59 us
    broadcast_in_dim x1, local copies, waits for them, and re-layouts, correlate(): jnp.zeros((rotated.shape[1], rotated.shape[2], size * here), jnp.bfloat16)  4.47 us
    ppermute x2, starting transfers between devices, correlate(): lax.ppermute(behind, 'chan', backward)  3.15 us
    ppermute x2, waiting for transfers between devices, correlate(): lax.ppermute(behind, 'chan', backward)  3.03 us
  transfers between devices with their start and end apart: 19, of which 12 were waited for; matrix products, arithmetic and copies ran while one was open for 48% of the time, Pallas kernels for 0%

profile of v6, /device:TPU:0, one launch (start us, length us, event | category | flops | bytes accessed | tf_op | source)
XLA Modules:
  0.0 78.4 jit_solution(12570993230276365802)
XLA Ops:
  0.0 0.7 convert_element_type.60
  0.7 1.1 %multiply_reduce_fusion = f32[1153]{0:T(1024)S(1)} fusion(f32[64,1152]{1,0:T(8,128)} %param.2, f32[64]{0:T(128)S(1)} %convert_element_type.60), kind=kLoop, calls=%fused_computation.47 | loop fusion | flops 146431 | bytes 299780 | tf_op jit(solution)/shard_map/reduce_sum | solution.py:54
  1.7 4.1 %collective-permute-start = (f32[1153]{0:T(1024)S(1)}, f32[1153]{0:T(1024)S(1)}, u32[]{:S(2)}, u32[]{:S(2)}) collective-permute-start(f32[1153]{0:T(1024)S(1)} %multiply_reduce_fusion), channel_id=1, source_target_pairs={{0,8},{1,9},{2,10},{3,11},{4,12},{5,13},{6,14},{7,15},{8,0},{9,1},... | collective-permute-start | bytes 13844 | tf_op jit(solution)/shard_map/ppermute | solution.py:27
  5.9 1.6 %collective-permute-done = f32[1153]{0:T(1024)S(1)} collective-permute-done((f32[1153]{0:T(1024)S(1)}, f32[1153]{0:T(1024)S(1)}, u32[]{:S(2)}, u32[]{:S(2)}) %collective-permute-start) | collective-permute-done | bytes 4644 | tf_op jit(solution)/shard_map/ppermute | solution.py:27
  7.5 1.9 %collective-permute-start.1 = (f32[1153]{0:T(1024)S(1)}, f32[1153]{0:T(1024)S(1)}, u32[]{:S(2)}, u32[]{:S(2)}) collective-permute-start(f32[1153]{0:T(1024)S(1)} %add.118), channel_id=1, source_target_pairs={{0,4},{1,5},{2,6},{3,7},{4,0},{5,1},{6,2},{7,3},{8,12},{9,13},{10,... | collective-permute-start | bytes 13844 | tf_op jit(solution)/shard_map/ppermute | solution.py:27
  9.4 1.7 %collective-permute-done.1 = f32[1153]{0:T(1024)S(1)} collective-permute-done((f32[1153]{0:T(1024)S(1)}, f32[1153]{0:T(1024)S(1)}, u32[]{:S(2)}, u32[]{:S(2)}) %collective-permute-start.1) | collective-permute-done | bytes 4644 | tf_op jit(solution)/shard_map/ppermute | solution.py:27
  11.1 1.8 %collective-permute-start.2 = (f32[1153]{0:T(1024)S(1)}, f32[1153]{0:T(1024)S(1)}, u32[]{:S(2)}, u32[]{:S(2)}) collective-permute-start(f32[1153]{0:T(1024)S(1)} %add.119), channel_id=1, source_target_pairs={{0,2},{1,3},{2,0},{3,1},{4,6},{5,7},{6,4},{7,5},{8,10},{9,11},{10,... | collective-permute-start | bytes 13844 | tf_op jit(solution)/shard_map/ppermute | solution.py:27
  13.0 1.8 %collective-permute-done.2 = f32[1153]{0:T(1024)S(1)} collective-permute-done((f32[1153]{0:T(1024)S(1)}, f32[1153]{0:T(1024)S(1)}, u32[]{:S(2)}, u32[]{:S(2)}) %collective-permute-start.2) | collective-permute-done | bytes 4644 | tf_op jit(solution)/shard_map/ppermute | solution.py:27
  14.8 0.5 cosine_multiply_fusion
  15.3 0.6 collective-permute-done.3
  16.0 0.5 slice.57
  17.2 1.1 %subtract_multiply_fusion = f32[64,1152]{1,0:T(8,128)S(1)} fusion(f32[64,1152]{1,0:T(8,128)} %param.2, f32[64]{0:T(128)S(1)} %convert_element_type.60, f32[1152]{0:T(1024)S(1)} %slice_divide_fusion), kind=kLoop, calls=%fused_computation.48 | loop fusion | flops 147456 | bytes 594688 | tf_op jit(solution)/shard_map/mul | solution.py:58
  18.4 0.6 convolution_bitcast_fusion
  19.0 0.1 fusion.45
  19.2 0.2 divide_convert_fusion.1
  19.4 0.2 collective-permute-start.4
  19.7 0.2 cosine_multiply_fusion.1
  19.9 1.9 %collective-permute-start.7 = (bf16[8,64,256]{2,1,0:T(8,128)(2,1)S(1)}, bf16[8,64,256]{2,1,0:T(8,128)(2,1)S(1)}, u32[]{:S(2)}, u32[]{:S(2)}) collective-permute-start(bf16[8,64,256]{2,1,0:T(8,128)(2,1)S(1)} %pad_maximum_fusion.1), channel_id=1, source_target_pairs={{0,2},{1,3},{2,6},{3,7},{4,0},{5,1},{6,10},{7,11},{8,4},{9,5},{10,... | collective-permute-start | bytes 786440 | tf_op jit(solution)/shard_map/ppermute | solution.py:144
  21.8 0.2 collective-permute-start.5
  22.0 0.1 broadcast_select_fusion.15
  22.2 0.2 copy.8
  22.3 0.2 copy.7
  22.5 4.4 %subtract_convert_fusion = (bf16[8,64,64,128]{3,2,0,1:T(8,128)(2,1)S(1)}, bf16[8,64,64,128]{3,2,0,1:T(8,128)(2,1)S(1)}) fusion(f32[64,128]{1,0:T(8,128)S(1)} %get-tuple-element.31, f32[8,64,128]{2,0,1:T(8,128)S(1)} %copy.8, f32[64,128]{1,0:T(8,128)S(1)} %get-tuple-element.30, f32[8,64,128]{2,0,1:T(8,128)S(1)} %copy.7), kind=kLoop, calls=%fused_computation.2 | loop fusion | flops 33554432 | bytes 17367040 | tf_op jit(solution)/shard_map/convert
  27.0 1.7 %collective-permute-done.7 = bf16[8,64,256]{2,1,0:T(8,128)(2,1)S(1)} collective-permute-done((bf16[8,64,256]{2,1,0:T(8,128)(2,1)S(1)}, bf16[8,64,256]{2,1,0:T(8,128)(2,1)S(1)}, u32[]{:S(2)}, u32[]{:S(2)}) %collective-permute-start.7) | collective-permute-done | bytes 262176 | tf_op jit(solution)/shard_map/ppermute | solution.py:144
  28.6 1.4 %collective-permute-done.5 = bf16[8,64,256]{2,1,0:T(8,128)(2,1)S(1)} collective-permute-done((bf16[8,64,256]{2,1,0:T(8,128)(2,1)S(1)}, bf16[8,64,256]{2,1,0:T(8,128)(2,1)S(1)}, u32[]{:S(2)}, u32[]{:S(2)}) %collective-permute-start.5) | collective-permute-done | bytes 262176 | tf_op jit(solution)/shard_map/ppermute | solution.py:143
  30.1 4.5 %broadcast_in_dim.2 = bf16[64,64,1024]{2,1,0:T(8,128)(2,1)} broadcast(bf16[]{:T(256)} %constant.87.clone.1), dimensions={} | broadcast | bytes 8388610 | tf_op jit(solution)/shard_map/broadcast_in_dim | solution.py:120
  34.5 5.6 %fusion = bf16[64,64,1024]{2,1,0:T(8,128)(2,1)} fusion(bf16[64,64,1024]{2,1,0:T(8,128)(2,1)} %broadcast_in_dim.2, s32[]{:T(128)S(6)} %select_n.342, bf16[8,64,256]{2,1,0:T(8,128)(2,1)S(1)} %get-tuple-element.26, bf16[8,64,256]{2,1,0:T(8,128)(2,1)S(1)} %get-tuple-element.25, bf16[8,64,64,128]{3,2,0,1:T(8,128)(2,1)S(1)} %get-tuple-element.6, ...), kind=kOutput, calls=%fused_computation.8 | convolution fusion | flops 2182610944 | bytes 18350084 | tf_op jit(solution)/shard_map/wilk,wjk->ilj/dot_general | solution.py:134
  40.1 1.6 %collective-permute-start.11 = (bf16[8,64,256]{2,1,0:T(8,128)(2,1)S(1)}, bf16[8,64,256]{2,1,0:T(8,128)(2,1)S(1)}, u32[]{:S(2)}, u32[]{:S(2)}) collective-permute-start(bf16[8,64,256]{2,1,0:T(8,128)(2,1)S(1)} %collective-permute-done.7), channel_id=1, source_target_pairs={{0,2},{1,3},{2,6},{3,7},{4,0},{5,1},{6,10},{7,11},{8,4},{9,5},{10,... | collective-permute-start | bytes 786440 | tf_op jit(solution)/shard_map/ppermute | solution.py:152
  41.7 0.4 collective-permute-start.9
  42.2 4.8 %bitcast_convert_fusion.2 = bf16[64,64,256]{2,1,0:T(8,128)(2,1)S(1)} fusion(bf16[8,64,256]{2,1,0:T(8,128)(2,1)S(1)} %get-tuple-element.22, bf16[8,64,256]{2,1,0:T(8,128)(2,1)S(1)} %get-tuple-element.21, bf16[8,64,256]{2,1,0:T(8,128)(2,1)S(1)} %get-tuple-element.20, bf16[8,64,256]{2,1,0:T(8,128)(2,1)S(1)} %get-tuple-element.19, ...), kind=kOutput, calls=%fused_computation.5 | convolution fusion | flops 4333764608 | bytes 19922944 | tf_op jit(solution)/shard_map/wilk,wjk->ilj/dot_general | solution.py:134
  47.1 1.7 %collective-permute-done.11 = bf16[8,64,256]{2,1,0:T(8,128)(2,1)S(1)} collective-permute-done((bf16[8,64,256]{2,1,0:T(8,128)(2,1)S(1)}, bf16[8,64,256]{2,1,0:T(8,128)(2,1)S(1)}, u32[]{:S(2)}, u32[]{:S(2)}) %collective-permute-start.11) | collective-permute-done | bytes 262176 | tf_op jit(solution)/shard_map/ppermute | solution.py:152
  48.8 1.2 %slice_dynamic-update-slice_fusion.5 = bf16[64,64,1024]{2,1,0:T(8,128)(2,1)} fusion(bf16[64,64,1024]{2,1,0:T(8,128)(2,1)} %fusion, s32[]{:T(128)S(6)} %select_n.354, bf16[64,64,256]{2,1,0:T(8,128)(2,1)S(1)} %bitcast_convert_fusion.2), kind=kLoop, calls=%fused_computation.16 | loop fusion | bytes 2097156 | tf_op jit(solution)/shard_map/dynamic_update_slice | solution.py:139
  50.1 0.4 collective-permute-start.10
  50.5 1.2 %slice_dynamic-update-slice_fusion.4 = bf16[64,64,1024]{2,1,0:T(8,128)(2,1)} fusion(bf16[64,64,1024]{2,1,0:T(8,128)(2,1)} %slice_dynamic-update-slice_fusion.5, s32[]{:T(128)S(6)} %select_n.362, bf16[64,64,256]{2,1,0:T(8,128)(2,1)S(1)} %bitcast_convert_fusion.2), kind=kLoop, calls=%fused_computation.15 | loop fusion | bytes 2097156 | tf_op jit(solution)/shard_map/dynamic_update_slice | solution.py:139
  51.7 1.6 %collective-permute-start.15 = (bf16[8,64,256]{2,1,0:T(8,128)(2,1)S(1)}, bf16[8,64,256]{2,1,0:T(8,128)(2,1)S(1)}, u32[]{:S(2)}, u32[]{:S(2)}) collective-permute-start(bf16[8,64,256]{2,1,0:T(8,128)(2,1)S(1)} %collective-permute-done.11), channel_id=1, source_target_pairs={{0,2},{1,3},{2,6},{3,7},{4,0},{5,1},{6,10},{7,11},{8,4},{9,5},{10,... | collective-permute-start | bytes 786440 | tf_op jit(solution)/shard_map/ppermute | solution.py:152
  53.2 0.5 collective-permute-start.13
  53.9 4.8 %bitcast_convert_fusion.1 = bf16[64,64,256]{2,1,0:T(8,128)(2,1)S(1)} fusion(bf16[8,64,256]{2,1,0:T(8,128)(2,1)S(1)} %get-tuple-element.18, bf16[8,64,256]{2,1,0:T(8,128)(2,1)S(1)} %get-tuple-element.17, bf16[8,64,256]{2,1,0:T(8,128)(2,1)S(1)} %get-tuple-element.16, bf16[8,64,256]{2,1,0:T(8,128)(2,1)S(1)} %get-tuple-element.15, ...), kind=kOutput, calls=%fused_computation.4 | convolution fusion | flops 4333764608 | bytes 19922944 | tf_op jit(solution)/shard_map/wilk,wjk->ilj/dot_general | solution.py:134
  58.7 1.3 %collective-permute-done.15 = bf16[8,64,256]{2,1,0:T(8,128)(2,1)S(1)} collective-permute-done((bf16[8,64,256]{2,1,0:T(8,128)(2,1)S(1)}, bf16[8,64,256]{2,1,0:T(8,128)(2,1)S(1)}, u32[]{:S(2)}, u32[]{:S(2)}) %collective-permute-start.15) | collective-permute-done | bytes 262176 | tf_op jit(solution)/shard_map/ppermute | solution.py:152
  60.0 1.2 %slice_dynamic-update-slice_fusion.3 = bf16[64,64,1024]{2,1,0:T(8,128)(2,1)} fusion(bf16[64,64,1024]{2,1,0:T(8,128)(2,1)} %slice_dynamic-update-slice_fusion.4, s32[]{:T(128)S(6)} %select_n.374, bf16[64,64,256]{2,1,0:T(8,128)(2,1)S(1)} %bitcast_convert_fusion.1), kind=kLoop, calls=%fused_computation.14 | loop fusion | bytes 2097156 | tf_op jit(solution)/shard_map/dynamic_update_slice | solution.py:139
  61.3 0.4 collective-permute-start.14
  61.7 1.2 %slice_dynamic-update-slice_fusion.2 = bf16[64,64,1024]{2,1,0:T(8,128)(2,1)} fusion(bf16[64,64,1024]{2,1,0:T(8,128)(2,1)} %slice_dynamic-update-slice_fusion.3, s32[]{:T(128)S(6)} %select_n.382, bf16[64,64,256]{2,1,0:T(8,128)(2,1)S(1)} %bitcast_convert_fusion.1), kind=kLoop, calls=%fused_computation.13 | loop fusion | bytes 2097156 | tf_op jit(solution)/shard_map/dynamic_update_slice | solution.py:139
  62.9 0.5 collective-permute-start.17
  63.4 4.8 %bitcast_convert_fusion = bf16[64,64,256]{2,1,0:T(8,128)(2,1)S(1)} fusion(bf16[8,64,256]{2,1,0:T(8,128)(2,1)S(1)} %get-tuple-element.14, bf16[8,64,256]{2,1,0:T(8,128)(2,1)S(1)} %get-tuple-element.13, bf16[8,64,256]{2,1,0:T(8,128)(2,1)S(1)} %get-tuple-element.12, bf16[8,64,256]{2,1,0:T(8,128)(2,1)S(1)} %get-tuple-element.11, ...), kind=kOutput, calls=%fused_computation.3 | convolution fusion | flops 4333764608 | bytes 19922944 | tf_op jit(solution)/shard_map/wilk,wjk->ilj/dot_general | solution.py:134
  68.3 1.2 %slice_dynamic-update-slice_fusion.1 = bf16[64,64,1024]{2,1,0:T(8,128)(2,1)} fusion(bf16[64,64,1024]{2,1,0:T(8,128)(2,1)} %slice_dynamic-update-slice_fusion.2, s32[]{:T(128)S(6)} %select_n.394, bf16[64,64,256]{2,1,0:T(8,128)(2,1)S(1)} %bitcast_convert_fusion), kind=kLoop, calls=%fused_computation.12 | loop fusion | bytes 2097156 | tf_op jit(solution)/shard_map/dynamic_update_slice | solution.py:139
  69.5 1.7 %collective-permute-done.17 = bf16[8,64,256]{2,1,0:T(8,128)(2,1)S(1)} collective-permute-done((bf16[8,64,256]{2,1,0:T(8,128)(2,1)S(1)}, bf16[8,64,256]{2,1,0:T(8,128)(2,1)S(1)}, u32[]{:S(2)}, u32[]{:S(2)}) %collective-permute-start.17) | collective-permute-done | bytes 262176 | tf_op jit(solution)/shard_map/ppermute | solution.py:151
  71.2 1.2 %slice_dynamic-update-slice_fusion = bf16[64,64,1024]{2,1,0:T(8,128)(2,1)} fusion(bf16[64,64,1024]{2,1,0:T(8,128)(2,1)} %slice_dynamic-update-slice_fusion.1, s32[]{:T(128)S(6)} %select_n.402, bf16[64,64,256]{2,1,0:T(8,128)(2,1)S(1)} %bitcast_convert_fusion), kind=kLoop, calls=%fused_computation.11 | loop fusion | bytes 2097156 | tf_op jit(solution)/shard_map/dynamic_update_slice | solution.py:139
  72.4 0.4 collective-permute-done.18
  72.8 5.6 %fusion.1 = bf16[64,64,1024]{2,1,0:T(8,128)(2,1)} fusion(bf16[64,64,1024]{2,1,0:T(8,128)(2,1)} %slice_dynamic-update-slice_fusion, s32[]{:T(128)S(6)} %select_n.412, bf16[8,64,256]{2,1,0:T(8,128)(2,1)S(1)} %get-tuple-element.10, bf16[8,64,256]{2,1,0:T(8,128)(2,1)S(1)} %get-tuple-element.9, bf16[8,64,64,128]{3,2,0,1:T(8,128)(2,1)S(1)} %get-tuple-element.6, ...), kind=kOutput, calls=%fused_computation.9 | convolution fusion | flops 2182610944 | bytes 18350084 | tf_op jit(solution)/shard_map/wilk,wjk->ilj/dot_general | solution.py:134
  (37 shorter events, 1.0 us)
Async XLA Ops:
  1.7 5.8 %collective-permute-start = (f32[1153]{0:T(1024)S(1)}, f32[1153]{0:T(1024)S(1)}, u32[]{:S(2)}, u32[]{:S(2)}) collective-permute-start(f32[1153]{0:T(1024)S(1)} %multiply_reduce_fusion), channel_id=1, source_target_pairs={{0,8},{1,9},{2,10},{3,11},{4,12},{5,13},{6,14},{7,15},{8,0},{9,1},... | collective-permute-start | bytes 13844 | tf_op jit(solution)/shard_map/ppermute | solution.py:27
  7.5 3.7 %collective-permute-start.1 = (f32[1153]{0:T(1024)S(1)}, f32[1153]{0:T(1024)S(1)}, u32[]{:S(2)}, u32[]{:S(2)}) collective-permute-start(f32[1153]{0:T(1024)S(1)} %add.118), channel_id=1, source_target_pairs={{0,4},{1,5},{2,6},{3,7},{4,0},{5,1},{6,2},{7,3},{8,12},{9,13},{10,... | collective-permute-start | bytes 13844 | tf_op jit(solution)/shard_map/ppermute | solution.py:27
  11.1 3.7 %collective-permute-start.2 = (f32[1153]{0:T(1024)S(1)}, f32[1153]{0:T(1024)S(1)}, u32[]{:S(2)}, u32[]{:S(2)}) collective-permute-start(f32[1153]{0:T(1024)S(1)} %add.119), channel_id=1, source_target_pairs={{0,2},{1,3},{2,0},{3,1},{4,6},{5,7},{6,4},{7,5},{8,10},{9,11},{10,... | collective-permute-start | bytes 13844 | tf_op jit(solution)/shard_map/ppermute | solution.py:27
  14.8 1.2 %collective-permute-start.3 = (f32[1153]{0:T(1024)S(1)}, f32[1153]{0:T(1024)S(1)}, u32[]{:S(2)}, u32[]{:S(2)}) collective-permute-start(f32[1153]{0:T(1024)S(1)} %add.120), channel_id=1, source_target_pairs={{0,1},{1,0},{2,3},{3,2},{4,5},{5,4},{6,7},{7,6},{8,9},{9,8},{10,11... | collective-permute-start | bytes 13844 | tf_op jit(solution)/shard_map/ppermute | solution.py:27
  19.4 2.6 %collective-permute-start.4 = (bf16[8,64,256]{2,1,0:T(8,128)(2,1)S(1)}, bf16[8,64,256]{2,1,0:T(8,128)(2,1)S(1)}, u32[]{:S(2)}, u32[]{:S(2)}) collective-permute-start(bf16[8,64,256]{2,1,0:T(8,128)(2,1)S(1)} %pad_maximum_fusion.1), channel_id=1, source_target_pairs={{0,1},{1,0},{2,3},{3,2},{4,5},{5,4},{6,7},{7,6},{8,9},{9,8},{10,11... | collective-permute-start | bytes 786440 | tf_op jit(solution)/shard_map/ppermute | solution.py:142
  19.9 8.7 %collective-permute-start.7 = (bf16[8,64,256]{2,1,0:T(8,128)(2,1)S(1)}, bf16[8,64,256]{2,1,0:T(8,128)(2,1)S(1)}, u32[]{:S(2)}, u32[]{:S(2)}) collective-permute-start(bf16[8,64,256]{2,1,0:T(8,128)(2,1)S(1)} %pad_maximum_fusion.1), channel_id=1, source_target_pairs={{0,2},{1,3},{2,6},{3,7},{4,0},{5,1},{6,10},{7,11},{8,4},{9,5},{10,... | collective-permute-start | bytes 786440 | tf_op jit(solution)/shard_map/ppermute | solution.py:144
  21.8 8.2 %collective-permute-start.5 = (bf16[8,64,256]{2,1,0:T(8,128)(2,1)S(1)}, bf16[8,64,256]{2,1,0:T(8,128)(2,1)S(1)}, u32[]{:S(2)}, u32[]{:S(2)}) collective-permute-start(bf16[8,64,256]{2,1,0:T(8,128)(2,1)S(1)} %pad_maximum_fusion.1), channel_id=1, source_target_pairs={{0,4},{1,5},{2,0},{3,1},{4,8},{5,9},{6,2},{7,3},{8,12},{9,13},{10,... | collective-permute-start | bytes 786440 | tf_op jit(solution)/shard_map/ppermute | solution.py:143
  28.6 13.5 %collective-permute-start.8 = (bf16[8,64,256]{2,1,0:T(8,128)(2,1)S(1)}, bf16[8,64,256]{2,1,0:T(8,128)(2,1)S(1)}, u32[]{:S(2)}, u32[]{:S(2)}) collective-permute-start(bf16[8,64,256]{2,1,0:T(8,128)(2,1)S(1)} %collective-permute-done.7), channel_id=1, source_target_pairs={{0,1},{1,0},{2,3},{3,2},{4,5},{5,4},{6,7},{7,6},{8,9},{9,8},{10,11... | collective-permute-start | bytes 786440 | tf_op jit(solution)/shard_map/ppermute | solution.py:150
  30.1 12.1 %collective-permute-start.6 = (bf16[8,64,256]{2,1,0:T(8,128)(2,1)S(1)}, bf16[8,64,256]{2,1,0:T(8,128)(2,1)S(1)}, u32[]{:S(2)}, u32[]{:S(2)}) collective-permute-start(bf16[8,64,256]{2,1,0:T(8,128)(2,1)S(1)} %collective-permute-done.5), channel_id=1, source_target_pairs={{0,1},{1,0},{2,3},{3,2},{4,5},{5,4},{6,7},{7,6},{8,9},{9,8},{10,11... | collective-permute-start | bytes 786440 | tf_op jit(solution)/shard_map/ppermute | solution.py:147
  40.1 8.7 %collective-permute-start.11 = (bf16[8,64,256]{2,1,0:T(8,128)(2,1)S(1)}, bf16[8,64,256]{2,1,0:T(8,128)(2,1)S(1)}, u32[]{:S(2)}, u32[]{:S(2)}) collective-permute-start(bf16[8,64,256]{2,1,0:T(8,128)(2,1)S(1)} %collective-permute-done.7), channel_id=1, source_target_pairs={{0,2},{1,3},{2,6},{3,7},{4,0},{5,1},{6,10},{7,11},{8,4},{9,5},{10,... | collective-permute-start | bytes 786440 | tf_op jit(solution)/shard_map/ppermute | solution.py:152
  41.7 8.4 %collective-permute-start.9 = (bf16[8,64,256]{2,1,0:T(8,128)(2,1)S(1)}, bf16[8,64,256]{2,1,0:T(8,128)(2,1)S(1)}, u32[]{:S(2)}, u32[]{:S(2)}) collective-permute-start(bf16[8,64,256]{2,1,0:T(8,128)(2,1)S(1)} %collective-permute-done.5), channel_id=1, source_target_pairs={{0,4},{1,5},{2,0},{3,1},{4,8},{5,9},{6,2},{7,3},{8,12},{9,13},{10,... | collective-permute-start | bytes 786440 | tf_op jit(solution)/shard_map/ppermute | solution.py:151
  48.8 4.9 %collective-permute-start.12 = (bf16[8,64,256]{2,1,0:T(8,128)(2,1)S(1)}, bf16[8,64,256]{2,1,0:T(8,128)(2,1)S(1)}, u32[]{:S(2)}, u32[]{:S(2)}) collective-permute-start(bf16[8,64,256]{2,1,0:T(8,128)(2,1)S(1)} %collective-permute-done.11), channel_id=1, source_target_pairs={{0,1},{1,0},{2,3},{3,2},{4,5},{5,4},{6,7},{7,6},{8,9},{9,8},{10,11... | collective-permute-start | bytes 786440 | tf_op jit(solution)/shard_map/ppermute | solution.py:150
  50.1 3.7 %collective-permute-start.10 = (bf16[8,64,256]{2,1,0:T(8,128)(2,1)S(1)}, bf16[8,64,256]{2,1,0:T(8,128)(2,1)S(1)}, u32[]{:S(2)}, u32[]{:S(2)}) collective-permute-start(bf16[8,64,256]{2,1,0:T(8,128)(2,1)S(1)} %collective-permute-done.9), channel_id=1, source_target_pairs={{0,1},{1,0},{2,3},{3,2},{4,5},{5,4},{6,7},{7,6},{8,9},{9,8},{10,11... | collective-permute-start | bytes 786440 | tf_op jit(solution)/shard_map/ppermute | solution.py:147
  51.7 8.3 %collective-permute-start.15 = (bf16[8,64,256]{2,1,0:T(8,128)(2,1)S(1)}, bf16[8,64,256]{2,1,0:T(8,128)(2,1)S(1)}, u32[]{:S(2)}, u32[]{:S(2)}) collective-permute-start(bf16[8,64,256]{2,1,0:T(8,128)(2,1)S(1)} %collective-permute-done.11), channel_id=1, source_target_pairs={{0,2},{1,3},{2,6},{3,7},{4,0},{5,1},{6,10},{7,11},{8,4},{9,5},{10,... | collective-permute-start | bytes 786440 | tf_op jit(solution)/shard_map/ppermute | solution.py:152
  53.2 8.0 %collective-permute-start.13 = (bf16[8,64,256]{2,1,0:T(8,128)(2,1)S(1)}, bf16[8,64,256]{2,1,0:T(8,128)(2,1)S(1)}, u32[]{:S(2)}, u32[]{:S(2)}) collective-permute-start(bf16[8,64,256]{2,1,0:T(8,128)(2,1)S(1)} %collective-permute-done.9), channel_id=1, source_target_pairs={{0,4},{1,5},{2,0},{3,1},{4,8},{5,9},{6,2},{7,3},{8,12},{9,13},{10,... | collective-permute-start | bytes 786440 | tf_op jit(solution)/shard_map/ppermute | solution.py:151
  60.0 3.3 %collective-permute-start.16 = (bf16[8,64,256]{2,1,0:T(8,128)(2,1)S(1)}, bf16[8,64,256]{2,1,0:T(8,128)(2,1)S(1)}, u32[]{:S(2)}, u32[]{:S(2)}) collective-permute-start(bf16[8,64,256]{2,1,0:T(8,128)(2,1)S(1)} %collective-permute-done.15), channel_id=1, source_target_pairs={{0,1},{1,0},{2,3},{3,2},{4,5},{5,4},{6,7},{7,6},{8,9},{9,8},{10,11... | collective-permute-start | bytes 786440 | tf_op jit(solution)/shard_map/ppermute | solution.py:150
  61.3 2.1 %collective-permute-start.14 = (bf16[8,64,256]{2,1,0:T(8,128)(2,1)S(1)}, bf16[8,64,256]{2,1,0:T(8,128)(2,1)S(1)}, u32[]{:S(2)}, u32[]{:S(2)}) collective-permute-start(bf16[8,64,256]{2,1,0:T(8,128)(2,1)S(1)} %collective-permute-done.13), channel_id=1, source_target_pairs={{0,1},{1,0},{2,3},{3,2},{4,5},{5,4},{6,7},{7,6},{8,9},{9,8},{10,11... | collective-permute-start | bytes 786440 | tf_op jit(solution)/shard_map/ppermute | solution.py:147
  62.9 8.3 %collective-permute-start.17 = (bf16[8,64,256]{2,1,0:T(8,128)(2,1)S(1)}, bf16[8,64,256]{2,1,0:T(8,128)(2,1)S(1)}, u32[]{:S(2)}, u32[]{:S(2)}) collective-permute-start(bf16[8,64,256]{2,1,0:T(8,128)(2,1)S(1)} %collective-permute-done.13), channel_id=1, source_target_pairs={{0,4},{1,5},{2,0},{3,1},{4,8},{5,9},{6,2},{7,3},{8,12},{9,13},{10,... | collective-permute-start | bytes 786440 | tf_op jit(solution)/shard_map/ppermute | solution.py:151
  71.2 1.5 %collective-permute-start.18 = (bf16[8,64,256]{2,1,0:T(8,128)(2,1)S(1)}, bf16[8,64,256]{2,1,0:T(8,128)(2,1)S(1)}, u32[]{:S(2)}, u32[]{:S(2)}) collective-permute-start(bf16[8,64,256]{2,1,0:T(8,128)(2,1)S(1)} %collective-permute-done.17), channel_id=1, source_target_pairs={{0,1},{1,0},{2,3},{3,2},{4,5},{5,4},{6,7},{7,6},{8,9},{9,8},{10,11... | collective-permute-start | bytes 786440 | tf_op jit(solution)/shard_map/ppermute | solution.py:147

commit v7 on v6

--- a/solution.py
+++ b/solution.py
@@ -140,21 +140,30 @@
         return result
 
     own_partner = lax.ppermute(whitened, "chan", partner)
-    ahead = lax.ppermute(whitened, "chan", forward)
-    behind = lax.ppermute(whitened, "chan", backward) if backward_hops else None
-    result = emit(result, [(0, chip_block(whitened, own_partner))])
+    unit = chip_block(whitened, own_partner)
+    result = emit(result, [(0, unit)])
+    first_core = me % 2 == 0
     for s in range(1, forward_hops + 1):
-        ahead_partner = lax.ppermute(ahead, "chan", partner)
-        behind_partner = None
-        if s <= backward_hops:
-            behind_partner = lax.ppermute(behind, "chan", partner)
-        next_ahead = lax.ppermute(ahead, "chan", forward) if s < forward_hops else None
-        next_behind = lax.ppermute(behind, "chan", backward) if s < backward_hops else None
-        pieces = [(-s, chip_block(ahead, ahead_partner))]
-        if s <= backward_hops:
-            pieces.append((s, chip_block(behind, behind_partner)))
-        result = emit(result, pieces)
-        ahead, behind = next_ahead, next_behind
+        both = s <= backward_hops
+        ring = [(2 * k, 2 * shifted(k, 1)) for k in range(chips)]
+        swap = [(2 * k, 2 * k + 1) for k in range(chips)]
+        if both:
+            ring += [(2 * k + 1, 2 * shifted(k, -1) + 1) for k in range(chips)]
+            swap += [(2 * k + 1, 2 * k) for k in range(chips)]
+        unit = lax.ppermute(unit, "chan", ring)
+        other = lax.ppermute(unit, "chan", swap)
+        if both:
+            rhs = jnp.concatenate([unit, other], axis=1)
+            out = jnp.einsum("wilk,wjk->ilj", rotated, rhs, preferred_element_type=jnp.float32)
+            out = out.astype(jnp.bfloat16)
+            mine = jnp.where(first_core, placed_chips[slot[-s]], placed_chips[slot[s]])
+            theirs = jnp.where(first_core, placed_chips[slot[s]], placed_chips[slot[-s]])
+            for t, chip in enumerate((mine, theirs)):
+                piece = out[:, :, t * 2 * here:(t + 1) * 2 * here]
+                result = lax.dynamic_update_slice(result, piece, (0, 0, chip * 2 * here))
+        else:
+            rhs = jnp.where(first_core, unit, other)
+            result = emit(result, [(-s, rhs)])
     return result
 
 

time: 78.6 us -> 77.4 us (0.985)
  waiting for transfers between devices: 14.2 us -> 10.2 us
  starting transfers between devices: 15.5 us -> 18.4 us
    dot_general x0 -> x3, matrix products: none -> 14.9 us  [correlate(): jnp.einsum('wilk,wjk->ilj', rotated, rhs, preferred_element_type=jnp.floa...]
    dot_general x5 -> x2, matrix products: 25.7 us -> 11.2 us  [emit(): jnp.einsum('wilk,wjk->ilj', rotated, rhs, preferred_element_type=jnp.floa...]
    ppermute x14 -> x8, waiting for transfers between devices: 8.43 us -> 3.33 us  [the longest x4 3.32 us: correlate(): unit = lax.ppermute(unit, 'chan', ring)]
    ppermute x14 -> x8, starting transfers between devices: 7.4 us -> 10.3 us  [the longest x4 8.75 us: correlate(): unit = lax.ppermute(unit, 'chan', ring)]
    ppermute x1, waiting for transfers between devices: 0.01 us -> 1.08 us  [correlate(): own_partner = lax.ppermute(whitened, 'chan', partner)]
  transfers between devices with their start and end apart: 19 -> 13, of which waited for: 12 -> 7; matrix products, arithmetic and copies ran while one was open for 48% -> 48% of each run, Pallas kernels for 0% -> 0%
where the time goes in v7:
time: 77.4 us; the launch traced here: 77.2 us
  matrix products  26.6 us (34%)
  starting transfers between devices  18.4 us (24%)
  local copies, waits for them, and re-layouts  12.6 us (16%)
  waiting for transfers between devices  10.2 us (13%)
  other arithmetic  8.52 us (11%)
  between operations  0.93 us (1%)
    dot_general x3, matrix products, correlate(): jnp.einsum('wilk,wjk->ilj', rotated, rhs, preferred_element_type=jnp.floa...  14.9 us
    dot_general x2, matrix products, emit(): jnp.einsum('wilk,wjk->ilj', rotated, rhs, preferred_element_type=jnp.floa...  11.2 us
    ppermute x4, starting transfers between devices, correlate(): unit = lax.ppermute(unit, 'chan', ring)  8.75 us
    ppermute x4, starting transfers between devices, butterfly_sum(): value = value + lax.ppermute(value, axis, pairs)  7.89 us
    dynamic_update_slice x6, local copies, waits for them, and re-layouts, correlate(): result = lax.dynamic_update_slice(result, piece, (0, 0, chip * 2 * here))  7.06 us
    ppermute x4, waiting for transfers between devices, butterfly_sum(): value = value + lax.ppermute(value, axis, pairs)  5.76 us
    another operation x2, other arithmetic  4.57 us
    broadcast_in_dim x1, local copies, waits for them, and re-layouts, correlate(): jnp.zeros((rotated.shape[1], rotated.shape[2], size * here), jnp.bfloat16)  4.47 us
  transfers between devices with their start and end apart: 13, of which 7 were waited for; matrix products, arithmetic and copies ran while one was open for 48% of the time, Pallas kernels for 0%

profile of v7, /device:TPU:0, one launch (start us, length us, event | category | flops | bytes accessed | tf_op | source)
XLA Modules:
  0.0 77.2 jit_solution(14572380586355539133)
XLA Ops:
  0.0 0.7 convert_element_type.60
  0.7 1.1 %multiply_reduce_fusion = f32[1153]{0:T(1024)S(1)} fusion(f32[64,1152]{1,0:T(8,128)} %param.2, f32[64]{0:T(128)S(1)} %convert_element_type.60), kind=kLoop, calls=%fused_computation.34 | loop fusion | flops 146431 | bytes 299780 | tf_op jit(solution)/shard_map/reduce_sum | solution.py:54
  1.7 4.1 %collective-permute-start = (f32[1153]{0:T(1024)S(1)}, f32[1153]{0:T(1024)S(1)}, u32[]{:S(2)}, u32[]{:S(2)}) collective-permute-start(f32[1153]{0:T(1024)S(1)} %multiply_reduce_fusion), channel_id=1, source_target_pairs={{0,8},{1,9},{2,10},{3,11},{4,12},{5,13},{6,14},{7,15},{8,0},{9,1},... | collective-permute-start | bytes 13844 | tf_op jit(solution)/shard_map/ppermute | solution.py:27
  5.9 1.6 %collective-permute-done = f32[1153]{0:T(1024)S(1)} collective-permute-done((f32[1153]{0:T(1024)S(1)}, f32[1153]{0:T(1024)S(1)}, u32[]{:S(2)}, u32[]{:S(2)}) %collective-permute-start) | collective-permute-done | bytes 4644 | tf_op jit(solution)/shard_map/ppermute | solution.py:27
  7.5 1.9 %collective-permute-start.1 = (f32[1153]{0:T(1024)S(1)}, f32[1153]{0:T(1024)S(1)}, u32[]{:S(2)}, u32[]{:S(2)}) collective-permute-start(f32[1153]{0:T(1024)S(1)} %add.119), channel_id=1, source_target_pairs={{0,4},{1,5},{2,6},{3,7},{4,0},{5,1},{6,2},{7,3},{8,12},{9,13},{10,... | collective-permute-start | bytes 13844 | tf_op jit(solution)/shard_map/ppermute | solution.py:27
  9.4 1.7 %collective-permute-done.1 = f32[1153]{0:T(1024)S(1)} collective-permute-done((f32[1153]{0:T(1024)S(1)}, f32[1153]{0:T(1024)S(1)}, u32[]{:S(2)}, u32[]{:S(2)}) %collective-permute-start.1) | collective-permute-done | bytes 4644 | tf_op jit(solution)/shard_map/ppermute | solution.py:27
  11.1 1.8 %collective-permute-start.2 = (f32[1153]{0:T(1024)S(1)}, f32[1153]{0:T(1024)S(1)}, u32[]{:S(2)}, u32[]{:S(2)}) collective-permute-start(f32[1153]{0:T(1024)S(1)} %add.120), channel_id=1, source_target_pairs={{0,2},{1,3},{2,0},{3,1},{4,6},{5,7},{6,4},{7,5},{8,10},{9,11},{10,... | collective-permute-start | bytes 13844 | tf_op jit(solution)/shard_map/ppermute | solution.py:27
  13.0 1.8 %collective-permute-done.2 = f32[1153]{0:T(1024)S(1)} collective-permute-done((f32[1153]{0:T(1024)S(1)}, f32[1153]{0:T(1024)S(1)}, u32[]{:S(2)}, u32[]{:S(2)}) %collective-permute-start.2) | collective-permute-done | bytes 4644 | tf_op jit(solution)/shard_map/ppermute | solution.py:27
  14.8 0.0 collective-permute-start.3
  14.8 0.5 cosine_multiply_fusion
  15.3 0.6 collective-permute-done.3
  16.0 0.5 slice.57
  17.2 1.1 %subtract_multiply_fusion = f32[64,1152]{1,0:T(8,128)S(1)} fusion(f32[64,1152]{1,0:T(8,128)} %param.2, f32[64]{0:T(128)S(1)} %convert_element_type.60, f32[1152]{0:T(1024)S(1)} %slice_divide_fusion), kind=kLoop, calls=%fused_computation.35 | loop fusion | flops 147456 | bytes 594688 | tf_op jit(solution)/shard_map/mul | solution.py:58
  18.3 0.1 copy.15
  18.4 0.1 copy.14
  18.4 0.6 convolution_bitcast_fusion
  19.0 0.1 fusion.31
  19.2 0.2 divide_convert_fusion.1
  19.4 0.2 collective-permute-start.4
  19.7 0.2 cosine_multiply_fusion.1
  19.9 1.1 %collective-permute-done.4 = bf16[8,64,256]{2,1,0:T(8,128)(2,1)S(1)} collective-permute-done((bf16[8,64,256]{2,1,0:T(8,128)(2,1)S(1)}, bf16[8,64,256]{2,1,0:T(8,128)(2,1)S(1)}, u32[]{:S(2)}, u32[]{:S(2)}) %collective-permute-start.4) | collective-permute-done | bytes 262176 | tf_op jit(solution)/shard_map/ppermute | solution.py:142
  21.0 0.1 broadcast_select_fusion.1
  21.2 0.2 copy.8
  21.4 0.2 copy.7
  21.6 2.0 %collective-permute-start.5 = (bf16[8,128,256]{2,1,0:T(8,128)(2,1)S(1)}, bf16[8,128,256]{2,1,0:T(8,128)(2,1)S(1)}, u32[]{:S(2)}, u32[]{:S(2)}) collective-permute-start(bf16[8,128,256]{2,1,0:T(8,128)(2,1)S(1)} %pad_maximum_fusion.1), channel_id=1, source_target_pairs={{0,4},{2,0},{4,8},{6,2},{8,12},{10,6},{12,14},{14,10},{1,3},{3,7},... | collective-permute-start | bytes 1572872 | tf_op jit(solution)/shard_map/ppermute | solution.py:153
  23.5 4.4 %subtract_convert_fusion = (bf16[8,64,64,128]{3,2,0,1:T(8,128)(2,1)S(1)}, bf16[8,64,64,128]{3,2,0,1:T(8,128)(2,1)S(1)}) fusion(f32[64,128]{1,0:T(8,128)S(1)} %get-tuple-element.17, f32[8,64,128]{2,0,1:T(8,128)S(1)} %copy.8, f32[64,128]{1,0:T(8,128)S(1)} %get-tuple-element.16, f32[8,64,128]{2,0,1:T(8,128)S(1)} %copy.7), kind=kLoop, calls=%fused_computation.2 | loop fusion | flops 33554432 | bytes 17367040 | tf_op jit(solution)/shard_map/convert
  28.0 2.9 %collective-permute-done.5 = bf16[8,128,256]{2,1,0:T(8,128)(2,1)S(1)} collective-permute-done((bf16[8,128,256]{2,1,0:T(8,128)(2,1)S(1)}, bf16[8,128,256]{2,1,0:T(8,128)(2,1)S(1)}, u32[]{:S(2)}, u32[]{:S(2)}) %collective-permute-start.5) | collective-permute-done | bytes 524320 | tf_op jit(solution)/shard_map/ppermute | solution.py:153
  30.8 1.9 %collective-permute-start.7 = (bf16[8,128,256]{2,1,0:T(8,128)(2,1)S(1)}, bf16[8,128,256]{2,1,0:T(8,128)(2,1)S(1)}, u32[]{:S(2)}, u32[]{:S(2)}) collective-permute-start(bf16[8,128,256]{2,1,0:T(8,128)(2,1)S(1)} %collective-permute-done.5), channel_id=1, source_target_pairs={{0,4},{2,0},{4,8},{6,2},{8,12},{10,6},{12,14},{14,10},{1,3},{3,7},... | collective-permute-start | bytes 1572872 | tf_op jit(solution)/shard_map/ppermute | solution.py:153
  32.7 4.5 %broadcast_in_dim.2 = bf16[64,64,1024]{2,1,0:T(8,128)(2,1)} broadcast(bf16[]{:T(256)} %constant.89.clone.1), dimensions={} | broadcast | bytes 8388610 | tf_op jit(solution)/shard_map/broadcast_in_dim | solution.py:120
  37.2 5.6 %fusion = bf16[64,64,1024]{2,1,0:T(8,128)(2,1)} fusion(bf16[64,64,1024]{2,1,0:T(8,128)(2,1)} %broadcast_in_dim.2, s32[]{:T(128)S(6)} %select_n.314, bf16[8,64,256]{2,1,0:T(8,128)(2,1)S(1)} %get-tuple-element.12, bf16[8,64,256]{2,1,0:T(8,128)(2,1)S(1)} %get-tuple-element.11, bf16[8,64,64,128]{3,2,0,1:T(8,128)(2,1)S(1)} %get-tuple-element.6, ...), kind=kOutput, calls=%fused_computation.8 | convolution fusion | flops 2182610944 | bytes 18350084 | tf_op jit(solution)/shard_map/wilk,wjk->ilj/dot_general | solution.py:134
  42.8 0.0 collective-permute-done.7
  42.8 0.2 collective-permute-start.8
  42.9 1.4 %collective-permute-start.9 = (bf16[8,128,256]{2,1,0:T(8,128)(2,1)S(1)}, bf16[8,128,256]{2,1,0:T(8,128)(2,1)S(1)}, u32[]{:S(2)}, u32[]{:S(2)}) collective-permute-start(bf16[8,128,256]{2,1,0:T(8,128)(2,1)S(1)} %collective-permute-done.7), channel_id=1, source_target_pairs={{0,4},{2,0},{4,8},{6,2},{8,12},{10,6},{12,14},{14,10},{1,3},{3,7},... | collective-permute-start | bytes 1572872 | tf_op jit(solution)/shard_map/ppermute | solution.py:153
  44.3 0.0 collective-permute-done.6
  44.4 5.0 %bitcast_convert_fusion.2 = bf16[64,64,256]{2,1,0:T(8,128)(2,1)S(1)} fusion(bf16[8,128,256]{2,1,0:T(8,128)(2,1)S(1)} %collective-permute-done.6, bf16[8,128,256]{2,1,0:T(8,128)(2,1)S(1)} %collective-permute-done.5, bf16[8,64,64,128]{3,2,0,1:T(8,128)(2,1)S(1)} %get-tuple-element.6, bf16[8,64,64,128]{3,2,0,1:T(8,128)(2,1)S(1)} %get-tuple-element.5), kind=kOutput, calls=%fused_computation.5 | convolution fusion | flops 4331667456 | bytes 19922944 | tf_op jit(solution)/shard_map/wilk,wjk->ilj/dot_general | solution.py:157
  49.3 1.2 %slice_dynamic-update-slice_fusion.5 = bf16[64,64,1024]{2,1,0:T(8,128)(2,1)} fusion(bf16[64,64,1024]{2,1,0:T(8,128)(2,1)} %fusion, s32[]{:T(128)S(6)} %select_n.330, bf16[64,64,256]{2,1,0:T(8,128)(2,1)S(1)} %bitcast_convert_fusion.2), kind=kLoop, calls=%fused_computation.16 | loop fusion | bytes 2097156 | tf_op jit(solution)/shard_map/dynamic_update_slice | solution.py:163
  50.5 1.2 %slice_dynamic-update-slice_fusion.4 = bf16[64,64,1024]{2,1,0:T(8,128)(2,1)} fusion(bf16[64,64,1024]{2,1,0:T(8,128)(2,1)} %slice_dynamic-update-slice_fusion.5, s32[]{:T(128)S(6)} %select_n.332, bf16[64,64,256]{2,1,0:T(8,128)(2,1)S(1)} %bitcast_convert_fusion.2), kind=kLoop, calls=%fused_computation.15 | loop fusion | bytes 2097156 | tf_op jit(solution)/shard_map/dynamic_update_slice | solution.py:163
  51.7 0.5 collective-permute-done.9
  52.1 0.0 collective-permute-start.10
  52.1 3.5 %collective-permute-start.11 = (bf16[8,128,256]{2,1,0:T(8,128)(2,1)S(1)}, bf16[8,128,256]{2,1,0:T(8,128)(2,1)S(1)}, u32[]{:S(2)}, u32[]{:S(2)}) collective-permute-start(bf16[8,128,256]{2,1,0:T(8,128)(2,1)S(1)} %collective-permute-done.9), channel_id=1, source_target_pairs={{0,4},{2,0},{4,8},{6,2},{8,12},{10,6},{12,14},{14,10},{16,20},{18,... | collective-permute-start | bytes 1572872 | tf_op jit(solution)/shard_map/ppermute | solution.py:153
  55.6 5.0 %bitcast_convert_fusion.1 = bf16[64,64,256]{2,1,0:T(8,128)(2,1)S(1)} fusion(bf16[8,128,256]{2,1,0:T(8,128)(2,1)S(1)} %collective-permute-done.8, bf16[8,128,256]{2,1,0:T(8,128)(2,1)S(1)} %collective-permute-done.7, bf16[8,64,64,128]{3,2,0,1:T(8,128)(2,1)S(1)} %get-tuple-element.6, bf16[8,64,64,128]{3,2,0,1:T(8,128)(2,1)S(1)} %get-tuple-element.5), kind=kOutput, calls=%fused_computation.4 | convolution fusion | flops 4331667456 | bytes 19922944 | tf_op jit(solution)/shard_map/wilk,wjk->ilj/dot_general | solution.py:157
  60.6 1.2 %slice_dynamic-update-slice_fusion.3 = bf16[64,64,1024]{2,1,0:T(8,128)(2,1)} fusion(bf16[64,64,1024]{2,1,0:T(8,128)(2,1)} %slice_dynamic-update-slice_fusion.4, s32[]{:T(128)S(6)} %select_n.348, bf16[64,64,256]{2,1,0:T(8,128)(2,1)S(1)} %bitcast_convert_fusion.1), kind=kLoop, calls=%fused_computation.14 | loop fusion | bytes 2097156 | tf_op jit(solution)/shard_map/dynamic_update_slice | solution.py:163
  61.8 1.2 %slice_dynamic-update-slice_fusion.2 = bf16[64,64,1024]{2,1,0:T(8,128)(2,1)} fusion(bf16[64,64,1024]{2,1,0:T(8,128)(2,1)} %slice_dynamic-update-slice_fusion.3, s32[]{:T(128)S(6)} %select_n.350, bf16[64,64,256]{2,1,0:T(8,128)(2,1)S(1)} %bitcast_convert_fusion.1), kind=kLoop, calls=%fused_computation.13 | loop fusion | bytes 2097156 | tf_op jit(solution)/shard_map/dynamic_update_slice | solution.py:163
  63.0 5.0 %bitcast_convert_fusion = bf16[64,64,256]{2,1,0:T(8,128)(2,1)S(1)} fusion(bf16[8,128,256]{2,1,0:T(8,128)(2,1)S(1)} %collective-permute-done.10, bf16[8,128,256]{2,1,0:T(8,128)(2,1)S(1)} %collective-permute-done.9, bf16[8,64,64,128]{3,2,0,1:T(8,128)(2,1)S(1)} %get-tuple-element.6, bf16[8,64,64,128]{3,2,0,1:T(8,128)(2,1)S(1)} %get-tuple-element.5), kind=kOutput, calls=%fused_computation.3 | convolution fusion | flops 4331667456 | bytes 19922944 | tf_op jit(solution)/shard_map/wilk,wjk->ilj/dot_general | solution.py:157
  67.9 1.3 %collective-permute-start.12 = (bf16[8,128,256]{2,1,0:T(8,128)(2,1)S(1)}, bf16[8,128,256]{2,1,0:T(8,128)(2,1)S(1)}, u32[]{:S(2)}, u32[]{:S(2)}) collective-permute-start(bf16[8,128,256]{2,1,0:T(8,128)(2,1)S(1)} %collective-permute-done.11), channel_id=1, source_target_pairs={{0,1},{2,3},{4,5},{6,7},{8,9},{10,11},{12,13},{14,15},{16,17},{18,... | collective-permute-start | bytes 1572872 | tf_op jit(solution)/shard_map/ppermute | solution.py:154
  69.3 1.2 %slice_dynamic-update-slice_fusion.1 = bf16[64,64,1024]{2,1,0:T(8,128)(2,1)} fusion(bf16[64,64,1024]{2,1,0:T(8,128)(2,1)} %slice_dynamic-update-slice_fusion.2, s32[]{:T(128)S(6)} %select_n.366, bf16[64,64,256]{2,1,0:T(8,128)(2,1)S(1)} %bitcast_convert_fusion), kind=kLoop, calls=%fused_computation.12 | loop fusion | bytes 2097156 | tf_op jit(solution)/shard_map/dynamic_update_slice | solution.py:163
  70.5 1.2 %slice_dynamic-update-slice_fusion = bf16[64,64,1024]{2,1,0:T(8,128)(2,1)} fusion(bf16[64,64,1024]{2,1,0:T(8,128)(2,1)} %slice_dynamic-update-slice_fusion.1, s32[]{:T(128)S(6)} %select_n.368, bf16[64,64,256]{2,1,0:T(8,128)(2,1)S(1)} %bitcast_convert_fusion), kind=kLoop, calls=%fused_computation.11 | loop fusion | bytes 2097156 | tf_op jit(solution)/shard_map/dynamic_update_slice | solution.py:163
  71.6 5.6 %fusion.1 = bf16[64,64,1024]{2,1,0:T(8,128)(2,1)} fusion(bf16[64,64,1024]{2,1,0:T(8,128)(2,1)} %slice_dynamic-update-slice_fusion, s32[]{:T(128)S(6)} %select_n.378, bf16[8,128,256]{2,1,0:T(8,128)(2,1)S(1)} %collective-permute-done.11, bf16[8,128,256]{2,1,0:T(8,128)(2,1)S(1)} %collective-permute-done.12, pred[]{:T(512)S(6)} %eq.37, ...), kind=kOutput, calls=%fused_computation.9 | convolution fusion | flops 2181824512 | bytes 18874372 | tf_op jit(solution)/shard_map/wilk,wjk->ilj/dot_general | solution.py:134
  (19 shorter events, 0.3 us)
Async XLA Ops:
  1.7 5.8 %collective-permute-start = (f32[1153]{0:T(1024)S(1)}, f32[1153]{0:T(1024)S(1)}, u32[]{:S(2)}, u32[]{:S(2)}) collective-permute-start(f32[1153]{0:T(1024)S(1)} %multiply_reduce_fusion), channel_id=1, source_target_pairs={{0,8},{1,9},{2,10},{3,11},{4,12},{5,13},{6,14},{7,15},{8,0},{9,1},... | collective-permute-start | bytes 13844 | tf_op jit(solution)/shard_map/ppermute | solution.py:27
  7.5 3.7 %collective-permute-start.1 = (f32[1153]{0:T(1024)S(1)}, f32[1153]{0:T(1024)S(1)}, u32[]{:S(2)}, u32[]{:S(2)}) collective-permute-start(f32[1153]{0:T(1024)S(1)} %add.119), channel_id=1, source_target_pairs={{0,4},{1,5},{2,6},{3,7},{4,0},{5,1},{6,2},{7,3},{8,12},{9,13},{10,... | collective-permute-start | bytes 13844 | tf_op jit(solution)/shard_map/ppermute | solution.py:27
  11.1 3.7 %collective-permute-start.2 = (f32[1153]{0:T(1024)S(1)}, f32[1153]{0:T(1024)S(1)}, u32[]{:S(2)}, u32[]{:S(2)}) collective-permute-start(f32[1153]{0:T(1024)S(1)} %add.120), channel_id=1, source_target_pairs={{0,2},{1,3},{2,0},{3,1},{4,6},{5,7},{6,4},{7,5},{8,10},{9,11},{10,... | collective-permute-start | bytes 13844 | tf_op jit(solution)/shard_map/ppermute | solution.py:27
  14.8 1.2 %collective-permute-start.3 = (f32[1153]{0:T(1024)S(1)}, f32[1153]{0:T(1024)S(1)}, u32[]{:S(2)}, u32[]{:S(2)}) collective-permute-start(f32[1153]{0:T(1024)S(1)} %add.121), channel_id=1, source_target_pairs={{0,1},{1,0},{2,3},{3,2},{4,5},{5,4},{6,7},{7,6},{8,9},{9,8},{10,11... | collective-permute-start | bytes 13844 | tf_op jit(solution)/shard_map/ppermute | solution.py:27
  19.4 1.6 %collective-permute-start.4 = (bf16[8,64,256]{2,1,0:T(8,128)(2,1)S(1)}, bf16[8,64,256]{2,1,0:T(8,128)(2,1)S(1)}, u32[]{:S(2)}, u32[]{:S(2)}) collective-permute-start(bf16[8,64,256]{2,1,0:T(8,128)(2,1)S(1)} %pad_maximum_fusion.2), channel_id=1, source_target_pairs={{0,1},{1,0},{2,3},{3,2},{4,5},{5,4},{6,7},{7,6},{8,9},{9,8},{10,11... | collective-permute-start | bytes 786440 | tf_op jit(solution)/shard_map/ppermute | solution.py:142
  21.6 9.2 %collective-permute-start.5 = (bf16[8,128,256]{2,1,0:T(8,128)(2,1)S(1)}, bf16[8,128,256]{2,1,0:T(8,128)(2,1)S(1)}, u32[]{:S(2)}, u32[]{:S(2)}) collective-permute-start(bf16[8,128,256]{2,1,0:T(8,128)(2,1)S(1)} %pad_maximum_fusion.1), channel_id=1, source_target_pairs={{0,4},{2,0},{4,8},{6,2},{8,12},{10,6},{12,14},{14,10},{1,3},{3,7},... | collective-permute-start | bytes 1572872 | tf_op jit(solution)/shard_map/ppermute | solution.py:153
  30.8 13.5 %collective-permute-start.6 = (bf16[8,128,256]{2,1,0:T(8,128)(2,1)S(1)}, bf16[8,128,256]{2,1,0:T(8,128)(2,1)S(1)}, u32[]{:S(2)}, u32[]{:S(2)}) collective-permute-start(bf16[8,128,256]{2,1,0:T(8,128)(2,1)S(1)} %collective-permute-done.5), channel_id=1, source_target_pairs={{0,1},{2,3},{4,5},{6,7},{8,9},{10,11},{12,13},{14,15},{1,0},{3,2},... | collective-permute-start | bytes 1572872 | tf_op jit(solution)/shard_map/ppermute | solution.py:154
  30.8 11.9 %collective-permute-start.7 = (bf16[8,128,256]{2,1,0:T(8,128)(2,1)S(1)}, bf16[8,128,256]{2,1,0:T(8,128)(2,1)S(1)}, u32[]{:S(2)}, u32[]{:S(2)}) collective-permute-start(bf16[8,128,256]{2,1,0:T(8,128)(2,1)S(1)} %collective-permute-done.5), channel_id=1, source_target_pairs={{0,4},{2,0},{4,8},{6,2},{8,12},{10,6},{12,14},{14,10},{1,3},{3,7},... | collective-permute-start | bytes 1572872 | tf_op jit(solution)/shard_map/ppermute | solution.py:153
  42.8 12.9 %collective-permute-start.8 = (bf16[8,128,256]{2,1,0:T(8,128)(2,1)S(1)}, bf16[8,128,256]{2,1,0:T(8,128)(2,1)S(1)}, u32[]{:S(2)}, u32[]{:S(2)}) collective-permute-start(bf16[8,128,256]{2,1,0:T(8,128)(2,1)S(1)} %collective-permute-done.7), channel_id=1, source_target_pairs={{0,1},{2,3},{4,5},{6,7},{8,9},{10,11},{12,13},{14,15},{1,0},{3,2},... | collective-permute-start | bytes 1572872 | tf_op jit(solution)/shard_map/ppermute | solution.py:154
  42.9 9.2 %collective-permute-start.9 = (bf16[8,128,256]{2,1,0:T(8,128)(2,1)S(1)}, bf16[8,128,256]{2,1,0:T(8,128)(2,1)S(1)}, u32[]{:S(2)}, u32[]{:S(2)}) collective-permute-start(bf16[8,128,256]{2,1,0:T(8,128)(2,1)S(1)} %collective-permute-done.7), channel_id=1, source_target_pairs={{0,4},{2,0},{4,8},{6,2},{8,12},{10,6},{12,14},{14,10},{1,3},{3,7},... | collective-permute-start | bytes 1572872 | tf_op jit(solution)/shard_map/ppermute | solution.py:153
  52.1 10.8 %collective-permute-start.10 = (bf16[8,128,256]{2,1,0:T(8,128)(2,1)S(1)}, bf16[8,128,256]{2,1,0:T(8,128)(2,1)S(1)}, u32[]{:S(2)}, u32[]{:S(2)}) collective-permute-start(bf16[8,128,256]{2,1,0:T(8,128)(2,1)S(1)} %collective-permute-done.9), channel_id=1, source_target_pairs={{0,1},{2,3},{4,5},{6,7},{8,9},{10,11},{12,13},{14,15},{1,0},{3,2},... | collective-permute-start | bytes 1572872 | tf_op jit(solution)/shard_map/ppermute | solution.py:154
  52.1 15.8 %collective-permute-start.11 = (bf16[8,128,256]{2,1,0:T(8,128)(2,1)S(1)}, bf16[8,128,256]{2,1,0:T(8,128)(2,1)S(1)}, u32[]{:S(2)}, u32[]{:S(2)}) collective-permute-start(bf16[8,128,256]{2,1,0:T(8,128)(2,1)S(1)} %collective-permute-done.9), channel_id=1, source_target_pairs={{0,4},{2,0},{4,8},{6,2},{8,12},{10,6},{12,14},{14,10},{16,20},{18,... | collective-permute-start | bytes 1572872 | tf_op jit(solution)/shard_map/ppermute | solution.py:153
  67.9 3.7 %collective-permute-start.12 = (bf16[8,128,256]{2,1,0:T(8,128)(2,1)S(1)}, bf16[8,128,256]{2,1,0:T(8,128)(2,1)S(1)}, u32[]{:S(2)}, u32[]{:S(2)}) collective-permute-start(bf16[8,128,256]{2,1,0:T(8,128)(2,1)S(1)} %collective-permute-done.11), channel_id=1, source_target_pairs={{0,1},{2,3},{4,5},{6,7},{8,9},{10,11},{12,13},{14,15},{16,17},{18,... | collective-permute-start | bytes 1572872 | tf_op jit(solution)/shard_map/ppermute | solution.py:154

commit v8 on v7

--- a/solution.py
+++ b/solution.py
@@ -145,12 +145,16 @@
     first_core = me % 2 == 0
     for s in range(1, forward_hops + 1):
         both = s <= backward_hops
+        opposite = not both and chips % 2 == 0
         ring = [(2 * k, 2 * shifted(k, 1)) for k in range(chips)]
         swap = [(2 * k, 2 * k + 1) for k in range(chips)]
-        if both:
+        if both or opposite:
             ring += [(2 * k + 1, 2 * shifted(k, -1) + 1) for k in range(chips)]
             swap += [(2 * k + 1, 2 * k) for k in range(chips)]
         unit = lax.ppermute(unit, "chan", ring)
+        if opposite:
+            result = emit(result, [(-s, unit)])
+            continue
         other = lax.ppermute(unit, "chan", swap)
         if both:
             rhs = jnp.concatenate([unit, other], axis=1)

time: 77.4 us -> 74.1 us (0.957)
  starting transfers between devices: 18.4 us -> 15 us
    ppermute x4, starting transfers between devices: 8.75 us -> 6.68 us  [correlate(): unit = lax.ppermute(unit, 'chan', ring)]
    ppermute x4 -> x3, starting transfers between devices: 1.5 us -> 0.18 us  [correlate(): other = lax.ppermute(unit, 'chan', swap)]
  transfers between devices with their start and end apart: 13 -> 12, of which waited for: 7 -> 7; matrix products, arithmetic and copies ran while one was open for 48% -> 50% of each run, Pallas kernels for 0% -> 0%
where the time goes in v8:
time: 74.1 us; the launch traced here: 73.9 us
  matrix products  26.7 us (36%)
  starting transfers between devices  15 us (20%)
  local copies, waits for them, and re-layouts  12.6 us (17%)
  waiting for transfers between devices  10.2 us (14%)
  other arithmetic  8.52 us (11%)
  between operations  0.9 us (1%)
    dot_general x3, matrix products, correlate(): jnp.einsum('wilk,wjk->ilj', rotated, rhs, preferred_element_type=jnp.floa...  14.9 us
    dot_general x2, matrix products, emit(): jnp.einsum('wilk,wjk->ilj', rotated, rhs, preferred_element_type=jnp.floa...  11.3 us
    ppermute x4, starting transfers between devices, butterfly_sum(): value = value + lax.ppermute(value, axis, pairs)  7.89 us
    dynamic_update_slice x6, local copies, waits for them, and re-layouts, correlate(): result = lax.dynamic_update_slice(result, piece, (0, 0, chip * 2 * here))  7.06 us
    ppermute x4, starting transfers between devices, correlate(): unit = lax.ppermute(unit, 'chan', ring)  6.68 us
    ppermute x4, waiting for transfers between devices, butterfly_sum(): value = value + lax.ppermute(value, axis, pairs)  5.76 us
    another operation x2, other arithmetic  4.57 us
    broadcast_in_dim x1, local copies, waits for them, and re-layouts, correlate(): jnp.zeros((rotated.shape[1], rotated.shape[2], size * here), jnp.bfloat16)  4.47 us
  transfers between devices with their start and end apart: 12, of which 7 were waited for; matrix products, arithmetic and copies ran while one was open for 50% of the time, Pallas kernels for 0%

profile of v8, /device:TPU:0, one launch (start us, length us, event | category | flops | bytes accessed | tf_op | source)
XLA Modules:
  0.0 73.9 jit_solution(16128766057638553819)
XLA Ops:
  0.0 0.7 convert_element_type.60
  0.7 1.1 %multiply_reduce_fusion = f32[1153]{0:T(1024)S(1)} fusion(f32[64,1152]{1,0:T(8,128)} %param.2, f32[64]{0:T(128)S(1)} %convert_element_type.60), kind=kLoop, calls=%fused_computation.32 | loop fusion | flops 146431 | bytes 299780 | tf_op jit(solution)/shard_map/reduce_sum | solution.py:54
  1.7 4.1 %collective-permute-start = (f32[1153]{0:T(1024)S(1)}, f32[1153]{0:T(1024)S(1)}, u32[]{:S(2)}, u32[]{:S(2)}) collective-permute-start(f32[1153]{0:T(1024)S(1)} %multiply_reduce_fusion), channel_id=1, source_target_pairs={{0,8},{1,9},{2,10},{3,11},{4,12},{5,13},{6,14},{7,15},{8,0},{9,1},... | collective-permute-start | bytes 13844 | tf_op jit(solution)/shard_map/ppermute | solution.py:27
  5.9 1.6 %collective-permute-done = f32[1153]{0:T(1024)S(1)} collective-permute-done((f32[1153]{0:T(1024)S(1)}, f32[1153]{0:T(1024)S(1)}, u32[]{:S(2)}, u32[]{:S(2)}) %collective-permute-start) | collective-permute-done | bytes 4644 | tf_op jit(solution)/shard_map/ppermute | solution.py:27
  7.5 1.9 %collective-permute-start.1 = (f32[1153]{0:T(1024)S(1)}, f32[1153]{0:T(1024)S(1)}, u32[]{:S(2)}, u32[]{:S(2)}) collective-permute-start(f32[1153]{0:T(1024)S(1)} %add.119), channel_id=1, source_target_pairs={{0,4},{1,5},{2,6},{3,7},{4,0},{5,1},{6,2},{7,3},{8,12},{9,13},{10,... | collective-permute-start | bytes 13844 | tf_op jit(solution)/shard_map/ppermute | solution.py:27
  9.4 1.7 %collective-permute-done.1 = f32[1153]{0:T(1024)S(1)} collective-permute-done((f32[1153]{0:T(1024)S(1)}, f32[1153]{0:T(1024)S(1)}, u32[]{:S(2)}, u32[]{:S(2)}) %collective-permute-start.1) | collective-permute-done | bytes 4644 | tf_op jit(solution)/shard_map/ppermute | solution.py:27
  11.1 1.8 %collective-permute-start.2 = (f32[1153]{0:T(1024)S(1)}, f32[1153]{0:T(1024)S(1)}, u32[]{:S(2)}, u32[]{:S(2)}) collective-permute-start(f32[1153]{0:T(1024)S(1)} %add.120), channel_id=1, source_target_pairs={{0,2},{1,3},{2,0},{3,1},{4,6},{5,7},{6,4},{7,5},{8,10},{9,11},{10,... | collective-permute-start | bytes 13844 | tf_op jit(solution)/shard_map/ppermute | solution.py:27
  13.0 1.8 %collective-permute-done.2 = f32[1153]{0:T(1024)S(1)} collective-permute-done((f32[1153]{0:T(1024)S(1)}, f32[1153]{0:T(1024)S(1)}, u32[]{:S(2)}, u32[]{:S(2)}) %collective-permute-start.2) | collective-permute-done | bytes 4644 | tf_op jit(solution)/shard_map/ppermute | solution.py:27
  14.8 0.0 collective-permute-start.3
  14.8 0.5 cosine_multiply_fusion
  15.3 0.6 collective-permute-done.3
  16.0 0.5 slice.57
  17.2 1.1 %subtract_multiply_fusion = f32[64,1152]{1,0:T(8,128)S(1)} fusion(f32[64,1152]{1,0:T(8,128)} %param.2, f32[64]{0:T(128)S(1)} %convert_element_type.60, f32[1152]{0:T(1024)S(1)} %slice_divide_fusion), kind=kLoop, calls=%fused_computation.33 | loop fusion | flops 147456 | bytes 594688 | tf_op jit(solution)/shard_map/mul | solution.py:58
  18.3 0.1 copy.15
  18.4 0.1 copy.14
  18.4 0.6 convolution_bitcast_fusion
  19.0 0.1 fusion.29
  19.2 0.2 divide_convert_fusion.1
  19.4 0.2 collective-permute-start.4
  19.7 0.2 cosine_multiply_fusion.1
  19.9 1.1 %collective-permute-done.4 = bf16[8,64,256]{2,1,0:T(8,128)(2,1)S(1)} collective-permute-done((bf16[8,64,256]{2,1,0:T(8,128)(2,1)S(1)}, bf16[8,64,256]{2,1,0:T(8,128)(2,1)S(1)}, u32[]{:S(2)}, u32[]{:S(2)}) %collective-permute-start.4) | collective-permute-done | bytes 262176 | tf_op jit(solution)/shard_map/ppermute | solution.py:142
  21.0 0.1 broadcast_select_fusion.1
  21.2 0.2 copy.8
  21.4 0.2 copy.7
  21.6 2.0 %collective-permute-start.5 = (bf16[8,128,256]{2,1,0:T(8,128)(2,1)S(1)}, bf16[8,128,256]{2,1,0:T(8,128)(2,1)S(1)}, u32[]{:S(2)}, u32[]{:S(2)}) collective-permute-start(bf16[8,128,256]{2,1,0:T(8,128)(2,1)S(1)} %pad_maximum_fusion.1), channel_id=1, source_target_pairs={{0,4},{2,0},{4,8},{6,2},{8,12},{10,6},{12,14},{14,10},{1,3},{3,7},... | collective-permute-start | bytes 1572872 | tf_op jit(solution)/shard_map/ppermute | solution.py:154
  23.5 4.4 %subtract_convert_fusion = (bf16[8,64,64,128]{3,2,0,1:T(8,128)(2,1)S(1)}, bf16[8,64,64,128]{3,2,0,1:T(8,128)(2,1)S(1)}) fusion(f32[64,128]{1,0:T(8,128)S(1)} %get-tuple-element.17, f32[8,64,128]{2,0,1:T(8,128)S(1)} %copy.8, f32[64,128]{1,0:T(8,128)S(1)} %get-tuple-element.16, f32[8,64,128]{2,0,1:T(8,128)S(1)} %copy.7), kind=kLoop, calls=%fused_computation.2 | loop fusion | flops 33554432 | bytes 17367040 | tf_op jit(solution)/shard_map/convert
  28.0 2.9 %collective-permute-done.5 = bf16[8,128,256]{2,1,0:T(8,128)(2,1)S(1)} collective-permute-done((bf16[8,128,256]{2,1,0:T(8,128)(2,1)S(1)}, bf16[8,128,256]{2,1,0:T(8,128)(2,1)S(1)}, u32[]{:S(2)}, u32[]{:S(2)}) %collective-permute-start.5) | collective-permute-done | bytes 524320 | tf_op jit(solution)/shard_map/ppermute | solution.py:154
  30.8 1.9 %collective-permute-start.7 = (bf16[8,128,256]{2,1,0:T(8,128)(2,1)S(1)}, bf16[8,128,256]{2,1,0:T(8,128)(2,1)S(1)}, u32[]{:S(2)}, u32[]{:S(2)}) collective-permute-start(bf16[8,128,256]{2,1,0:T(8,128)(2,1)S(1)} %collective-permute-done.5), channel_id=1, source_target_pairs={{0,4},{2,0},{4,8},{6,2},{8,12},{10,6},{12,14},{14,10},{1,3},{3,7},... | collective-permute-start | bytes 1572872 | tf_op jit(solution)/shard_map/ppermute | solution.py:154
  32.7 4.5 %broadcast_in_dim.2 = bf16[64,64,1024]{2,1,0:T(8,128)(2,1)} broadcast(bf16[]{:T(256)} %constant.89.clone.1), dimensions={} | broadcast | bytes 8388610 | tf_op jit(solution)/shard_map/broadcast_in_dim | solution.py:120
  37.2 5.6 %fusion = bf16[64,64,1024]{2,1,0:T(8,128)(2,1)} fusion(bf16[64,64,1024]{2,1,0:T(8,128)(2,1)} %broadcast_in_dim.2, s32[]{:T(128)S(6)} %select_n.306, bf16[8,64,256]{2,1,0:T(8,128)(2,1)S(1)} %get-tuple-element.12, bf16[8,64,256]{2,1,0:T(8,128)(2,1)S(1)} %get-tuple-element.11, bf16[8,64,64,128]{3,2,0,1:T(8,128)(2,1)S(1)} %get-tuple-element.6, ...), kind=kOutput, calls=%fused_computation.8 | convolution fusion | flops 2182610944 | bytes 18350084 | tf_op jit(solution)/shard_map/wilk,wjk->ilj/dot_general | solution.py:134
  42.8 0.0 collective-permute-done.7
  42.8 0.2 collective-permute-start.8
  42.9 1.4 %collective-permute-start.9 = (bf16[8,128,256]{2,1,0:T(8,128)(2,1)S(1)}, bf16[8,128,256]{2,1,0:T(8,128)(2,1)S(1)}, u32[]{:S(2)}, u32[]{:S(2)}) collective-permute-start(bf16[8,128,256]{2,1,0:T(8,128)(2,1)S(1)} %collective-permute-done.7), channel_id=1, source_target_pairs={{0,4},{2,0},{4,8},{6,2},{8,12},{10,6},{12,14},{14,10},{1,3},{3,7},... | collective-permute-start | bytes 1572872 | tf_op jit(solution)/shard_map/ppermute | solution.py:154
  44.3 0.0 collective-permute-done.6
  44.4 5.0 %bitcast_convert_fusion.2 = bf16[64,64,256]{2,1,0:T(8,128)(2,1)S(1)} fusion(bf16[8,128,256]{2,1,0:T(8,128)(2,1)S(1)} %collective-permute-done.6, bf16[8,128,256]{2,1,0:T(8,128)(2,1)S(1)} %collective-permute-done.5, bf16[8,64,64,128]{3,2,0,1:T(8,128)(2,1)S(1)} %get-tuple-element.6, bf16[8,64,64,128]{3,2,0,1:T(8,128)(2,1)S(1)} %get-tuple-element.5), kind=kOutput, calls=%fused_computation.5 | convolution fusion | flops 4331667456 | bytes 19922944 | tf_op jit(solution)/shard_map/wilk,wjk->ilj/dot_general | solution.py:161
  49.3 1.2 %slice_dynamic-update-slice_fusion.5 = bf16[64,64,1024]{2,1,0:T(8,128)(2,1)} fusion(bf16[64,64,1024]{2,1,0:T(8,128)(2,1)} %fusion, s32[]{:T(128)S(6)} %select_n.322, bf16[64,64,256]{2,1,0:T(8,128)(2,1)S(1)} %bitcast_convert_fusion.2), kind=kLoop, calls=%fused_computation.16 | loop fusion | bytes 2097156 | tf_op jit(solution)/shard_map/dynamic_update_slice | solution.py:167
  50.5 1.2 %slice_dynamic-update-slice_fusion.4 = bf16[64,64,1024]{2,1,0:T(8,128)(2,1)} fusion(bf16[64,64,1024]{2,1,0:T(8,128)(2,1)} %slice_dynamic-update-slice_fusion.5, s32[]{:T(128)S(6)} %select_n.324, bf16[64,64,256]{2,1,0:T(8,128)(2,1)S(1)} %bitcast_convert_fusion.2), kind=kLoop, calls=%fused_computation.15 | loop fusion | bytes 2097156 | tf_op jit(solution)/shard_map/dynamic_update_slice | solution.py:167
  51.7 0.5 collective-permute-done.9
  52.1 1.4 %collective-permute-start.11 = (bf16[8,128,256]{2,1,0:T(8,128)(2,1)S(1)}, bf16[8,128,256]{2,1,0:T(8,128)(2,1)S(1)}, u32[]{:S(2)}, u32[]{:S(2)}) collective-permute-start(bf16[8,128,256]{2,1,0:T(8,128)(2,1)S(1)} %collective-permute-done.9), channel_id=1, source_target_pairs={{0,4},{2,0},{4,8},{6,2},{8,12},{10,6},{12,14},{14,10},{1,3},{3,7},... | collective-permute-start | bytes 1572872 | tf_op jit(solution)/shard_map/ppermute | solution.py:154
  53.5 0.0 collective-permute-done.8
  53.5 5.0 %bitcast_convert_fusion.1 = bf16[64,64,256]{2,1,0:T(8,128)(2,1)S(1)} fusion(bf16[8,128,256]{2,1,0:T(8,128)(2,1)S(1)} %collective-permute-done.8, bf16[8,128,256]{2,1,0:T(8,128)(2,1)S(1)} %collective-permute-done.7, bf16[8,64,64,128]{3,2,0,1:T(8,128)(2,1)S(1)} %get-tuple-element.6, bf16[8,64,64,128]{3,2,0,1:T(8,128)(2,1)S(1)} %get-tuple-element.5), kind=kOutput, calls=%fused_computation.4 | convolution fusion | flops 4331667456 | bytes 19922944 | tf_op jit(solution)/shard_map/wilk,wjk->ilj/dot_general | solution.py:161
  58.5 1.2 %slice_dynamic-update-slice_fusion.3 = bf16[64,64,1024]{2,1,0:T(8,128)(2,1)} fusion(bf16[64,64,1024]{2,1,0:T(8,128)(2,1)} %slice_dynamic-update-slice_fusion.4, s32[]{:T(128)S(6)} %select_n.340, bf16[64,64,256]{2,1,0:T(8,128)(2,1)S(1)} %bitcast_convert_fusion.1), kind=kLoop, calls=%fused_computation.14 | loop fusion | bytes 2097156 | tf_op jit(solution)/shard_map/dynamic_update_slice | solution.py:167
  59.7 1.2 %slice_dynamic-update-slice_fusion.2 = bf16[64,64,1024]{2,1,0:T(8,128)(2,1)} fusion(bf16[64,64,1024]{2,1,0:T(8,128)(2,1)} %slice_dynamic-update-slice_fusion.3, s32[]{:T(128)S(6)} %select_n.342, bf16[64,64,256]{2,1,0:T(8,128)(2,1)S(1)} %bitcast_convert_fusion.1), kind=kLoop, calls=%fused_computation.13 | loop fusion | bytes 2097156 | tf_op jit(solution)/shard_map/dynamic_update_slice | solution.py:167
  60.9 0.0 collective-permute-done.10
  60.9 5.0 %bitcast_convert_fusion = bf16[64,64,256]{2,1,0:T(8,128)(2,1)S(1)} fusion(bf16[8,128,256]{2,1,0:T(8,128)(2,1)S(1)} %collective-permute-done.10, bf16[8,128,256]{2,1,0:T(8,128)(2,1)S(1)} %collective-permute-done.9, bf16[8,64,64,128]{3,2,0,1:T(8,128)(2,1)S(1)} %get-tuple-element.6, bf16[8,64,64,128]{3,2,0,1:T(8,128)(2,1)S(1)} %get-tuple-element.5), kind=kOutput, calls=%fused_computation.3 | convolution fusion | flops 4331667456 | bytes 19922944 | tf_op jit(solution)/shard_map/wilk,wjk->ilj/dot_general | solution.py:161
  65.8 1.2 %slice_dynamic-update-slice_fusion.1 = bf16[64,64,1024]{2,1,0:T(8,128)(2,1)} fusion(bf16[64,64,1024]{2,1,0:T(8,128)(2,1)} %slice_dynamic-update-slice_fusion.2, s32[]{:T(128)S(6)} %select_n.358, bf16[64,64,256]{2,1,0:T(8,128)(2,1)S(1)} %bitcast_convert_fusion), kind=kLoop, calls=%fused_computation.12 | loop fusion | bytes 2097156 | tf_op jit(solution)/shard_map/dynamic_update_slice | solution.py:167
  67.0 1.2 %slice_dynamic-update-slice_fusion = bf16[64,64,1024]{2,1,0:T(8,128)(2,1)} fusion(bf16[64,64,1024]{2,1,0:T(8,128)(2,1)} %slice_dynamic-update-slice_fusion.1, s32[]{:T(128)S(6)} %select_n.360, bf16[64,64,256]{2,1,0:T(8,128)(2,1)S(1)} %bitcast_convert_fusion), kind=kLoop, calls=%fused_computation.11 | loop fusion | bytes 2097156 | tf_op jit(solution)/shard_map/dynamic_update_slice | solution.py:167
  68.2 5.7 %fusion.1 = bf16[64,64,1024]{2,1,0:T(8,128)(2,1)} fusion(bf16[64,64,1024]{2,1,0:T(8,128)(2,1)} %slice_dynamic-update-slice_fusion, s32[]{:T(128)S(6)} %select_n.368, bf16[8,128,256]{2,1,0:T(8,128)(2,1)S(1)} %collective-permute-done.11, bf16[8,64,64,128]{3,2,0,1:T(8,128)(2,1)S(1)} %get-tuple-element.6, bf16[8,64,64,128]{3,2,0,1:T(8,128)(2,1)S(1)} %get-tuple-element.5), kind=kOutput, calls=%fused_computation.9 | convolution fusion | flops 2181562368 | bytes 18350084 | tf_op jit(solution)/shard_map/wilk,wjk->ilj/dot_general | solution.py:134
  (17 shorter events, 0.3 us)
Async XLA Ops:
  1.7 5.8 %collective-permute-start = (f32[1153]{0:T(1024)S(1)}, f32[1153]{0:T(1024)S(1)}, u32[]{:S(2)}, u32[]{:S(2)}) collective-permute-start(f32[1153]{0:T(1024)S(1)} %multiply_reduce_fusion), channel_id=1, source_target_pairs={{0,8},{1,9},{2,10},{3,11},{4,12},{5,13},{6,14},{7,15},{8,0},{9,1},... | collective-permute-start | bytes 13844 | tf_op jit(solution)/shard_map/ppermute | solution.py:27
  7.5 3.7 %collective-permute-start.1 = (f32[1153]{0:T(1024)S(1)}, f32[1153]{0:T(1024)S(1)}, u32[]{:S(2)}, u32[]{:S(2)}) collective-permute-start(f32[1153]{0:T(1024)S(1)} %add.119), channel_id=1, source_target_pairs={{0,4},{1,5},{2,6},{3,7},{4,0},{5,1},{6,2},{7,3},{8,12},{9,13},{10,... | collective-permute-start | bytes 13844 | tf_op jit(solution)/shard_map/ppermute | solution.py:27
  11.1 3.7 %collective-permute-start.2 = (f32[1153]{0:T(1024)S(1)}, f32[1153]{0:T(1024)S(1)}, u32[]{:S(2)}, u32[]{:S(2)}) collective-permute-start(f32[1153]{0:T(1024)S(1)} %add.120), channel_id=1, source_target_pairs={{0,2},{1,3},{2,0},{3,1},{4,6},{5,7},{6,4},{7,5},{8,10},{9,11},{10,... | collective-permute-start | bytes 13844 | tf_op jit(solution)/shard_map/ppermute | solution.py:27
  14.8 1.2 %collective-permute-start.3 = (f32[1153]{0:T(1024)S(1)}, f32[1153]{0:T(1024)S(1)}, u32[]{:S(2)}, u32[]{:S(2)}) collective-permute-start(f32[1153]{0:T(1024)S(1)} %add.121), channel_id=1, source_target_pairs={{0,1},{1,0},{2,3},{3,2},{4,5},{5,4},{6,7},{7,6},{8,9},{9,8},{10,11... | collective-permute-start | bytes 13844 | tf_op jit(solution)/shard_map/ppermute | solution.py:27
  19.4 1.6 %collective-permute-start.4 = (bf16[8,64,256]{2,1,0:T(8,128)(2,1)S(1)}, bf16[8,64,256]{2,1,0:T(8,128)(2,1)S(1)}, u32[]{:S(2)}, u32[]{:S(2)}) collective-permute-start(bf16[8,64,256]{2,1,0:T(8,128)(2,1)S(1)} %pad_maximum_fusion.2), channel_id=1, source_target_pairs={{0,1},{1,0},{2,3},{3,2},{4,5},{5,4},{6,7},{7,6},{8,9},{9,8},{10,11... | collective-permute-start | bytes 786440 | tf_op jit(solution)/shard_map/ppermute | solution.py:142
  21.6 9.2 %collective-permute-start.5 = (bf16[8,128,256]{2,1,0:T(8,128)(2,1)S(1)}, bf16[8,128,256]{2,1,0:T(8,128)(2,1)S(1)}, u32[]{:S(2)}, u32[]{:S(2)}) collective-permute-start(bf16[8,128,256]{2,1,0:T(8,128)(2,1)S(1)} %pad_maximum_fusion.1), channel_id=1, source_target_pairs={{0,4},{2,0},{4,8},{6,2},{8,12},{10,6},{12,14},{14,10},{1,3},{3,7},... | collective-permute-start | bytes 1572872 | tf_op jit(solution)/shard_map/ppermute | solution.py:154
  30.8 13.5 %collective-permute-start.6 = (bf16[8,128,256]{2,1,0:T(8,128)(2,1)S(1)}, bf16[8,128,256]{2,1,0:T(8,128)(2,1)S(1)}, u32[]{:S(2)}, u32[]{:S(2)}) collective-permute-start(bf16[8,128,256]{2,1,0:T(8,128)(2,1)S(1)} %collective-permute-done.5), channel_id=1, source_target_pairs={{0,1},{2,3},{4,5},{6,7},{8,9},{10,11},{12,13},{14,15},{1,0},{3,2},... | collective-permute-start | bytes 1572872 | tf_op jit(solution)/shard_map/ppermute | solution.py:158
  30.8 11.9 %collective-permute-start.7 = (bf16[8,128,256]{2,1,0:T(8,128)(2,1)S(1)}, bf16[8,128,256]{2,1,0:T(8,128)(2,1)S(1)}, u32[]{:S(2)}, u32[]{:S(2)}) collective-permute-start(bf16[8,128,256]{2,1,0:T(8,128)(2,1)S(1)} %collective-permute-done.5), channel_id=1, source_target_pairs={{0,4},{2,0},{4,8},{6,2},{8,12},{10,6},{12,14},{14,10},{1,3},{3,7},... | collective-permute-start | bytes 1572872 | tf_op jit(solution)/shard_map/ppermute | solution.py:154
  42.8 10.8 %collective-permute-start.8 = (bf16[8,128,256]{2,1,0:T(8,128)(2,1)S(1)}, bf16[8,128,256]{2,1,0:T(8,128)(2,1)S(1)}, u32[]{:S(2)}, u32[]{:S(2)}) collective-permute-start(bf16[8,128,256]{2,1,0:T(8,128)(2,1)S(1)} %collective-permute-done.7), channel_id=1, source_target_pairs={{0,1},{2,3},{4,5},{6,7},{8,9},{10,11},{12,13},{14,15},{1,0},{3,2},... | collective-permute-start | bytes 1572872 | tf_op jit(solution)/shard_map/ppermute | solution.py:158
  42.9 9.2 %collective-permute-start.9 = (bf16[8,128,256]{2,1,0:T(8,128)(2,1)S(1)}, bf16[8,128,256]{2,1,0:T(8,128)(2,1)S(1)}, u32[]{:S(2)}, u32[]{:S(2)}) collective-permute-start(bf16[8,128,256]{2,1,0:T(8,128)(2,1)S(1)} %collective-permute-done.7), channel_id=1, source_target_pairs={{0,4},{2,0},{4,8},{6,2},{8,12},{10,6},{12,14},{14,10},{1,3},{3,7},... | collective-permute-start | bytes 1572872 | tf_op jit(solution)/shard_map/ppermute | solution.py:154
  52.1 8.7 %collective-permute-start.10 = (bf16[8,128,256]{2,1,0:T(8,128)(2,1)S(1)}, bf16[8,128,256]{2,1,0:T(8,128)(2,1)S(1)}, u32[]{:S(2)}, u32[]{:S(2)}) collective-permute-start(bf16[8,128,256]{2,1,0:T(8,128)(2,1)S(1)} %collective-permute-done.9), channel_id=1, source_target_pairs={{0,1},{2,3},{4,5},{6,7},{8,9},{10,11},{12,13},{14,15},{1,0},{3,2},... | collective-permute-start | bytes 1572872 | tf_op jit(solution)/shard_map/ppermute | solution.py:158
  52.1 16.0 %collective-permute-start.11 = (bf16[8,128,256]{2,1,0:T(8,128)(2,1)S(1)}, bf16[8,128,256]{2,1,0:T(8,128)(2,1)S(1)}, u32[]{:S(2)}, u32[]{:S(2)}) collective-permute-start(bf16[8,128,256]{2,1,0:T(8,128)(2,1)S(1)} %collective-permute-done.9), channel_id=1, source_target_pairs={{0,4},{2,0},{4,8},{6,2},{8,12},{10,6},{12,14},{14,10},{1,3},{3,7},... | collective-permute-start | bytes 1572872 | tf_op jit(solution)/shard_map/ppermute | solution.py:154
